TPU v7x, 512 devices: a whole 4x8x8 slice. The times are simulated.
512 devices in a mesh: group: 32 (over y, x), member: 16 (over z, core).
Axes of the slice: x: 4, y: 8, z: 8, core: 2. Of those that a mesh axis runs over, the one named last changes fastest.
Arguments:
- feats: bfloat16 [262144, 1024], P(('group', 'member')), may hold values from -24 to 24
- transform: bfloat16 [1024, 1024], replicated, may hold values from -0.1875 to 0.1875
- bias: float32 [1024], replicated, may hold values from -3 to 3
- tile_list: int32 [2048, 8], P(('group', 'member')), may hold values from 0 to 255, as said below
- nbr_slot: int32 [262144, 16], P(('group', 'member')), may hold values from 0 to 255
- nbr_weight: int32 [262144, 16], P(('group', 'member')), may hold values from 1 to 16
- cotangent: bfloat16 [262144, 1024], P(('group', 'member')), may hold values from -6 to 6
Outputs:
- embedding: bfloat16 [262144, 1024], P(('group', 'member'))
- feat_grad: bfloat16 [262144, 1024], P(('group', 'member'))
- transform_grad: float32 [1024, 1024], P('member')
Inputs may be any that keep to these rules, and one draw needn't show every extreme that they name: `tile_list`: each block lists 8 different tiles of its own group; group tile g lies on member g // 16 of that group. Over all blocks of one device, the tiles that lie on another member are at most one distinct tile for each such member.
All inputs are finite; a program needn't handle non-finite values.
Results may differ from a plain program's by a relative error of at most 0.013.
Values may be sent and summed in bfloat16 or wider, within the bound.
No kernel may reach another device: no remote copies, remote signals or barrier semaphores. Data moves between devices by JAX's collectives and lax.ppermute only.
A program may use at most 64 MiB of HBM per device.

v0:
```python
import math

import jax
import jax.numpy as jnp
from jax import lax
from jax.sharding import PartitionSpec as P

TILE = 32


def adjacency_of(slot_rows, weights, cand_width):
    columns = lax.broadcasted_iota(jnp.int32, slot_rows.shape + (cand_width,), slot_rows.ndim)
    matched_weights = jnp.where(slot_rows[..., None] == columns, weights[..., None], 0)
    return jnp.sum(matched_weights, axis=-2).astype(jnp.bfloat16)


def on_device(feats, transform, bias, tile_list, nbr_slot, nbr_weight, cotangent):
    rows_dev, feat_width = feats.shape
    hidden_width = transform.shape[1]
    blocks, tiles_per = tile_list.shape
    block_rows = rows_dev // blocks
    members = lax.axis_size("member")
    groups = lax.axis_size("group")
    member_here = lax.axis_index("member")
    tiles_dev = rows_dev // TILE
    cand_width = tiles_per * TILE
    preact = jnp.dot(feats, transform, preferred_element_type=jnp.float32) + bias
    message = jnp.maximum(preact, 0.0).astype(jnp.bfloat16)
    own_tiles = message.reshape(tiles_dev, TILE, hidden_width)
    holder = tile_list // tiles_dev
    local_index = tile_list % tiles_dev
    foreign = holder != member_here
    peer_ids = lax.broadcasted_iota(jnp.int32, (1, 1, members), 2)
    matched = (holder[..., None] == peer_ids) & foreign[..., None]
    wanted = jnp.max(jnp.where(matched, local_index[..., None], -1), axis=(0, 1))
    asked_for = lax.all_to_all(
        wanted.reshape(members, 1), "member", split_axis=0, concat_axis=0, tiled=True
    )[:, 0]
    served = jnp.clip(asked_for, 0, tiles_dev - 1)
    remote = lax.all_to_all(own_tiles[served], "member", split_axis=0, concat_axis=0, tiled=True)
    tile_pool = jnp.concatenate([remote, own_tiles], axis=0)
    pool_index = jnp.where(foreign, holder, members + local_index).reshape(-1)
    candidates = tile_pool[pool_index].reshape(blocks, cand_width, hidden_width)
    slot_rows = nbr_slot.reshape(blocks, block_rows, -1)
    weights = nbr_weight.reshape(blocks, block_rows, -1)
    adjacency = adjacency_of(slot_rows, weights, cand_width)
    weight_total = jnp.sum(weights, axis=2).astype(jnp.float32)[..., None]
    gathered = jnp.einsum("brc,bch->brh", adjacency, candidates, preferred_element_type=jnp.float32)
    combined = gathered / weight_total + message.reshape(blocks, block_rows, hidden_width).astype(
        jnp.float32
    )
    inv_rms = lax.rsqrt(jnp.mean(combined * combined, axis=2, keepdims=True) + 1e-06)
    normed = combined * inv_rms
    embedding = normed.astype(jnp.bfloat16).reshape(rows_dev, hidden_width)
    incoming = cotangent.reshape(blocks, block_rows, hidden_width).astype(jnp.float32)
    mixed_grad = inv_rms * (incoming - normed * jnp.mean(incoming * normed, axis=2, keepdims=True))
    agg_grad = (mixed_grad / weight_total).astype(jnp.bfloat16)
    cand_grad = jnp.einsum("brc,brh->bch", adjacency, agg_grad, preferred_element_type=jnp.float32)
    cand_grad = cand_grad.reshape(blocks * tiles_per, TILE, hidden_width)
    pool_size = members + tiles_dev
    pool_grad = jax.ops.segment_sum(cand_grad, pool_index, num_segments=pool_size)
    returned = pool_grad[:members].astype(jnp.bfloat16)
    came_back = lax.all_to_all(returned, "member", split_axis=0, concat_axis=0, tiled=True)
    back_rows = jnp.where((asked_for >= 0)[:, None, None], came_back.astype(jnp.float32), 0.0)
    tile_grad = pool_grad[members:].at[served].add(back_rows)
    message_grad = mixed_grad.reshape(rows_dev, hidden_width) + tile_grad.reshape(
        rows_dev, hidden_width
    )
    pre_grad = jnp.where(preact > 0, message_grad, 0.0).astype(jnp.bfloat16)
    feat_grad = lax.dot_general(
        pre_grad, transform, (((1,), (1,)), ((), ())), preferred_element_type=jnp.float32
    ).astype(jnp.bfloat16)
    row_share = lax.psum_scatter(
        lax.dot_general(
            feats, pre_grad, (((0,), (0,)), ((), ())), preferred_element_type=jnp.float32
        ),
        "member",
        scatter_dimension=0,
        tiled=True,
    )
    factor = 1.0 / math.sqrt(rows_dev * members * groups)
    transform_grad = lax.psum(row_share, "group") * factor
    return (embedding, feat_grad, transform_grad)


def solution(mesh):
    return jax.shard_map(
        on_device,
        mesh=mesh,
        in_specs=(
            P(("group", "member"), None),
            P(),
            P(),
            P(("group", "member"), None),
            P(("group", "member"), None),
            P(("group", "member"), None),
            P(("group", "member"), None),
        ),
        out_specs=(P(("group", "member"), None), P(("group", "member"), None), P("member", None)),
        check_vma=False,
    )
```

profile of v0, /device:TPU:6, one launch (start us, length us, event | category | flops | bytes accessed | tf_op | source)
XLA Modules:
  0.0 373.2 jit_solution(13772715015103534861)
XLA Ops:
  7.2 0.0 copy-start
  7.2 0.8 add_select_fusion.2
  8.0 0.1 select_reduce_fusion.1
  8.1 0.7 copy.26
  8.8 10.4 %all-to-all-start = ((s32[16,1,1]{2,1,0:T(1,128)}), s32[16,1,1]{2,1,0:T(1,128)S(1)}, u32[]{:S(2)}, u32[]{:S(2)}) async-start(s32[16,1,1]{2,1,0:T(1,128)} %copy.26), calls=%async_computation | async-start | bytes 16384 | tf_op jit(solution)/shard_map/all_to_all | solution.py:36
  19.3 3.9 %maximum_convert_fusion = (bf16[512,1024]{1,0:T(8,128)(2,1)S(1)}, f32[512,1024]{1,0:T(8,128)}) fusion(f32[1024]{0:T(1024)} %param.9, bf16[512,1024]{1,0:T(8,128)(2,1)} %param.7, bf16[1024,1024]{1,0:T(8,128)(2,1)S(1)} %copy-done), kind=kOutput, calls=%fused_computation.20 | convolution fusion | flops 1075314688 | bytes 6295552 | tf_op jit(solution)/shard_map/dot_general | solution.py:27
  23.1 3.6 all-to-all-done
  26.8 0.4 clamp_reduce_fusion
  27.2 0.0 copy-start.5
  27.2 0.0 copy-start.6
  27.2 1.6 gather_fusion
  28.8 4.3 %all-to-all-start.1 = ((bf16[16,32,1024]{2,1,0:T(8,128)(2,1)}), bf16[16,32,1024]{2,1,0:T(8,128)(2,1)}, u32[]{:S(2)}, u32[]{:S(2)}) async-start(bf16[16,32,1024]{2,1,0:T(8,128)(2,1)} %gather_fusion), calls=%async_computation.1 | async-start | bytes 2097152 | tf_op jit(solution)/shard_map/all_to_all | solution.py:40
  33.1 0.1 reshape.142
  33.2 0.1 reshape.116
  33.3 0.0 copy-done.5
  33.3 0.1 copy.31
  33.5 0.8 copy.30
  34.3 5.9 %select_reduce_fusion = s32[4,128,256]{2,1,0:T(8,128)} fusion(s32[4,128,16]{2,1,0:T(8,128)S(1)} %bitcast.44, s32[4,128,16]{2,1,0:T(8,128)} %bitcast.45), kind=kLoop, calls=%fused_computation.4 | loop fusion | flops 6160384 | bytes 589824 | tf_op jit(solution)/shard_map/reduce_sum | solution.py:14
  40.2 19.4 %all-to-all-done.1 = bf16[16,32,1024]{2,1,0:T(8,128)(2,1)} async-done(((bf16[16,32,1024]{2,1,0:T(8,128)(2,1)}), bf16[16,32,1024]{2,1,0:T(8,128)(2,1)}, u32[]{:S(2)}, u32[]{:S(2)}) %all-to-all-start.1) | async-done | bytes 1048608 | tf_op jit(solution)/shard_map/all_to_all | solution.py:40
  59.7 2.8 pad_maximum_fusion
  62.4 3.6 gather_fusion.1
  66.0 2.6 multiply_reduce_fusion
  68.6 0.4 fusion
  69.0 1.4 fusion.1
  70.5 2.8 fusion.4
  73.2 2.5 broadcast_in_dim.61
  75.7 10.0 %scatter_fusion = f32[32,32,1024]{2,1,0:T(8,128)} fusion(f32[32,32,1024]{2,1,0:T(8,128)} %broadcast_in_dim.61, s32[32]{0:T(128)S(1)} %reshape.142, f32[32,32,1024]{2,1,0:T(8,128)} %bitcast.38), kind=kCustom, calls=%fused_computation.2 | custom fusion | flops 1048576 | bytes 12583040 | tf_op jit(solution)/shard_map/scatter-add | solution.py:61
  85.7 2.7 slice.16
  88.4 4.8 %all-to-all-start.2 = ((bf16[16,32,1024]{2,1,0:T(8,128)(2,1)}), bf16[16,32,1024]{2,1,0:T(8,128)(2,1)S(1)}, u32[]{:S(2)}, u32[]{:S(2)}) async-start(bf16[16,32,1024]{2,1,0:T(8,128)(2,1)} %slice.16), calls=%async_computation.2 | async-start | bytes 2097152 | tf_op jit(solution)/shard_map/all_to_all | solution.py:63
  93.3 0.0 reduce-scatter.4.cloned.1.call-start
  93.3 0.4 compare_reduce_fusion
  93.7 3.2 slice.13
  96.9 22.9 %all-to-all-done.2 = bf16[16,32,1024]{2,1,0:T(8,128)(2,1)S(1)} async-done(((bf16[16,32,1024]{2,1,0:T(8,128)(2,1)}), bf16[16,32,1024]{2,1,0:T(8,128)(2,1)S(1)}, u32[]{:S(2)}, u32[]{:S(2)}) %all-to-all-start.2) | async-done | bytes 1048608 | tf_op jit(solution)/shard_map/all_to_all | solution.py:63
  119.7 1.7 convert_select_fusion
  121.4 5.1 %scatter_fusion.1 = f32[16,32,1024]{2,1,0:T(8,128)} fusion(f32[16,32,1024]{2,1,0:T(8,128)} %slice.13, s32[16]{0:T(128)S(1)} %fusion.10, f32[16,32,1024]{2,1,0:T(8,128)} %convert_select_fusion), kind=kCustom, calls=%fused_computation.3 | custom fusion | flops 524288 | bytes 6291520 | tf_op jit(solution)/shard_map/scatter-add | solution.py:65
  126.5 0.0 copy-done.7
  126.5 3.7 fusion.3
  130.2 3.3 convolution_bitcast_fusion
  133.5 5.3 %copy.32 = f32[1024,1024]{1,0:T(8,128)} copy(f32[1024,1024]{0,1:T(8,128)} %convolution_bitcast_fusion) | data formatting | bytes 8388608
  138.8 0.0 reduce-scatter.4.cloned.1.call-update
  138.9 0.0 all-reduce.2.cloned.1.call-start
  138.9 66.0 %reduce-scatter.4.cloned.1.call-done = f32[64,1024]{1,0:T(8,128)} async-done(((f32[1024,1024]{1,0:T(8,128)}), f32[64,1024]{1,0:T(8,128)}) %reduce-scatter.4.cloned.1.call-update) | async-done | bytes 262160
  204.9 1.9 copy.33
  206.9 0.0 all-reduce.2.cloned.1.call-update
  206.9 2.3 convolution_convert_fusion
  209.2 155.2 %all-reduce.2.cloned.1.call-done = f32[64,1024]{0,1:T(8,128)} async-done(((f32[64,1024]{0,1:T(8,128)}), f32[64,1024]{0,1:T(8,128)}) %all-reduce.2.cloned.1.call-update) | async-done | bytes 262160 | tf_op jit(solution)/shard_map/psum | solution.py:82
  364.4 1.1 broadcast_multiply_fusion
  365.4 0.9 copy.28
  (20 shorter events, 0.1 us)
Async XLA Ops:
  7.2 12.1 %copy-start = (bf16[1024,1024]{1,0:T(8,128)(2,1)S(1)}, bf16[1024,1024]{1,0:T(8,128)(2,1)}, u32[]{:S(2)}) copy-start(bf16[1024,1024]{1,0:T(8,128)(2,1)} %param.8) | copy-start | bytes 6291460
  8.8 18.0 %all-to-all-start = ((s32[16,1,1]{2,1,0:T(1,128)}), s32[16,1,1]{2,1,0:T(1,128)S(1)}, u32[]{:S(2)}, u32[]{:S(2)}) async-start(s32[16,1,1]{2,1,0:T(1,128)} %copy.26), calls=%async_computation | async-start | bytes 16384 | tf_op jit(solution)/shard_map/all_to_all | solution.py:36
  27.2 6.1 %copy-start.5 = (s32[512,16]{0,1:T(8,128)S(1)}, s32[512,16]{0,1:T(8,128)}, u32[]{:S(2)}) copy-start(s32[512,16]{0,1:T(8,128)} %param.12) | copy-start | bytes 98308
  27.2 6.3 %copy-start.6 = (s32[512,16]{0,1:T(8,128)S(1)}, s32[512,16]{0,1:T(8,128)}, u32[]{:S(2)}) copy-start(s32[512,16]{0,1:T(8,128)} %param.11) | copy-start | bytes 98308
  28.8 30.9 %all-to-all-start.1 = ((bf16[16,32,1024]{2,1,0:T(8,128)(2,1)}), bf16[16,32,1024]{2,1,0:T(8,128)(2,1)}, u32[]{:S(2)}, u32[]{:S(2)}) async-start(bf16[16,32,1024]{2,1,0:T(8,128)(2,1)} %gather_fusion), calls=%async_computation.1 | async-start | bytes 2097152 | tf_op jit(solution)/shard_map/all_to_all | solution.py:40
  66.0 2.6 copy-start.2
  69.0 1.4 copy-start.4
  70.5 2.8 copy-start.1
  88.4 31.3 %all-to-all-start.2 = ((bf16[16,32,1024]{2,1,0:T(8,128)(2,1)}), bf16[16,32,1024]{2,1,0:T(8,128)(2,1)S(1)}, u32[]{:S(2)}, u32[]{:S(2)}) async-start(bf16[16,32,1024]{2,1,0:T(8,128)(2,1)} %slice.16), calls=%async_computation.2 | async-start | bytes 2097152 | tf_op jit(solution)/shard_map/all_to_all | solution.py:63
  93.3 111.7 %reduce-scatter.4.cloned.1.call-start = ((), (), s32[]{:S(2)}) async-start(), calls=%async_computation.5 | async-start | bytes 4456448
  121.4 5.1 %copy-start.7 = (f32[1024]{0:T(1024)S(1)}, f32[1024]{0:T(1024)}, u32[]{:S(2)}) copy-start(f32[1024]{0:T(1024)} %param.9) | copy-start | bytes 12292
  126.5 3.7 copy-start.3
  138.9 225.5 %all-reduce.2.cloned.1.call-start = ((), (), s32[]{:S(2)}) async-start(), calls=%async_computation.4 | async-start | bytes 1048576 | tf_op jit(solution)/shard_map/psum | solution.py:82
Sparse Core Ops, SparseCore 0:
  139.0 65.8 reduce-scatter.3
  208.3 156.0 all-reduce.1
where the time goes:
time: 375 us; the launch traced here: 373 us
  waiting for transfers between devices  267 us (71%)
  other arithmetic  33.9 us (9%)
  local copies, waits for them, and re-layouts  23.5 us (6%)
  starting transfers between devices  19.7 us (5%)
  matrix products  14.7 us (4%)
  between operations  14.2 us (4%)
    psum x1, waiting for transfers between devices, on_device(): transform_grad = lax.psum(row_share, 'group') * factor  155 us
    unnamed x3, waiting for transfers between devices  66.1 us
    all_to_all x1, waiting for transfers between devices, on_device(): lax.all_to_all(returned, 'member', split_axis=0, concat_axis=0, tiled=True)  22.9 us
    all_to_all x1, waiting for transfers between devices, on_device(): lax.all_to_all(own_tiles[served], 'member', split_axis=0, concat_axis=0,...  19.4 us
    all_to_all x1, starting transfers between devices, on_device(): lax.all_to_all(wanted.reshape(members, 1), 'member', split_axis=0, concat...  10.4 us
    scatter-add x1, other arithmetic, on_device(): jax.ops.segment_sum(cand_grad, pool_index, num_segments=pool_size)  10 us
    unnamed x19, local copies, waits for them, and re-layouts  8.22 us
  transfers between devices with their start and end apart: 5, of which 5 were waited for; matrix products, arithmetic and copies ran while one was open for 4% of the time, Pallas kernels for 0%

commit v1 on v0

--- a/solution.py
+++ b/solution.py
@@ -12,6 +12,28 @@
     columns = lax.broadcasted_iota(jnp.int32, slot_rows.shape + (cand_width,), slot_rows.ndim)
     matched_weights = jnp.where(slot_rows[..., None] == columns, weights[..., None], 0)
     return jnp.sum(matched_weights, axis=-2).astype(jnp.bfloat16)
+
+
+def xor_pairs(n, bit):
+    return [(i, i ^ (1 << bit)) for i in range(n)]
+
+
+def reduce_rows(part):
+    members = lax.axis_size("member")
+    groups = lax.axis_size("group")
+    member_here = lax.axis_index("member")
+    rows, cols = part.shape
+    acc = part.reshape(members, rows // members, cols)
+    for k in range(members.bit_length() - 1):
+        pairs = acc.reshape(acc.shape[0] // 2, 2, *acc.shape[1:])
+        bit = (member_here >> k) & 1
+        keep = lax.dynamic_index_in_dim(pairs, bit, 1, keepdims=False)
+        send = lax.dynamic_index_in_dim(pairs, 1 - bit, 1, keepdims=False)
+        acc = keep + lax.ppermute(send, "member", xor_pairs(members, k))
+    acc = acc.reshape(rows // members, cols)
+    for k in range(groups.bit_length() - 1):
+        acc = acc + lax.ppermute(acc, "group", xor_pairs(groups, k))
+    return acc
 
 
 def on_device(feats, transform, bias, tile_list, nbr_slot, nbr_weight, cotangent):
@@ -70,16 +92,11 @@
     feat_grad = lax.dot_general(
         pre_grad, transform, (((1,), (1,)), ((), ())), preferred_element_type=jnp.float32
     ).astype(jnp.bfloat16)
-    row_share = lax.psum_scatter(
-        lax.dot_general(
-            feats, pre_grad, (((0,), (0,)), ((), ())), preferred_element_type=jnp.float32
-        ),
-        "member",
-        scatter_dimension=0,
-        tiled=True,
+    partial = lax.dot_general(
+        feats, pre_grad, (((0,), (0,)), ((), ())), preferred_element_type=jnp.float32
     )
     factor = 1.0 / math.sqrt(rows_dev * members * groups)
-    transform_grad = lax.psum(row_share, "group") * factor
+    transform_grad = reduce_rows(partial) * factor
     return (embedding, feat_grad, transform_grad)
 
 

time: 375 us -> 282 us (0.75)
  waiting for transfers between devices: 267 us -> 151 us
  starting transfers between devices: 19.7 us -> 52.7 us
  between operations: 14.2 us -> 0.95 us
  other arithmetic: 33.9 us -> 40.2 us
    psum x1 -> x0, waiting for transfers between devices: 155 us -> none  [on_device(): transform_grad = lax.psum(row_share, 'group') * factor]
    ppermute x0 -> x9, waiting for transfers between devices: none -> 105 us  [the longest x4 68.8 us: reduce_rows(): acc = keep + lax.ppermute(send, 'member', xor_pairs(members, k))]
    unnamed x3 -> x0, waiting for transfers between devices: 66.1 us -> none
    ppermute x0 -> x9, starting transfers between devices: none -> 33.1 us  [the longest x5 21.6 us: reduce_rows(): acc = acc + lax.ppermute(acc, 'group', xor_pairs(groups, k))]
    add x0 -> x7, other arithmetic: none -> 5.67 us  [the longest x3 5.55 us: reduce_rows(): acc = keep + lax.ppermute(send, 'member', xor_pairs(members, k))]
    unnamed x19 -> x24, local copies, waits for them, and re-layouts: 8.22 us -> 4.08 us
  transfers between devices with their start and end apart: 5 -> 12, of which waited for: 5 -> 12; matrix products, arithmetic and copies ran while one was open for 4% -> 6% of each run, Pallas kernels for 0% -> 0%
where the time goes in v1:
time: 282 us; the launch traced here: 281 us
  waiting for transfers between devices  151 us (54%)
  starting transfers between devices  52.7 us (19%)
  other arithmetic  40.2 us (14%)
  local copies, waits for them, and re-layouts  22.9 us (8%)
  matrix products  12.7 us (5%)
    ppermute x4, waiting for transfers between devices, reduce_rows(): acc = keep + lax.ppermute(send, 'member', xor_pairs(members, k))  68.8 us
    ppermute x5, waiting for transfers between devices, reduce_rows(): acc = acc + lax.ppermute(acc, 'group', xor_pairs(groups, k))  36.5 us
    all_to_all x1, waiting for transfers between devices, on_device(): lax.all_to_all(returned, 'member', split_axis=0, concat_axis=0, tiled=True)  22.9 us
    ppermute x5, starting transfers between devices, reduce_rows(): acc = acc + lax.ppermute(acc, 'group', xor_pairs(groups, k))  21.6 us
    all_to_all x1, waiting for transfers between devices, on_device(): lax.all_to_all(own_tiles[served], 'member', split_axis=0, concat_axis=0,...  19.4 us
    ppermute x4, starting transfers between devices, reduce_rows(): acc = keep + lax.ppermute(send, 'member', xor_pairs(members, k))  11.6 us
    all_to_all x1, starting transfers between devices, on_device(): lax.all_to_all(wanted.reshape(members, 1), 'member', split_axis=0, concat...  10.4 us
    scatter-add x1, other arithmetic, on_device(): jax.ops.segment_sum(cand_grad, pool_index, num_segments=pool_size)  10 us
  transfers between devices with their start and end apart: 12, of which 12 were waited for; matrix products, arithmetic and copies ran while one was open for 6% of the time, Pallas kernels for 0%

profile of v1, /device:TPU:6, one launch (start us, length us, event | category | flops | bytes accessed | tf_op | source)
XLA Modules:
  0.0 280.9 jit_solution(13433944353572246631)
XLA Ops:
  2.3 10.4 %all-to-all-start = ((s32[16,1,1]{2,1,0:T(1,128)}), s32[16,1,1]{2,1,0:T(1,128)S(1)}, u32[]{:S(2)}, u32[]{:S(2)}) async-start(s32[16,1,1]{2,1,0:T(1,128)} %copy.29), calls=%async_computation | async-start | bytes 16384 | tf_op jit(solution)/shard_map/all_to_all | solution.py:58
  12.7 3.8 %maximum_convert_fusion = (bf16[512,1024]{1,0:T(8,128)(2,1)S(1)}, f32[512,1024]{1,0:T(8,128)}) fusion(f32[1024]{0:T(1024)} %param.9, bf16[512,1024]{1,0:T(8,128)(2,1)} %param.7, bf16[1024,1024]{1,0:T(8,128)(2,1)S(1)} %copy-done), kind=kOutput, calls=%fused_computation.21 | convolution fusion | flops 1075314688 | bytes 6295552 | tf_op jit(solution)/shard_map/dot_general | solution.py:49
  16.6 3.7 %all-to-all-done = s32[16,1,1]{2,1,0:T(1,128)S(1)} async-done(((s32[16,1,1]{2,1,0:T(1,128)}), s32[16,1,1]{2,1,0:T(1,128)S(1)}, u32[]{:S(2)}, u32[]{:S(2)}) %all-to-all-start) | async-done | bytes 96 | tf_op jit(solution)/shard_map/all_to_all | solution.py:58
  20.7 1.6 gather_fusion
  22.2 4.3 %all-to-all-start.1 = ((bf16[16,32,1024]{2,1,0:T(8,128)(2,1)}), bf16[16,32,1024]{2,1,0:T(8,128)(2,1)}, u32[]{:S(2)}, u32[]{:S(2)}) async-start(bf16[16,32,1024]{2,1,0:T(8,128)(2,1)} %gather_fusion), calls=%async_computation.1 | async-start | bytes 2097152 | tf_op jit(solution)/shard_map/all_to_all | solution.py:62
  27.8 5.9 %select_reduce_fusion = s32[4,128,256]{2,1,0:T(8,128)} fusion(s32[4,128,16]{2,1,0:T(8,128)S(1)} %bitcast.66, s32[4,128,16]{2,1,0:T(8,128)} %bitcast.67), kind=kLoop, calls=%fused_computation.4 | loop fusion | flops 6160384 | bytes 589824 | tf_op jit(solution)/shard_map/reduce_sum | solution.py:14
  33.7 19.4 %all-to-all-done.1 = bf16[16,32,1024]{2,1,0:T(8,128)(2,1)} async-done(((bf16[16,32,1024]{2,1,0:T(8,128)(2,1)}), bf16[16,32,1024]{2,1,0:T(8,128)(2,1)}, u32[]{:S(2)}, u32[]{:S(2)}) %all-to-all-start.1) | async-done | bytes 1048608 | tf_op jit(solution)/shard_map/all_to_all | solution.py:62
  53.1 2.7 pad_maximum_fusion
  55.9 3.6 %gather_fusion.1 = bf16[32,32,1024]{2,1,0:T(8,128)(2,1)} fusion(bf16[32,32,1024]{2,1,0:T(8,128)(2,1)} %pad_maximum_fusion, s32[1024]{0:T(1024)S(1)} %pad_clamp_fusion), kind=kCustom, calls=%fused_computation.1 | custom fusion | bytes 4194432 | tf_op jit(solution)/shard_map/gather | solution.py:65
  59.4 2.6 multiply_reduce_fusion
  62.5 1.4 fusion.1
  63.9 2.8 fusion.4
  66.7 2.5 broadcast_in_dim.61
  69.1 10.0 %scatter_fusion = f32[32,32,1024]{2,1,0:T(8,128)} fusion(f32[32,32,1024]{2,1,0:T(8,128)} %broadcast_in_dim.61, s32[32]{0:T(128)S(1)} %reshape.159, f32[32,32,1024]{2,1,0:T(8,128)} %bitcast.58), kind=kCustom, calls=%fused_computation.2 | custom fusion | flops 1048576 | bytes 12583040 | tf_op jit(solution)/shard_map/scatter-add | solution.py:83
  79.2 2.7 slice.16
  81.9 4.8 %all-to-all-start.2 = ((bf16[16,32,1024]{2,1,0:T(8,128)(2,1)}), bf16[16,32,1024]{2,1,0:T(8,128)(2,1)S(1)}, u32[]{:S(2)}, u32[]{:S(2)}) async-start(bf16[16,32,1024]{2,1,0:T(8,128)(2,1)} %slice.16), calls=%async_computation.2 | async-start | bytes 2097152 | tf_op jit(solution)/shard_map/all_to_all | solution.py:85
  87.1 3.2 %slice.13 = f32[16,32,1024]{2,1,0:T(8,128)} slice(f32[32,32,1024]{2,1,0:T(8,128)} %scatter_fusion), slice={[16:32], [0:32], [0:1024]} | slice | bytes 4194304 | tf_op jit(solution)/shard_map/slice | solution.py:87
  90.2 22.9 %all-to-all-done.2 = bf16[16,32,1024]{2,1,0:T(8,128)(2,1)S(1)} async-done(((bf16[16,32,1024]{2,1,0:T(8,128)(2,1)}), bf16[16,32,1024]{2,1,0:T(8,128)(2,1)S(1)}, u32[]{:S(2)}, u32[]{:S(2)}) %all-to-all-start.2) | async-done | bytes 1048608 | tf_op jit(solution)/shard_map/all_to_all | solution.py:85
  113.2 1.7 convert_select_fusion
  114.9 5.1 %scatter_fusion.1 = f32[16,32,1024]{2,1,0:T(8,128)} fusion(f32[16,32,1024]{2,1,0:T(8,128)} %slice.13, s32[16]{0:T(128)S(1)} %fusion.10, f32[16,32,1024]{2,1,0:T(8,128)} %convert_select_fusion), kind=kCustom, calls=%fused_computation.3 | custom fusion | flops 524288 | bytes 6291520 | tf_op jit(solution)/shard_map/scatter-add | solution.py:87
  119.9 3.7 %fusion.3 = bf16[512,1024]{1,0:T(8,128)(2,1)S(1)} fusion(f32[16,32,1024]{2,1,0:T(8,128)} %scatter_fusion.1, f32[4,128,1024]{2,1,0:T(8,128)} %copy-done.3, f32[512,1024]{1,0:T(8,128)} %get-tuple-element.9, f32[1024]{0:T(1024)S(1)} %copy-done.11), kind=kLoop, calls=%fused_computation.16 | loop fusion | flops 2621440 | bytes 7344128 | tf_op jit(solution)/shard_map/convert_element_type | solution.py:91
  123.7 1.3 fusion.12
  125.0 1.6 dynamic-slice_bitcast_fusion
  127.6 3.9 %collective-permute-start = (f32[8,64,1024]{2,1,0:T(8,128)}, f32[8,64,1024]{2,1,0:T(8,128)}, u32[]{:S(2)}, u32[]{:S(2)}) collective-permute-start(f32[8,64,1024]{2,1,0:T(8,128)} %dynamic-slice_bitcast_fusion), channel_id=1, source_target_pairs={{0,1},{1,0},{2,3},{3,2},{4,5},{5,4},{6,7},{7,6},{8,9},{9,8},{10,11... | collective-permute-start | bytes 6291464 | tf_op jit(solution)/shard_map/ppermute | solution.py:32
  131.5 4.1 %collective-permute-done = f32[8,64,1024]{2,1,0:T(8,128)} collective-permute-done((f32[8,64,1024]{2,1,0:T(8,128)}, f32[8,64,1024]{2,1,0:T(8,128)}, u32[]{:S(2)}, u32[]{:S(2)}) %collective-permute-start) | collective-permute-done | bytes 2097184 | tf_op jit(solution)/shard_map/ppermute | solution.py:32
  135.6 2.6 bitcast_add_fusion
  138.2 1.3 copy-done.2
  139.5 1.0 dynamic-slice_bitcast_fusion.1
  140.6 1.9 collective-permute-start.1
  142.5 25.7 %collective-permute-done.1 = f32[4,64,1024]{2,1,0:T(8,128)} collective-permute-done((f32[4,64,1024]{2,1,0:T(8,128)}, f32[4,64,1024]{2,1,0:T(8,128)}, u32[]{:S(2)}, u32[]{:S(2)}) %collective-permute-start.1) | collective-permute-done | bytes 1048608 | tf_op jit(solution)/shard_map/ppermute | solution.py:32
  168.2 1.7 bitcast_add_fusion.2
  171.7 2.3 collective-permute-start.2
  174.1 25.3 %collective-permute-done.2 = f32[2,64,1024]{2,1,0:T(8,128)} collective-permute-done((f32[2,64,1024]{2,1,0:T(8,128)}, f32[2,64,1024]{2,1,0:T(8,128)}, u32[]{:S(2)}, u32[]{:S(2)}) %collective-permute-start.2) | collective-permute-done | bytes 524320 | tf_op jit(solution)/shard_map/ppermute | solution.py:32
  199.4 1.3 bitcast_add_fusion.3
  201.5 3.4 %collective-permute-start.3 = (f32[1,64,1024]{2,1,0:T(8,128)S(1)}, f32[1,64,1024]{2,1,0:T(8,128)}, u32[]{:S(2)}, u32[]{:S(2)}) collective-permute-start(f32[1,64,1024]{2,1,0:T(8,128)S(1)} %constant_dynamic-slice_fusion), channel_id=1, source_target_pairs={{0,8},{1,9},{2,10},{3,11},{4,12},{5,13},{6,14},{7,15},{8,0},{9,1},... | collective-permute-start | bytes 786440 | tf_op jit(solution)/shard_map/ppermute | solution.py:32
  204.9 13.6 %collective-permute-done.3 = f32[1,64,1024]{2,1,0:T(8,128)} collective-permute-done((f32[1,64,1024]{2,1,0:T(8,128)S(1)}, f32[1,64,1024]{2,1,0:T(8,128)}, u32[]{:S(2)}, u32[]{:S(2)}) %collective-permute-start.3) | collective-permute-done | bytes 262176 | tf_op jit(solution)/shard_map/ppermute | solution.py:32
  218.5 1.1 add_bitcast_fusion
  219.6 2.9 %collective-permute-start.4 = (f32[64,1024]{1,0:T(8,128)S(1)}, f32[64,1024]{1,0:T(8,128)S(1)}, u32[]{:S(2)}, u32[]{:S(2)}) collective-permute-start(f32[64,1024]{1,0:T(8,128)S(1)} %add_bitcast_fusion), channel_id=1, source_target_pairs={{0,16},{16,0},{32,48},{48,32},{64,80},{80,64},{96,112},{112,96},{1... | collective-permute-start | bytes 786440 | tf_op jit(solution)/shard_map/ppermute | solution.py:35
  222.5 6.4 %collective-permute-done.4 = f32[64,1024]{1,0:T(8,128)S(1)} collective-permute-done((f32[64,1024]{1,0:T(8,128)S(1)}, f32[64,1024]{1,0:T(8,128)S(1)}, u32[]{:S(2)}, u32[]{:S(2)}) %collective-permute-start.4) | collective-permute-done | bytes 262176 | tf_op jit(solution)/shard_map/ppermute | solution.py:35
  229.0 3.0 %collective-permute-start.5 = (f32[64,1024]{1,0:T(8,128)S(1)}, f32[64,1024]{1,0:T(8,128)S(1)}, u32[]{:S(2)}, u32[]{:S(2)}) collective-permute-start(f32[64,1024]{1,0:T(8,128)S(1)} %add.146), channel_id=1, source_target_pairs={{0,32},{16,48},{32,0},{48,16},{64,96},{80,112},{96,64},{112,80},{1... | collective-permute-start | bytes 786440 | tf_op jit(solution)/shard_map/ppermute | solution.py:35
  232.0 7.1 %collective-permute-done.5 = f32[64,1024]{1,0:T(8,128)S(1)} collective-permute-done((f32[64,1024]{1,0:T(8,128)S(1)}, f32[64,1024]{1,0:T(8,128)S(1)}, u32[]{:S(2)}, u32[]{:S(2)}) %collective-permute-start.5) | collective-permute-done | bytes 262176 | tf_op jit(solution)/shard_map/ppermute | solution.py:35
  239.1 3.8 %collective-permute-start.6 = (f32[64,1024]{1,0:T(8,128)S(1)}, f32[64,1024]{1,0:T(8,128)S(1)}, u32[]{:S(2)}, u32[]{:S(2)}) collective-permute-start(f32[64,1024]{1,0:T(8,128)S(1)} %add.147), channel_id=1, source_target_pairs={{0,64},{16,80},{32,96},{48,112},{64,0},{80,16},{96,32},{112,48},{1... | collective-permute-start | bytes 786440 | tf_op jit(solution)/shard_map/ppermute | solution.py:35
  242.9 4.5 %collective-permute-done.6 = f32[64,1024]{1,0:T(8,128)S(1)} collective-permute-done((f32[64,1024]{1,0:T(8,128)S(1)}, f32[64,1024]{1,0:T(8,128)S(1)}, u32[]{:S(2)}, u32[]{:S(2)}) %collective-permute-start.6) | collective-permute-done | bytes 262176 | tf_op jit(solution)/shard_map/ppermute | solution.py:35
  247.4 5.3 %collective-permute-start.7 = (f32[64,1024]{1,0:T(8,128)S(1)}, f32[64,1024]{1,0:T(8,128)S(1)}, u32[]{:S(2)}, u32[]{:S(2)}) collective-permute-start(f32[64,1024]{1,0:T(8,128)S(1)} %add.148), channel_id=1, source_target_pairs={{0,128},{16,144},{32,160},{48,176},{64,192},{80,208},{96,224},{112... | collective-permute-start | bytes 786440 | tf_op jit(solution)/shard_map/ppermute | solution.py:35
  252.7 8.8 %collective-permute-done.7 = f32[64,1024]{1,0:T(8,128)S(1)} collective-permute-done((f32[64,1024]{1,0:T(8,128)S(1)}, f32[64,1024]{1,0:T(8,128)S(1)}, u32[]{:S(2)}, u32[]{:S(2)}) %collective-permute-start.7) | collective-permute-done | bytes 262176 | tf_op jit(solution)/shard_map/ppermute | solution.py:35
  261.5 6.6 %collective-permute-start.8 = (f32[64,1024]{1,0:T(8,128)S(1)}, f32[64,1024]{1,0:T(8,128)S(1)}, u32[]{:S(2)}, u32[]{:S(2)}) collective-permute-start(f32[64,1024]{1,0:T(8,128)S(1)} %add.149), channel_id=1, source_target_pairs={{0,256},{16,272},{32,288},{48,304},{64,320},{80,336},{96,352},{112... | collective-permute-start | bytes 786440 | tf_op jit(solution)/shard_map/ppermute | solution.py:35
  268.1 2.3 convolution_convert_fusion
  270.4 9.7 %collective-permute-done.8 = f32[64,1024]{1,0:T(8,128)S(1)} collective-permute-done((f32[64,1024]{1,0:T(8,128)S(1)}, f32[64,1024]{1,0:T(8,128)S(1)}, u32[]{:S(2)}, u32[]{:S(2)}) %collective-permute-start.8) | collective-permute-done | bytes 262176 | tf_op jit(solution)/shard_map/ppermute | solution.py:35
  (49 shorter events, 8.5 us)
Async XLA Ops:
  0.6 12.1 %copy-start = (bf16[1024,1024]{1,0:T(8,128)(2,1)S(1)}, bf16[1024,1024]{1,0:T(8,128)(2,1)}, u32[]{:S(2)}) copy-start(bf16[1024,1024]{1,0:T(8,128)(2,1)} %param.8) | copy-start | bytes 6291460
  2.3 18.0 %all-to-all-start = ((s32[16,1,1]{2,1,0:T(1,128)}), s32[16,1,1]{2,1,0:T(1,128)S(1)}, u32[]{:S(2)}, u32[]{:S(2)}) async-start(s32[16,1,1]{2,1,0:T(1,128)} %copy.29), calls=%async_computation | async-start | bytes 16384 | tf_op jit(solution)/shard_map/all_to_all | solution.py:58
  20.6 6.1 %copy-start.9 = (s32[512,16]{0,1:T(8,128)S(1)}, s32[512,16]{0,1:T(8,128)}, u32[]{:S(2)}) copy-start(s32[512,16]{0,1:T(8,128)} %param.12) | copy-start | bytes 98308
  20.7 6.3 %copy-start.10 = (s32[512,16]{0,1:T(8,128)S(1)}, s32[512,16]{0,1:T(8,128)}, u32[]{:S(2)}) copy-start(s32[512,16]{0,1:T(8,128)} %param.11) | copy-start | bytes 98308
  22.2 30.9 %all-to-all-start.1 = ((bf16[16,32,1024]{2,1,0:T(8,128)(2,1)}), bf16[16,32,1024]{2,1,0:T(8,128)(2,1)}, u32[]{:S(2)}, u32[]{:S(2)}) async-start(bf16[16,32,1024]{2,1,0:T(8,128)(2,1)} %gather_fusion), calls=%async_computation.1 | async-start | bytes 2097152 | tf_op jit(solution)/shard_map/all_to_all | solution.py:62
  59.4 2.6 copy-start.5
  62.5 1.4 copy-start.8
  63.9 2.8 copy-start.3
  81.9 31.3 %all-to-all-start.2 = ((bf16[16,32,1024]{2,1,0:T(8,128)(2,1)}), bf16[16,32,1024]{2,1,0:T(8,128)(2,1)S(1)}, u32[]{:S(2)}, u32[]{:S(2)}) async-start(bf16[16,32,1024]{2,1,0:T(8,128)(2,1)} %slice.16), calls=%async_computation.2 | async-start | bytes 2097152 | tf_op jit(solution)/shard_map/all_to_all | solution.py:85
  114.9 5.1 %copy-start.11 = (f32[1024]{0:T(1024)S(1)}, f32[1024]{0:T(1024)}, u32[]{:S(2)}) copy-start(f32[1024]{0:T(1024)} %param.9) | copy-start | bytes 12292
  119.9 3.7 %copy-start.7 = (bf16[512,1024]{1,0:T(8,128)(2,1)S(1)}, bf16[512,1024]{1,0:T(8,128)(2,1)}, u32[]{:S(2)}) copy-start(bf16[512,1024]{1,0:T(8,128)(2,1)} %param.7) | copy-start | bytes 3145732
  125.0 2.6 copy-start.1
  127.6 8.0 %collective-permute-start = (f32[8,64,1024]{2,1,0:T(8,128)}, f32[8,64,1024]{2,1,0:T(8,128)}, u32[]{:S(2)}, u32[]{:S(2)}) collective-permute-start(f32[8,64,1024]{2,1,0:T(8,128)} %dynamic-slice_bitcast_fusion), channel_id=1, source_target_pairs={{0,1},{1,0},{2,3},{3,2},{4,5},{5,4},{6,7},{7,6},{8,9},{9,8},{10,11... | collective-permute-start | bytes 6291464 | tf_op jit(solution)/shard_map/ppermute | solution.py:32
  138.2 1.3 copy-start.2
  140.6 27.6 %collective-permute-start.1 = (f32[4,64,1024]{2,1,0:T(8,128)}, f32[4,64,1024]{2,1,0:T(8,128)}, u32[]{:S(2)}, u32[]{:S(2)}) collective-permute-start(f32[4,64,1024]{2,1,0:T(8,128)} %dynamic-slice_bitcast_fusion.1), channel_id=1, source_target_pairs={{0,2},{1,3},{2,0},{3,1},{4,6},{5,7},{6,4},{7,5},{8,10},{9,11},{10,... | collective-permute-start | bytes 3145736 | tf_op jit(solution)/shard_map/ppermute | solution.py:32
  169.9 1.0 copy-start.4
  171.7 27.7 %collective-permute-start.2 = (f32[2,64,1024]{2,1,0:T(8,128)}, f32[2,64,1024]{2,1,0:T(8,128)}, u32[]{:S(2)}, u32[]{:S(2)}) collective-permute-start(f32[2,64,1024]{2,1,0:T(8,128)} %dynamic-slice_bitcast_fusion.2), channel_id=1, source_target_pairs={{0,4},{1,5},{2,6},{3,7},{4,0},{5,1},{6,2},{7,3},{8,12},{9,13},{10,... | collective-permute-start | bytes 1572872 | tf_op jit(solution)/shard_map/ppermute | solution.py:32
  200.6 0.8 copy-start.6
  201.5 17.1 %collective-permute-start.3 = (f32[1,64,1024]{2,1,0:T(8,128)S(1)}, f32[1,64,1024]{2,1,0:T(8,128)}, u32[]{:S(2)}, u32[]{:S(2)}) collective-permute-start(f32[1,64,1024]{2,1,0:T(8,128)S(1)} %constant_dynamic-slice_fusion), channel_id=1, source_target_pairs={{0,8},{1,9},{2,10},{3,11},{4,12},{5,13},{6,14},{7,15},{8,0},{9,1},... | collective-permute-start | bytes 786440 | tf_op jit(solution)/shard_map/ppermute | solution.py:32
  219.6 9.4 %collective-permute-start.4 = (f32[64,1024]{1,0:T(8,128)S(1)}, f32[64,1024]{1,0:T(8,128)S(1)}, u32[]{:S(2)}, u32[]{:S(2)}) collective-permute-start(f32[64,1024]{1,0:T(8,128)S(1)} %add_bitcast_fusion), channel_id=1, source_target_pairs={{0,16},{16,0},{32,48},{48,32},{64,80},{80,64},{96,112},{112,96},{1... | collective-permute-start | bytes 786440 | tf_op jit(solution)/shard_map/ppermute | solution.py:35
  229.0 10.0 %collective-permute-start.5 = (f32[64,1024]{1,0:T(8,128)S(1)}, f32[64,1024]{1,0:T(8,128)S(1)}, u32[]{:S(2)}, u32[]{:S(2)}) collective-permute-start(f32[64,1024]{1,0:T(8,128)S(1)} %add.146), channel_id=1, source_target_pairs={{0,32},{16,48},{32,0},{48,16},{64,96},{80,112},{96,64},{112,80},{1... | collective-permute-start | bytes 786440 | tf_op jit(solution)/shard_map/ppermute | solution.py:35
  239.1 8.3 %collective-permute-start.6 = (f32[64,1024]{1,0:T(8,128)S(1)}, f32[64,1024]{1,0:T(8,128)S(1)}, u32[]{:S(2)}, u32[]{:S(2)}) collective-permute-start(f32[64,1024]{1,0:T(8,128)S(1)} %add.147), channel_id=1, source_target_pairs={{0,64},{16,80},{32,96},{48,112},{64,0},{80,16},{96,32},{112,48},{1... | collective-permute-start | bytes 786440 | tf_op jit(solution)/shard_map/ppermute | solution.py:35
  247.4 14.1 %collective-permute-start.7 = (f32[64,1024]{1,0:T(8,128)S(1)}, f32[64,1024]{1,0:T(8,128)S(1)}, u32[]{:S(2)}, u32[]{:S(2)}) collective-permute-start(f32[64,1024]{1,0:T(8,128)S(1)} %add.148), channel_id=1, source_target_pairs={{0,128},{16,144},{32,160},{48,176},{64,192},{80,208},{96,224},{112... | collective-permute-start | bytes 786440 | tf_op jit(solution)/shard_map/ppermute | solution.py:35
  261.5 18.6 %collective-permute-start.8 = (f32[64,1024]{1,0:T(8,128)S(1)}, f32[64,1024]{1,0:T(8,128)S(1)}, u32[]{:S(2)}, u32[]{:S(2)}) collective-permute-start(f32[64,1024]{1,0:T(8,128)S(1)} %add.149), channel_id=1, source_target_pairs={{0,256},{16,272},{32,288},{48,304},{64,320},{80,336},{96,352},{112... | collective-permute-start | bytes 786440 | tf_op jit(solution)/shard_map/ppermute | solution.py:35

commit v2 on v1

--- a/solution.py
+++ b/solution.py
@@ -29,10 +29,13 @@
         bit = (member_here >> k) & 1
         keep = lax.dynamic_index_in_dim(pairs, bit, 1, keepdims=False)
         send = lax.dynamic_index_in_dim(pairs, 1 - bit, 1, keepdims=False)
-        acc = keep + lax.ppermute(send, "member", xor_pairs(members, k))
+        sent = lax.ppermute(send.astype(jnp.bfloat16), "member", xor_pairs(members, k))
+        acc = keep + sent.astype(jnp.float32)
     acc = acc.reshape(rows // members, cols)
     for k in range(groups.bit_length() - 1):
-        acc = acc + lax.ppermute(acc, "group", xor_pairs(groups, k))
+        mine = acc.astype(jnp.bfloat16)
+        theirs = lax.ppermute(mine, "group", xor_pairs(groups, k))
+        acc = mine.astype(jnp.float32) + theirs.astype(jnp.float32)
     return acc
 
 

time: 282 us -> 235 us (0.83)
  waiting for transfers between devices: 151 us -> 103 us
    ppermute x9, waiting for transfers between devices: 105 us -> 57.5 us  [the longest x4 39.3 us: reduce_rows(): lax.ppermute(send.astype(jnp.bfloat16), 'member', xor_pairs(members, k))]
    squeeze x4 -> x0, local copies, waits for them, and re-layouts: 3.48 us -> none  [reduce_rows(): send = lax.dynamic_index_in_dim(pairs, 1 - bit, 1, keepdims=False)]
    add x7 -> x3, other arithmetic: 5.67 us -> 4.84 us  [reduce_rows(): acc = keep + sent.astype(jnp.float32)]
  transfers between devices with their start and end apart: 12 -> 12, of which waited for: 12 -> 12; matrix products, arithmetic and copies ran while one was open for 6% -> 7% of each run, Pallas kernels for 0% -> 0%
where the time goes in v2:
time: 235 us; the launch traced here: 233 us
  waiting for transfers between devices  103 us (44%)
  starting transfers between devices  53 us (23%)
  other arithmetic  39.6 us (17%)
  local copies, waits for them, and re-layouts  23.1 us (10%)
  matrix products  12.7 us (5%)
    ppermute x4, waiting for transfers between devices, reduce_rows(): lax.ppermute(send.astype(jnp.bfloat16), 'member', xor_pairs(members, k))  39.3 us
    all_to_all x1, waiting for transfers between devices, on_device(): lax.all_to_all(returned, 'member', split_axis=0, concat_axis=0, tiled=True)  22.9 us
    ppermute x5, starting transfers between devices, reduce_rows(): theirs = lax.ppermute(mine, 'group', xor_pairs(groups, k))  21.8 us
    all_to_all x1, waiting for transfers between devices, on_device(): lax.all_to_all(own_tiles[served], 'member', split_axis=0, concat_axis=0,...  19.4 us
    ppermute x5, waiting for transfers between devices, reduce_rows(): theirs = lax.ppermute(mine, 'group', xor_pairs(groups, k))  18.1 us
    ppermute x4, starting transfers between devices, reduce_rows(): lax.ppermute(send.astype(jnp.bfloat16), 'member', xor_pairs(members, k))  11.6 us
    all_to_all x1, starting transfers between devices, on_device(): lax.all_to_all(wanted.reshape(members, 1), 'member', split_axis=0, concat...  10.4 us
    scatter-add x1, other arithmetic, on_device(): jax.ops.segment_sum(cand_grad, pool_index, num_segments=pool_size)  10.1 us
  transfers between devices with their start and end apart: 12, of which 12 were waited for; matrix products, arithmetic and copies ran while one was open for 7% of the time, Pallas kernels for 0%

profile of v2, /device:TPU:6, one launch (start us, length us, event | category | flops | bytes accessed | tf_op | source)
XLA Modules:
  0.0 232.8 jit_solution(17449207556838736013)
XLA Ops:
  2.3 10.4 %all-to-all-start = ((s32[16,1,1]{2,1,0:T(1,128)}), s32[16,1,1]{2,1,0:T(1,128)S(1)}, u32[]{:S(2)}, u32[]{:S(2)}) async-start(s32[16,1,1]{2,1,0:T(1,128)} %copy.32), calls=%async_computation | async-start | bytes 16384 | tf_op jit(solution)/shard_map/all_to_all | solution.py:61
  12.7 3.8 %maximum_convert_fusion = (bf16[512,1024]{1,0:T(8,128)(2,1)S(1)}, f32[512,1024]{1,0:T(8,128)}) fusion(f32[1024]{0:T(1024)} %param.9, bf16[512,1024]{1,0:T(8,128)(2,1)} %param.7, bf16[1024,1024]{1,0:T(8,128)(2,1)S(1)} %copy-done), kind=kOutput, calls=%fused_computation.21 | convolution fusion | flops 1075314688 | bytes 6295552 | tf_op jit(solution)/shard_map/dot_general | solution.py:52
  16.6 3.7 %all-to-all-done = s32[16,1,1]{2,1,0:T(1,128)S(1)} async-done(((s32[16,1,1]{2,1,0:T(1,128)}), s32[16,1,1]{2,1,0:T(1,128)S(1)}, u32[]{:S(2)}, u32[]{:S(2)}) %all-to-all-start) | async-done | bytes 96 | tf_op jit(solution)/shard_map/all_to_all | solution.py:61
  20.7 1.6 gather_fusion
  22.2 4.3 %all-to-all-start.1 = ((bf16[16,32,1024]{2,1,0:T(8,128)(2,1)}), bf16[16,32,1024]{2,1,0:T(8,128)(2,1)}, u32[]{:S(2)}, u32[]{:S(2)}) async-start(bf16[16,32,1024]{2,1,0:T(8,128)(2,1)} %gather_fusion), calls=%async_computation.1 | async-start | bytes 2097152 | tf_op jit(solution)/shard_map/all_to_all | solution.py:65
  27.8 5.9 %select_reduce_fusion = s32[4,128,256]{2,1,0:T(8,128)} fusion(s32[4,128,16]{2,1,0:T(8,128)S(1)} %bitcast.70, s32[4,128,16]{2,1,0:T(8,128)} %bitcast.71), kind=kLoop, calls=%fused_computation.4 | loop fusion | flops 6160384 | bytes 589824 | tf_op jit(solution)/shard_map/reduce_sum | solution.py:14
  33.7 19.4 %all-to-all-done.1 = bf16[16,32,1024]{2,1,0:T(8,128)(2,1)} async-done(((bf16[16,32,1024]{2,1,0:T(8,128)(2,1)}), bf16[16,32,1024]{2,1,0:T(8,128)(2,1)}, u32[]{:S(2)}, u32[]{:S(2)}) %all-to-all-start.1) | async-done | bytes 1048608 | tf_op jit(solution)/shard_map/all_to_all | solution.py:65
  53.1 2.7 %pad_maximum_fusion = bf16[32,32,1024]{2,1,0:T(8,128)(2,1)} fusion(bf16[16,32,1024]{2,1,0:T(8,128)(2,1)S(1)} %bitcast.64, bf16[16,32,1024]{2,1,0:T(8,128)(2,1)} %all-to-all-done.1), kind=kLoop, calls=%fused_computation.11 | loop fusion | flops 1048576 | bytes 4194304 | tf_op jit(solution)/shard_map/concatenate | solution.py:66
  55.9 3.6 %gather_fusion.1 = bf16[32,32,1024]{2,1,0:T(8,128)(2,1)} fusion(bf16[32,32,1024]{2,1,0:T(8,128)(2,1)} %pad_maximum_fusion, s32[1024]{0:T(1024)S(1)} %pad_clamp_fusion), kind=kCustom, calls=%fused_computation.1 | custom fusion | bytes 4194432 | tf_op jit(solution)/shard_map/gather | solution.py:68
  59.4 2.6 %multiply_reduce_fusion = (f32[4,128]{1,0:T(4,128)S(1)}, f32[4,128,1024]{2,1,0:T(8,128)S(1)}) fusion(bf16[4,128,1024]{2,1,0:T(8,128)(2,1)S(1)} %bitcast.65, f32[4,128]{1,0:T(4,128)S(1)} %convert_bitcast_fusion, bf16[4,256,1024]{2,1,0:T(8,128)(2,1)} %bitcast.69, s32[4,128,256]{2,1,0:T(8,128)} %select_reduce_fusion), kind=kOutput, calls=%fused_computation.20 | convolution fusion | flops 271187456 | bytes 5771264 | tf_op jit(solution)/shard_map/brc,bch->brh/dot_general | solution.py:73
  62.5 1.4 fusion.1
  63.9 2.8 %fusion.4 = f32[4,256,1024]{2,1,0:T(8,128)} fusion(f32[4,128,1024]{2,1,0:T(8,128)S(1)} %get-tuple-element.5, f32[4,128]{1,0:T(4,128)S(1)} %convert_bitcast_fusion, s32[4,128,256]{2,1,0:T(8,128)S(1)} %copy-done.8), kind=kOutput, calls=%fused_computation.24 | convolution fusion | flops 269615104 | bytes 6817792 | tf_op jit(solution)/shard_map/brc,brh->bch/dot_general | solution.py:83
  66.7 2.5 %broadcast_in_dim.61 = f32[32,32,1024]{2,1,0:T(8,128)} broadcast(f32[]{:T(128)} %constant.74.clone.1), dimensions={} | broadcast | bytes 4194308 | tf_op jit(solution)/shard_map/broadcast_in_dim | solution.py:86
  69.1 10.1 %scatter_fusion = f32[32,32,1024]{2,1,0:T(8,128)} fusion(f32[32,32,1024]{2,1,0:T(8,128)} %broadcast_in_dim.61, s32[32]{0:T(128)S(1)} %reshape.162, f32[32,32,1024]{2,1,0:T(8,128)} %bitcast.62), kind=kCustom, calls=%fused_computation.2 | custom fusion | flops 1048576 | bytes 12583040 | tf_op jit(solution)/shard_map/scatter-add | solution.py:86
  79.2 2.7 %slice.16 = bf16[16,32,1024]{2,1,0:T(8,128)(2,1)} slice(f32[32,32,1024]{2,1,0:T(8,128)} %scatter_fusion), slice={[0:16], [0:32], [0:1024]} | slice | bytes 2097152 | tf_op jit(solution)/shard_map/slice | solution.py:87
  81.9 4.8 %all-to-all-start.2 = ((bf16[16,32,1024]{2,1,0:T(8,128)(2,1)}), bf16[16,32,1024]{2,1,0:T(8,128)(2,1)S(1)}, u32[]{:S(2)}, u32[]{:S(2)}) async-start(bf16[16,32,1024]{2,1,0:T(8,128)(2,1)} %slice.16), calls=%async_computation.2 | async-start | bytes 2097152 | tf_op jit(solution)/shard_map/all_to_all | solution.py:88
  87.1 3.2 %slice.13 = f32[16,32,1024]{2,1,0:T(8,128)} slice(f32[32,32,1024]{2,1,0:T(8,128)} %scatter_fusion), slice={[16:32], [0:32], [0:1024]} | slice | bytes 4194304 | tf_op jit(solution)/shard_map/slice | solution.py:90
  90.3 22.9 %all-to-all-done.2 = bf16[16,32,1024]{2,1,0:T(8,128)(2,1)S(1)} async-done(((bf16[16,32,1024]{2,1,0:T(8,128)(2,1)}), bf16[16,32,1024]{2,1,0:T(8,128)(2,1)S(1)}, u32[]{:S(2)}, u32[]{:S(2)}) %all-to-all-start.2) | async-done | bytes 1048608 | tf_op jit(solution)/shard_map/all_to_all | solution.py:88
  113.2 1.7 convert_select_fusion
  114.9 5.1 %scatter_fusion.1 = f32[16,32,1024]{2,1,0:T(8,128)} fusion(f32[16,32,1024]{2,1,0:T(8,128)} %slice.13, s32[16]{0:T(128)S(1)} %fusion.14, f32[16,32,1024]{2,1,0:T(8,128)} %convert_select_fusion), kind=kCustom, calls=%fused_computation.3 | custom fusion | flops 524288 | bytes 6291520 | tf_op jit(solution)/shard_map/scatter-add | solution.py:90
  120.0 3.7 %fusion.3 = bf16[512,1024]{1,0:T(8,128)(2,1)S(1)} fusion(f32[16,32,1024]{2,1,0:T(8,128)} %scatter_fusion.1, f32[4,128,1024]{2,1,0:T(8,128)} %copy-done.2, f32[512,1024]{1,0:T(8,128)} %get-tuple-element.9, f32[1024]{0:T(1024)S(1)} %copy-done.11), kind=kLoop, calls=%fused_computation.17 | loop fusion | flops 2621440 | bytes 7344128 | tf_op jit(solution)/shard_map/convert_element_type | solution.py:94
  123.8 1.3 fusion.16
  125.1 1.9 copy-done.1
  127.0 1.1 fusion.5
  128.2 3.8 %collective-permute-start = (bf16[8,64,1024]{2,1,0:T(8,128)(2,1)}, bf16[8,64,1024]{2,1,0:T(8,128)(2,1)}, u32[]{:S(2)}, u32[]{:S(2)}) collective-permute-start(bf16[8,64,1024]{2,1,0:T(8,128)(2,1)} %fusion.5), channel_id=1, source_target_pairs={{0,1},{1,0},{2,3},{3,2},{4,5},{5,4},{6,7},{7,6},{8,9},{9,8},{10,11... | collective-permute-start | bytes 3145736 | tf_op jit(solution)/shard_map/ppermute | solution.py:32
  132.0 2.6 %collective-permute-done = bf16[8,64,1024]{2,1,0:T(8,128)(2,1)} collective-permute-done((bf16[8,64,1024]{2,1,0:T(8,128)(2,1)}, bf16[8,64,1024]{2,1,0:T(8,128)(2,1)}, u32[]{:S(2)}, u32[]{:S(2)}) %collective-permute-start) | collective-permute-done | bytes 1048608 | tf_op jit(solution)/shard_map/ppermute | solution.py:32
  134.6 2.2 bitcast_add_fusion
  136.8 1.3 copy-done.3
  139.0 1.9 collective-permute-start.1
  140.9 14.5 %collective-permute-done.1 = bf16[4,64,1024]{2,1,0:T(8,128)(2,1)} collective-permute-done((bf16[4,64,1024]{2,1,0:T(8,128)(2,1)}, bf16[4,64,1024]{2,1,0:T(8,128)(2,1)}, u32[]{:S(2)}, u32[]{:S(2)}) %collective-permute-start.1) | collective-permute-done | bytes 524320 | tf_op jit(solution)/shard_map/ppermute | solution.py:32
  155.4 1.5 bitcast_add_fusion.2
  156.9 1.0 copy-done.5
  158.6 2.5 %collective-permute-start.2 = (bf16[2,64,1024]{2,1,0:T(8,128)(2,1)}, bf16[2,64,1024]{2,1,0:T(8,128)(2,1)S(1)}, u32[]{:S(2)}, u32[]{:S(2)}) collective-permute-start(bf16[2,64,1024]{2,1,0:T(8,128)(2,1)} %fusion.8), channel_id=1, source_target_pairs={{0,4},{1,5},{2,6},{3,7},{4,0},{5,1},{6,2},{7,3},{8,12},{9,13},{10,... | collective-permute-start | bytes 786440 | tf_op jit(solution)/shard_map/ppermute | solution.py:32
  161.1 13.9 %collective-permute-done.2 = bf16[2,64,1024]{2,1,0:T(8,128)(2,1)S(1)} collective-permute-done((bf16[2,64,1024]{2,1,0:T(8,128)(2,1)}, bf16[2,64,1024]{2,1,0:T(8,128)(2,1)S(1)}, u32[]{:S(2)}, u32[]{:S(2)}) %collective-permute-start.2) | collective-permute-done | bytes 262176 | tf_op jit(solution)/shard_map/ppermute | solution.py:32
  175.0 1.1 bitcast_add_fusion.3
  176.9 3.5 %collective-permute-start.3 = (bf16[1,64,1024]{2,1,0:T(8,128)(2,1)S(1)}, bf16[1,64,1024]{2,1,0:T(8,128)(2,1)S(1)}, u32[]{:S(2)}, u32[]{:S(2)}) collective-permute-start(bf16[1,64,1024]{2,1,0:T(8,128)(2,1)S(1)} %dynamic-slice_convert_fusion.2), channel_id=1, source_target_pairs={{0,8},{1,9},{2,10},{3,11},{4,12},{5,13},{6,14},{7,15},{8,0},{9,1},... | collective-permute-start | bytes 393224 | tf_op jit(solution)/shard_map/ppermute | solution.py:32
  180.4 8.4 %collective-permute-done.3 = bf16[1,64,1024]{2,1,0:T(8,128)(2,1)S(1)} collective-permute-done((bf16[1,64,1024]{2,1,0:T(8,128)(2,1)S(1)}, bf16[1,64,1024]{2,1,0:T(8,128)(2,1)S(1)}, u32[]{:S(2)}, u32[]{:S(2)}) %collective-permute-start.3) | collective-permute-done | bytes 131104 | tf_op jit(solution)/shard_map/ppermute | solution.py:32
  188.8 1.0 fusion.9
  189.7 2.6 %collective-permute-start.4 = (bf16[64,1024]{1,0:T(8,128)(2,1)S(1)}, bf16[64,1024]{1,0:T(8,128)(2,1)S(1)}, u32[]{:S(2)}, u32[]{:S(2)}) collective-permute-start(bf16[64,1024]{1,0:T(8,128)(2,1)S(1)} %fusion.9), channel_id=1, source_target_pairs={{0,16},{16,0},{32,48},{48,32},{64,80},{80,64},{96,112},{112,96},{1... | collective-permute-start | bytes 393224 | tf_op jit(solution)/shard_map/ppermute | solution.py:37
  192.4 4.2 %collective-permute-done.4 = bf16[64,1024]{1,0:T(8,128)(2,1)S(1)} collective-permute-done((bf16[64,1024]{1,0:T(8,128)(2,1)S(1)}, bf16[64,1024]{1,0:T(8,128)(2,1)S(1)}, u32[]{:S(2)}, u32[]{:S(2)}) %collective-permute-start.4) | collective-permute-done | bytes 131104 | tf_op jit(solution)/shard_map/ppermute | solution.py:37
  196.6 3.4 %collective-permute-start.5 = (bf16[64,1024]{1,0:T(8,128)(2,1)S(1)}, bf16[64,1024]{1,0:T(8,128)(2,1)S(1)}, u32[]{:S(2)}, u32[]{:S(2)}) collective-permute-start(bf16[64,1024]{1,0:T(8,128)(2,1)S(1)} %add_convert_fusion.3), channel_id=1, source_target_pairs={{0,32},{16,48},{32,0},{48,16},{64,96},{80,112},{96,64},{112,80},{1... | collective-permute-start | bytes 393224 | tf_op jit(solution)/shard_map/ppermute | solution.py:37
  200.0 5.0 %collective-permute-done.5 = bf16[64,1024]{1,0:T(8,128)(2,1)S(1)} collective-permute-done((bf16[64,1024]{1,0:T(8,128)(2,1)S(1)}, bf16[64,1024]{1,0:T(8,128)(2,1)S(1)}, u32[]{:S(2)}, u32[]{:S(2)}) %collective-permute-start.5) | collective-permute-done | bytes 131104 | tf_op jit(solution)/shard_map/ppermute | solution.py:37
  205.0 3.5 %collective-permute-start.6 = (bf16[64,1024]{1,0:T(8,128)(2,1)S(1)}, bf16[64,1024]{1,0:T(8,128)(2,1)S(1)}, u32[]{:S(2)}, u32[]{:S(2)}) collective-permute-start(bf16[64,1024]{1,0:T(8,128)(2,1)S(1)} %add_convert_fusion.2), channel_id=1, source_target_pairs={{0,64},{16,80},{32,96},{48,112},{64,0},{80,16},{96,32},{112,48},{1... | collective-permute-start | bytes 393224 | tf_op jit(solution)/shard_map/ppermute | solution.py:37
  208.5 3.4 %collective-permute-done.6 = bf16[64,1024]{1,0:T(8,128)(2,1)S(1)} collective-permute-done((bf16[64,1024]{1,0:T(8,128)(2,1)S(1)}, bf16[64,1024]{1,0:T(8,128)(2,1)S(1)}, u32[]{:S(2)}, u32[]{:S(2)}) %collective-permute-start.6) | collective-permute-done | bytes 131104 | tf_op jit(solution)/shard_map/ppermute | solution.py:37
  211.9 4.4 %collective-permute-start.7 = (bf16[64,1024]{1,0:T(8,128)(2,1)S(1)}, bf16[64,1024]{1,0:T(8,128)(2,1)S(1)}, u32[]{:S(2)}, u32[]{:S(2)}) collective-permute-start(bf16[64,1024]{1,0:T(8,128)(2,1)S(1)} %add_convert_fusion.1), channel_id=1, source_target_pairs={{0,128},{16,144},{32,160},{48,176},{64,192},{80,208},{96,224},{112... | collective-permute-start | bytes 393224 | tf_op jit(solution)/shard_map/ppermute | solution.py:37
  216.4 4.7 %collective-permute-done.7 = bf16[64,1024]{1,0:T(8,128)(2,1)S(1)} collective-permute-done((bf16[64,1024]{1,0:T(8,128)(2,1)S(1)}, bf16[64,1024]{1,0:T(8,128)(2,1)S(1)}, u32[]{:S(2)}, u32[]{:S(2)}) %collective-permute-start.7) | collective-permute-done | bytes 131104 | tf_op jit(solution)/shard_map/ppermute | solution.py:37
  221.1 7.9 %collective-permute-start.8 = (bf16[64,1024]{1,0:T(8,128)(2,1)S(1)}, bf16[64,1024]{1,0:T(8,128)(2,1)S(1)}, u32[]{:S(2)}, u32[]{:S(2)}) collective-permute-start(bf16[64,1024]{1,0:T(8,128)(2,1)S(1)} %add_convert_fusion), channel_id=1, source_target_pairs={{0,256},{16,272},{32,288},{48,304},{64,320},{80,336},{96,352},{112... | collective-permute-start | bytes 393224 | tf_op jit(solution)/shard_map/ppermute | solution.py:37
  229.1 2.3 convolution_convert_fusion
  (49 shorter events, 8.1 us)
Async XLA Ops:
  0.6 12.1 %copy-start = (bf16[1024,1024]{1,0:T(8,128)(2,1)S(1)}, bf16[1024,1024]{1,0:T(8,128)(2,1)}, u32[]{:S(2)}) copy-start(bf16[1024,1024]{1,0:T(8,128)(2,1)} %param.8) | copy-start | bytes 6291460
  2.3 18.0 %all-to-all-start = ((s32[16,1,1]{2,1,0:T(1,128)}), s32[16,1,1]{2,1,0:T(1,128)S(1)}, u32[]{:S(2)}, u32[]{:S(2)}) async-start(s32[16,1,1]{2,1,0:T(1,128)} %copy.32), calls=%async_computation | async-start | bytes 16384 | tf_op jit(solution)/shard_map/all_to_all | solution.py:61
  20.6 6.1 %copy-start.9 = (s32[512,16]{0,1:T(8,128)S(1)}, s32[512,16]{0,1:T(8,128)}, u32[]{:S(2)}) copy-start(s32[512,16]{0,1:T(8,128)} %param.12) | copy-start | bytes 98308
  20.7 6.3 %copy-start.10 = (s32[512,16]{0,1:T(8,128)S(1)}, s32[512,16]{0,1:T(8,128)}, u32[]{:S(2)}) copy-start(s32[512,16]{0,1:T(8,128)} %param.11) | copy-start | bytes 98308
  22.2 30.9 %all-to-all-start.1 = ((bf16[16,32,1024]{2,1,0:T(8,128)(2,1)}), bf16[16,32,1024]{2,1,0:T(8,128)(2,1)}, u32[]{:S(2)}, u32[]{:S(2)}) async-start(bf16[16,32,1024]{2,1,0:T(8,128)(2,1)} %gather_fusion), calls=%async_computation.1 | async-start | bytes 2097152 | tf_op jit(solution)/shard_map/all_to_all | solution.py:65
  59.4 2.6 %copy-start.4 = (bf16[512,1024]{1,0:T(8,128)(2,1)S(1)}, bf16[512,1024]{1,0:T(8,128)(2,1)}, u32[]{:S(2)}) copy-start(bf16[512,1024]{1,0:T(8,128)(2,1)} %param.13) | copy-start | bytes 3145732
  62.5 1.4 copy-start.8
  63.9 2.8 %copy-start.2 = (f32[4,128,1024]{2,1,0:T(8,128)}, f32[4,128,1024]{2,1,0:T(8,128)S(1)}, u32[]{:S(2)}) copy-start(f32[4,128,1024]{2,1,0:T(8,128)S(1)} %get-tuple-element.5) | copy-start | bytes 6291460
  81.9 31.3 %all-to-all-start.2 = ((bf16[16,32,1024]{2,1,0:T(8,128)(2,1)}), bf16[16,32,1024]{2,1,0:T(8,128)(2,1)S(1)}, u32[]{:S(2)}, u32[]{:S(2)}) async-start(bf16[16,32,1024]{2,1,0:T(8,128)(2,1)} %slice.16), calls=%async_computation.2 | async-start | bytes 2097152 | tf_op jit(solution)/shard_map/all_to_all | solution.py:88
  114.9 5.1 %copy-start.11 = (f32[1024]{0:T(1024)S(1)}, f32[1024]{0:T(1024)}, u32[]{:S(2)}) copy-start(f32[1024]{0:T(1024)} %param.9) | copy-start | bytes 12292
  120.0 3.7 %copy-start.7 = (bf16[512,1024]{1,0:T(8,128)(2,1)S(1)}, bf16[512,1024]{1,0:T(8,128)(2,1)}, u32[]{:S(2)}) copy-start(bf16[512,1024]{1,0:T(8,128)(2,1)} %param.7) | copy-start | bytes 3145732
  125.1 1.9 copy-start.1
  128.2 6.4 %collective-permute-start = (bf16[8,64,1024]{2,1,0:T(8,128)(2,1)}, bf16[8,64,1024]{2,1,0:T(8,128)(2,1)}, u32[]{:S(2)}, u32[]{:S(2)}) collective-permute-start(bf16[8,64,1024]{2,1,0:T(8,128)(2,1)} %fusion.5), channel_id=1, source_target_pairs={{0,1},{1,0},{2,3},{3,2},{4,5},{5,4},{6,7},{7,6},{8,9},{9,8},{10,11... | collective-permute-start | bytes 3145736 | tf_op jit(solution)/shard_map/ppermute | solution.py:32
  136.8 1.3 copy-start.3
  139.0 16.4 %collective-permute-start.1 = (bf16[4,64,1024]{2,1,0:T(8,128)(2,1)}, bf16[4,64,1024]{2,1,0:T(8,128)(2,1)}, u32[]{:S(2)}, u32[]{:S(2)}) collective-permute-start(bf16[4,64,1024]{2,1,0:T(8,128)(2,1)} %fusion.7), channel_id=1, source_target_pairs={{0,2},{1,3},{2,0},{3,1},{4,6},{5,7},{6,4},{7,5},{8,10},{9,11},{10,... | collective-permute-start | bytes 1572872 | tf_op jit(solution)/shard_map/ppermute | solution.py:32
  156.9 1.0 copy-start.5
  158.6 16.3 %collective-permute-start.2 = (bf16[2,64,1024]{2,1,0:T(8,128)(2,1)}, bf16[2,64,1024]{2,1,0:T(8,128)(2,1)S(1)}, u32[]{:S(2)}, u32[]{:S(2)}) collective-permute-start(bf16[2,64,1024]{2,1,0:T(8,128)(2,1)} %fusion.8), channel_id=1, source_target_pairs={{0,4},{1,5},{2,6},{3,7},{4,0},{5,1},{6,2},{7,3},{8,12},{9,13},{10,... | collective-permute-start | bytes 786440 | tf_op jit(solution)/shard_map/ppermute | solution.py:32
  176.1 0.8 copy-start.6
  176.9 11.9 %collective-permute-start.3 = (bf16[1,64,1024]{2,1,0:T(8,128)(2,1)S(1)}, bf16[1,64,1024]{2,1,0:T(8,128)(2,1)S(1)}, u32[]{:S(2)}, u32[]{:S(2)}) collective-permute-start(bf16[1,64,1024]{2,1,0:T(8,128)(2,1)S(1)} %dynamic-slice_convert_fusion.2), channel_id=1, source_target_pairs={{0,8},{1,9},{2,10},{3,11},{4,12},{5,13},{6,14},{7,15},{8,0},{9,1},... | collective-permute-start | bytes 393224 | tf_op jit(solution)/shard_map/ppermute | solution.py:32
  189.7 6.9 %collective-permute-start.4 = (bf16[64,1024]{1,0:T(8,128)(2,1)S(1)}, bf16[64,1024]{1,0:T(8,128)(2,1)S(1)}, u32[]{:S(2)}, u32[]{:S(2)}) collective-permute-start(bf16[64,1024]{1,0:T(8,128)(2,1)S(1)} %fusion.9), channel_id=1, source_target_pairs={{0,16},{16,0},{32,48},{48,32},{64,80},{80,64},{96,112},{112,96},{1... | collective-permute-start | bytes 393224 | tf_op jit(solution)/shard_map/ppermute | solution.py:37
  196.6 8.4 %collective-permute-start.5 = (bf16[64,1024]{1,0:T(8,128)(2,1)S(1)}, bf16[64,1024]{1,0:T(8,128)(2,1)S(1)}, u32[]{:S(2)}, u32[]{:S(2)}) collective-permute-start(bf16[64,1024]{1,0:T(8,128)(2,1)S(1)} %add_convert_fusion.3), channel_id=1, source_target_pairs={{0,32},{16,48},{32,0},{48,16},{64,96},{80,112},{96,64},{112,80},{1... | collective-permute-start | bytes 393224 | tf_op jit(solution)/shard_map/ppermute | solution.py:37
  205.0 6.9 %collective-permute-start.6 = (bf16[64,1024]{1,0:T(8,128)(2,1)S(1)}, bf16[64,1024]{1,0:T(8,128)(2,1)S(1)}, u32[]{:S(2)}, u32[]{:S(2)}) collective-permute-start(bf16[64,1024]{1,0:T(8,128)(2,1)S(1)} %add_convert_fusion.2), channel_id=1, source_target_pairs={{0,64},{16,80},{32,96},{48,112},{64,0},{80,16},{96,32},{112,48},{1... | collective-permute-start | bytes 393224 | tf_op jit(solution)/shard_map/ppermute | solution.py:37
  211.9 9.2 %collective-permute-start.7 = (bf16[64,1024]{1,0:T(8,128)(2,1)S(1)}, bf16[64,1024]{1,0:T(8,128)(2,1)S(1)}, u32[]{:S(2)}, u32[]{:S(2)}) collective-permute-start(bf16[64,1024]{1,0:T(8,128)(2,1)S(1)} %add_convert_fusion.1), channel_id=1, source_target_pairs={{0,128},{16,144},{32,160},{48,176},{64,192},{80,208},{96,224},{112... | collective-permute-start | bytes 393224 | tf_op jit(solution)/shard_map/ppermute | solution.py:37
  221.1 10.9 %collective-permute-start.8 = (bf16[64,1024]{1,0:T(8,128)(2,1)S(1)}, bf16[64,1024]{1,0:T(8,128)(2,1)S(1)}, u32[]{:S(2)}, u32[]{:S(2)}) collective-permute-start(bf16[64,1024]{1,0:T(8,128)(2,1)S(1)} %add_convert_fusion), channel_id=1, source_target_pairs={{0,256},{16,272},{32,288},{48,304},{64,320},{80,336},{96,352},{112... | collective-permute-start | bytes 393224 | tf_op jit(solution)/shard_map/ppermute | solution.py:37

commit v3 on v1

--- a/solution.py
+++ b/solution.py
@@ -18,18 +18,40 @@
     return [(i, i ^ (1 << bit)) for i in range(n)]
 
 
+def shifted_pairs(members, bit):
+    chips = members // 2
+    pairs = []
+    for m in range(members):
+        chip, core = divmod(m, 2)
+        label = ((chip - core) % chips) ^ (1 << bit)
+        pairs.append((m, 2 * ((label + core) % chips) + core))
+    return pairs
+
+
+def halve(acc, bit):
+    pairs = acc.reshape(acc.shape[0] // 2, 2, *acc.shape[1:])
+    keep = lax.dynamic_index_in_dim(pairs, bit, 1, keepdims=False)
+    send = lax.dynamic_index_in_dim(pairs, 1 - bit, 1, keepdims=False)
+    return keep, send
+
+
 def reduce_rows(part):
     members = lax.axis_size("member")
     groups = lax.axis_size("group")
     member_here = lax.axis_index("member")
+    chips = members // 2
+    chip, core = member_here // 2, member_here % 2
     rows, cols = part.shape
     acc = part.reshape(members, rows // members, cols)
-    for k in range(members.bit_length() - 1):
-        pairs = acc.reshape(acc.shape[0] // 2, 2, *acc.shape[1:])
-        bit = (member_here >> k) & 1
-        keep = lax.dynamic_index_in_dim(pairs, bit, 1, keepdims=False)
-        send = lax.dynamic_index_in_dim(pairs, 1 - bit, 1, keepdims=False)
-        acc = keep + lax.ppermute(send, "member", xor_pairs(members, k))
+    keep, send = halve(acc, core)
+    sent = lax.ppermute(send.astype(jnp.bfloat16), "member", xor_pairs(members, 0))
+    acc = keep + sent.astype(jnp.float32)
+    acc = lax.dynamic_slice_in_dim(jnp.concatenate([acc, acc], axis=0), core, chips, 0)
+    label = (chip - core) % chips
+    for k in range(chips.bit_length() - 1):
+        keep, send = halve(acc, (label >> k) & 1)
+        sent = lax.ppermute(send.astype(jnp.bfloat16), "member", shifted_pairs(members, k))
+        acc = keep + sent.astype(jnp.float32)
     acc = acc.reshape(rows // members, cols)
     for k in range(groups.bit_length() - 1):
         acc = acc + lax.ppermute(acc, "group", xor_pairs(groups, k))

time: 282 us -> 246 us (0.87)
  waiting for transfers between devices: 151 us -> 116 us
    ppermute x4, waiting for transfers between devices: 68.8 us -> 32.2 us  [the longest x3 29.8 us: reduce_rows(): lax.ppermute(send.astype(jnp.bfloat16), 'member', shifted_pairs(members, k))]
    squeeze x4 -> x0, local copies, waits for them, and re-layouts: 3.48 us -> none  [reduce_rows(): send = lax.dynamic_index_in_dim(pairs, 1 - bit, 1, keepdims=False)]
  transfers between devices with their start and end apart: 12 -> 12, of which waited for: 12 -> 12; matrix products, arithmetic and copies ran while one was open for 6% -> 7% of each run, Pallas kernels for 0% -> 0%
where the time goes in v3:
time: 246 us; the launch traced here: 244 us
  waiting for transfers between devices  116 us (47%)
  starting transfers between devices  51.2 us (21%)
  other arithmetic  39.9 us (16%)
  local copies, waits for them, and re-layouts  23.1 us (9%)
  matrix products  12.7 us (5%)
    ppermute x5, waiting for transfers between devices, reduce_rows(): acc = acc + lax.ppermute(acc, 'group', xor_pairs(groups, k))  37.4 us
    ppermute x3, waiting for transfers between devices, reduce_rows(): lax.ppermute(send.astype(jnp.bfloat16), 'member', shifted_pairs(members, k))  29.8 us
    all_to_all x1, waiting for transfers between devices, on_device(): lax.all_to_all(returned, 'member', split_axis=0, concat_axis=0, tiled=True)  22.9 us
    ppermute x5, starting transfers between devices, reduce_rows(): acc = acc + lax.ppermute(acc, 'group', xor_pairs(groups, k))  21.3 us
    all_to_all x1, waiting for transfers between devices, on_device(): lax.all_to_all(own_tiles[served], 'member', split_axis=0, concat_axis=0,...  19.4 us
    all_to_all x1, starting transfers between devices, on_device(): lax.all_to_all(wanted.reshape(members, 1), 'member', split_axis=0, concat...  10.4 us
    scatter-add x1, other arithmetic, on_device(): jax.ops.segment_sum(cand_grad, pool_index, num_segments=pool_size)  10 us
    ppermute x3, starting transfers between devices, reduce_rows(): lax.ppermute(send.astype(jnp.bfloat16), 'member', shifted_pairs(members, k))  6.09 us
  transfers between devices with their start and end apart: 12, of which 12 were waited for; matrix products, arithmetic and copies ran while one was open for 7% of the time, Pallas kernels for 0%

profile of v3, /device:TPU:6, one launch (start us, length us, event | category | flops | bytes accessed | tf_op | source)
XLA Modules:
  0.0 243.5 jit_solution(2522674981170505433)
XLA Ops:
  2.3 10.4 %all-to-all-start = ((s32[16,1,1]{2,1,0:T(1,128)}), s32[16,1,1]{2,1,0:T(1,128)S(1)}, u32[]{:S(2)}, u32[]{:S(2)}) async-start(s32[16,1,1]{2,1,0:T(1,128)} %copy.32), calls=%async_computation | async-start | bytes 16384 | tf_op jit(solution)/shard_map/all_to_all | solution.py:80
  12.7 3.8 %maximum_convert_fusion = (bf16[512,1024]{1,0:T(8,128)(2,1)S(1)}, f32[512,1024]{1,0:T(8,128)}) fusion(f32[1024]{0:T(1024)} %param.9, bf16[512,1024]{1,0:T(8,128)(2,1)} %param.7, bf16[1024,1024]{1,0:T(8,128)(2,1)S(1)} %copy-done), kind=kOutput, calls=%fused_computation.24 | convolution fusion | flops 1075314688 | bytes 6295552 | tf_op jit(solution)/shard_map/dot_general | solution.py:71
  16.6 3.7 %all-to-all-done = s32[16,1,1]{2,1,0:T(1,128)S(1)} async-done(((s32[16,1,1]{2,1,0:T(1,128)}), s32[16,1,1]{2,1,0:T(1,128)S(1)}, u32[]{:S(2)}, u32[]{:S(2)}) %all-to-all-start) | async-done | bytes 96 | tf_op jit(solution)/shard_map/all_to_all | solution.py:80
  20.7 1.6 gather_fusion
  22.2 4.3 %all-to-all-start.1 = ((bf16[16,32,1024]{2,1,0:T(8,128)(2,1)}), bf16[16,32,1024]{2,1,0:T(8,128)(2,1)}, u32[]{:S(2)}, u32[]{:S(2)}) async-start(bf16[16,32,1024]{2,1,0:T(8,128)(2,1)} %gather_fusion), calls=%async_computation.1 | async-start | bytes 2097152 | tf_op jit(solution)/shard_map/all_to_all | solution.py:84
  27.8 5.9 %select_reduce_fusion = s32[4,128,256]{2,1,0:T(8,128)} fusion(s32[4,128,16]{2,1,0:T(8,128)S(1)} %bitcast.70, s32[4,128,16]{2,1,0:T(8,128)} %bitcast.71), kind=kLoop, calls=%fused_computation.4 | loop fusion | flops 6160384 | bytes 589824 | tf_op jit(solution)/shard_map/reduce_sum | solution.py:14
  33.7 19.4 %all-to-all-done.1 = bf16[16,32,1024]{2,1,0:T(8,128)(2,1)} async-done(((bf16[16,32,1024]{2,1,0:T(8,128)(2,1)}), bf16[16,32,1024]{2,1,0:T(8,128)(2,1)}, u32[]{:S(2)}, u32[]{:S(2)}) %all-to-all-start.1) | async-done | bytes 1048608 | tf_op jit(solution)/shard_map/all_to_all | solution.py:84
  53.1 2.7 %pad_maximum_fusion = bf16[32,32,1024]{2,1,0:T(8,128)(2,1)} fusion(bf16[16,32,1024]{2,1,0:T(8,128)(2,1)S(1)} %bitcast.64, bf16[16,32,1024]{2,1,0:T(8,128)(2,1)} %all-to-all-done.1), kind=kLoop, calls=%fused_computation.14 | loop fusion | flops 1048576 | bytes 4194304 | tf_op jit(solution)/shard_map/concatenate | solution.py:85
  55.9 3.6 %gather_fusion.1 = bf16[32,32,1024]{2,1,0:T(8,128)(2,1)} fusion(bf16[32,32,1024]{2,1,0:T(8,128)(2,1)} %pad_maximum_fusion, s32[1024]{0:T(1024)S(1)} %pad_clamp_fusion), kind=kCustom, calls=%fused_computation.1 | custom fusion | bytes 4194432 | tf_op jit(solution)/shard_map/gather | solution.py:87
  59.4 2.6 %multiply_reduce_fusion = (f32[4,128]{1,0:T(4,128)S(1)}, f32[4,128,1024]{2,1,0:T(8,128)S(1)}) fusion(bf16[4,128,1024]{2,1,0:T(8,128)(2,1)S(1)} %bitcast.65, f32[4,128]{1,0:T(4,128)S(1)} %convert_bitcast_fusion, bf16[4,256,1024]{2,1,0:T(8,128)(2,1)} %bitcast.69, s32[4,128,256]{2,1,0:T(8,128)} %select_reduce_fusion), kind=kOutput, calls=%fused_computation.23 | convolution fusion | flops 271187456 | bytes 5771264 | tf_op jit(solution)/shard_map/brc,bch->brh/dot_general | solution.py:92
  62.5 1.4 fusion.1
  63.9 2.8 %fusion.5 = f32[4,256,1024]{2,1,0:T(8,128)} fusion(f32[4,128,1024]{2,1,0:T(8,128)S(1)} %get-tuple-element.5, f32[4,128]{1,0:T(4,128)S(1)} %convert_bitcast_fusion, s32[4,128,256]{2,1,0:T(8,128)S(1)} %copy-done.8), kind=kOutput, calls=%fused_computation.27 | convolution fusion | flops 269615104 | bytes 6817792 | tf_op jit(solution)/shard_map/brc,brh->bch/dot_general | solution.py:102
  66.7 2.5 %broadcast_in_dim.61 = f32[32,32,1024]{2,1,0:T(8,128)} broadcast(f32[]{:T(128)} %constant.100.clone.1), dimensions={} | broadcast | bytes 4194308 | tf_op jit(solution)/shard_map/broadcast_in_dim | solution.py:105
  69.1 10.0 %scatter_fusion = f32[32,32,1024]{2,1,0:T(8,128)} fusion(f32[32,32,1024]{2,1,0:T(8,128)} %broadcast_in_dim.61, s32[32]{0:T(128)S(1)} %reshape.164, f32[32,32,1024]{2,1,0:T(8,128)} %bitcast.62), kind=kCustom, calls=%fused_computation.2 | custom fusion | flops 1048576 | bytes 12583040 | tf_op jit(solution)/shard_map/scatter-add | solution.py:105
  79.2 2.7 %slice.16 = bf16[16,32,1024]{2,1,0:T(8,128)(2,1)} slice(f32[32,32,1024]{2,1,0:T(8,128)} %scatter_fusion), slice={[0:16], [0:32], [0:1024]} | slice | bytes 2097152 | tf_op jit(solution)/shard_map/slice | solution.py:106
  81.9 4.9 %all-to-all-start.2 = ((bf16[16,32,1024]{2,1,0:T(8,128)(2,1)}), bf16[16,32,1024]{2,1,0:T(8,128)(2,1)S(1)}, u32[]{:S(2)}, u32[]{:S(2)}) async-start(bf16[16,32,1024]{2,1,0:T(8,128)(2,1)} %slice.16), calls=%async_computation.2 | async-start | bytes 2097152 | tf_op jit(solution)/shard_map/all_to_all | solution.py:107
  87.2 3.2 %slice.13 = f32[16,32,1024]{2,1,0:T(8,128)} slice(f32[32,32,1024]{2,1,0:T(8,128)} %scatter_fusion), slice={[16:32], [0:32], [0:1024]} | slice | bytes 4194304 | tf_op jit(solution)/shard_map/slice | solution.py:109
  90.4 22.9 %all-to-all-done.2 = bf16[16,32,1024]{2,1,0:T(8,128)(2,1)S(1)} async-done(((bf16[16,32,1024]{2,1,0:T(8,128)(2,1)}), bf16[16,32,1024]{2,1,0:T(8,128)(2,1)S(1)}, u32[]{:S(2)}, u32[]{:S(2)}) %all-to-all-start.2) | async-done | bytes 1048608 | tf_op jit(solution)/shard_map/all_to_all | solution.py:107
  113.3 1.7 convert_select_fusion
  115.0 5.0 %scatter_fusion.1 = f32[16,32,1024]{2,1,0:T(8,128)} fusion(f32[16,32,1024]{2,1,0:T(8,128)} %slice.13, s32[16]{0:T(128)S(1)} %fusion.14, f32[16,32,1024]{2,1,0:T(8,128)} %convert_select_fusion), kind=kCustom, calls=%fused_computation.3 | custom fusion | flops 524288 | bytes 6291520 | tf_op jit(solution)/shard_map/scatter-add | solution.py:109
  120.0 3.7 %fusion.4 = bf16[512,1024]{1,0:T(8,128)(2,1)S(1)} fusion(f32[16,32,1024]{2,1,0:T(8,128)} %scatter_fusion.1, f32[4,128,1024]{2,1,0:T(8,128)} %copy-done.2, f32[512,1024]{1,0:T(8,128)} %get-tuple-element.9, f32[1024]{0:T(1024)S(1)} %copy-done.11), kind=kLoop, calls=%fused_computation.20 | loop fusion | flops 2621440 | bytes 7344128 | tf_op jit(solution)/shard_map/convert_element_type | solution.py:113
  123.7 1.3 fusion.16
  125.1 1.9 copy-done.1
  127.0 1.1 fusion.6
  128.1 4.2 %collective-permute-start = (bf16[8,64,1024]{2,1,0:T(8,128)(2,1)}, bf16[8,64,1024]{2,1,0:T(8,128)(2,1)}, u32[]{:S(2)}, u32[]{:S(2)}) collective-permute-start(bf16[8,64,1024]{2,1,0:T(8,128)(2,1)} %fusion.6), channel_id=1, source_target_pairs={{0,1},{1,0},{2,3},{3,2},{4,5},{5,4},{6,7},{7,6},{8,9},{9,8},{10,11... | collective-permute-start | bytes 3145736 | tf_op jit(solution)/shard_map/ppermute | solution.py:47
  132.3 2.4 collective-permute-done
  134.7 2.2 bitcast_add_fusion
  137.5 1.3 copy-done.3
  139.7 1.9 collective-permute-start.1
  141.6 9.5 %collective-permute-done.1 = bf16[4,64,1024]{2,1,0:T(8,128)(2,1)} collective-permute-done((bf16[4,64,1024]{2,1,0:T(8,128)(2,1)}, bf16[4,64,1024]{2,1,0:T(8,128)(2,1)}, u32[]{:S(2)}, u32[]{:S(2)}) %collective-permute-start.1) | collective-permute-done | bytes 524320 | tf_op jit(solution)/shard_map/ppermute | solution.py:53
  151.0 1.5 bitcast_add_fusion.2
  154.3 2.3 collective-permute-start.2
  156.5 11.5 %collective-permute-done.2 = bf16[2,64,1024]{2,1,0:T(8,128)(2,1)S(1)} collective-permute-done((bf16[2,64,1024]{2,1,0:T(8,128)(2,1)}, bf16[2,64,1024]{2,1,0:T(8,128)(2,1)S(1)}, u32[]{:S(2)}, u32[]{:S(2)}) %collective-permute-start.2) | collective-permute-done | bytes 262176 | tf_op jit(solution)/shard_map/ppermute | solution.py:53
  168.1 1.1 bitcast_add_fusion.3
  170.0 1.9 collective-permute-start.3
  171.9 8.8 %collective-permute-done.3 = bf16[1,64,1024]{2,1,0:T(8,128)(2,1)S(1)} collective-permute-done((bf16[1,64,1024]{2,1,0:T(8,128)(2,1)S(1)}, bf16[1,64,1024]{2,1,0:T(8,128)(2,1)S(1)}, u32[]{:S(2)}, u32[]{:S(2)}) %collective-permute-start.3) | collective-permute-done | bytes 131104 | tf_op jit(solution)/shard_map/ppermute | solution.py:53
  180.8 1.0 add_bitcast_fusion
  181.7 3.4 %collective-permute-start.4 = (f32[64,1024]{1,0:T(8,128)S(1)}, f32[64,1024]{1,0:T(8,128)S(1)}, u32[]{:S(2)}, u32[]{:S(2)}) collective-permute-start(f32[64,1024]{1,0:T(8,128)S(1)} %add_bitcast_fusion), channel_id=1, source_target_pairs={{0,16},{16,0},{32,48},{48,32},{64,80},{80,64},{96,112},{112,96},{1... | collective-permute-start | bytes 786440 | tf_op jit(solution)/shard_map/ppermute | solution.py:57
  185.1 6.0 %collective-permute-done.4 = f32[64,1024]{1,0:T(8,128)S(1)} collective-permute-done((f32[64,1024]{1,0:T(8,128)S(1)}, f32[64,1024]{1,0:T(8,128)S(1)}, u32[]{:S(2)}, u32[]{:S(2)}) %collective-permute-start.4) | collective-permute-done | bytes 262176 | tf_op jit(solution)/shard_map/ppermute | solution.py:57
  191.1 2.2 collective-permute-start.5
  193.3 7.8 %collective-permute-done.5 = f32[64,1024]{1,0:T(8,128)S(1)} collective-permute-done((f32[64,1024]{1,0:T(8,128)S(1)}, f32[64,1024]{1,0:T(8,128)S(1)}, u32[]{:S(2)}, u32[]{:S(2)}) %collective-permute-start.5) | collective-permute-done | bytes 262176 | tf_op jit(solution)/shard_map/ppermute | solution.py:57
  201.2 4.8 %collective-permute-start.6 = (f32[64,1024]{1,0:T(8,128)S(1)}, f32[64,1024]{1,0:T(8,128)S(1)}, u32[]{:S(2)}, u32[]{:S(2)}) collective-permute-start(f32[64,1024]{1,0:T(8,128)S(1)} %add.161), channel_id=1, source_target_pairs={{0,64},{16,80},{32,96},{48,112},{64,0},{80,16},{96,32},{112,48},{1... | collective-permute-start | bytes 786440 | tf_op jit(solution)/shard_map/ppermute | solution.py:57
  206.0 4.3 %collective-permute-done.6 = f32[64,1024]{1,0:T(8,128)S(1)} collective-permute-done((f32[64,1024]{1,0:T(8,128)S(1)}, f32[64,1024]{1,0:T(8,128)S(1)}, u32[]{:S(2)}, u32[]{:S(2)}) %collective-permute-start.6) | collective-permute-done | bytes 262176 | tf_op jit(solution)/shard_map/ppermute | solution.py:57
  210.3 3.4 %collective-permute-start.7 = (f32[64,1024]{1,0:T(8,128)S(1)}, f32[64,1024]{1,0:T(8,128)S(1)}, u32[]{:S(2)}, u32[]{:S(2)}) collective-permute-start(f32[64,1024]{1,0:T(8,128)S(1)} %add.162), channel_id=1, source_target_pairs={{0,128},{16,144},{32,160},{48,176},{64,192},{80,208},{96,224},{112... | collective-permute-start | bytes 786440 | tf_op jit(solution)/shard_map/ppermute | solution.py:57
  213.7 10.2 %collective-permute-done.7 = f32[64,1024]{1,0:T(8,128)S(1)} collective-permute-done((f32[64,1024]{1,0:T(8,128)S(1)}, f32[64,1024]{1,0:T(8,128)S(1)}, u32[]{:S(2)}, u32[]{:S(2)}) %collective-permute-start.7) | collective-permute-done | bytes 262176 | tf_op jit(solution)/shard_map/ppermute | solution.py:57
  224.0 7.6 %collective-permute-start.8 = (f32[64,1024]{1,0:T(8,128)S(1)}, f32[64,1024]{1,0:T(8,128)S(1)}, u32[]{:S(2)}, u32[]{:S(2)}) collective-permute-start(f32[64,1024]{1,0:T(8,128)S(1)} %add.163), channel_id=1, source_target_pairs={{0,256},{16,272},{32,288},{48,304},{64,320},{80,336},{96,352},{112... | collective-permute-start | bytes 786440 | tf_op jit(solution)/shard_map/ppermute | solution.py:57
  231.5 2.3 convolution_convert_fusion
  233.8 9.0 %collective-permute-done.8 = f32[64,1024]{1,0:T(8,128)S(1)} collective-permute-done((f32[64,1024]{1,0:T(8,128)S(1)}, f32[64,1024]{1,0:T(8,128)S(1)}, u32[]{:S(2)}, u32[]{:S(2)}) %collective-permute-start.8) | collective-permute-done | bytes 262176 | tf_op jit(solution)/shard_map/ppermute | solution.py:57
  (50 shorter events, 8.8 us)
Async XLA Ops:
  0.6 12.1 %copy-start = (bf16[1024,1024]{1,0:T(8,128)(2,1)S(1)}, bf16[1024,1024]{1,0:T(8,128)(2,1)}, u32[]{:S(2)}) copy-start(bf16[1024,1024]{1,0:T(8,128)(2,1)} %param.8) | copy-start | bytes 6291460
  2.3 18.0 %all-to-all-start = ((s32[16,1,1]{2,1,0:T(1,128)}), s32[16,1,1]{2,1,0:T(1,128)S(1)}, u32[]{:S(2)}, u32[]{:S(2)}) async-start(s32[16,1,1]{2,1,0:T(1,128)} %copy.32), calls=%async_computation | async-start | bytes 16384 | tf_op jit(solution)/shard_map/all_to_all | solution.py:80
  20.6 6.1 %copy-start.9 = (s32[512,16]{0,1:T(8,128)S(1)}, s32[512,16]{0,1:T(8,128)}, u32[]{:S(2)}) copy-start(s32[512,16]{0,1:T(8,128)} %param.12) | copy-start | bytes 98308
  20.7 6.3 %copy-start.10 = (s32[512,16]{0,1:T(8,128)S(1)}, s32[512,16]{0,1:T(8,128)}, u32[]{:S(2)}) copy-start(s32[512,16]{0,1:T(8,128)} %param.11) | copy-start | bytes 98308
  22.2 30.9 %all-to-all-start.1 = ((bf16[16,32,1024]{2,1,0:T(8,128)(2,1)}), bf16[16,32,1024]{2,1,0:T(8,128)(2,1)}, u32[]{:S(2)}, u32[]{:S(2)}) async-start(bf16[16,32,1024]{2,1,0:T(8,128)(2,1)} %gather_fusion), calls=%async_computation.1 | async-start | bytes 2097152 | tf_op jit(solution)/shard_map/all_to_all | solution.py:84
  59.4 2.6 %copy-start.4 = (bf16[512,1024]{1,0:T(8,128)(2,1)S(1)}, bf16[512,1024]{1,0:T(8,128)(2,1)}, u32[]{:S(2)}) copy-start(bf16[512,1024]{1,0:T(8,128)(2,1)} %param.13) | copy-start | bytes 3145732
  62.5 1.4 copy-start.8
  63.9 2.8 %copy-start.2 = (f32[4,128,1024]{2,1,0:T(8,128)}, f32[4,128,1024]{2,1,0:T(8,128)S(1)}, u32[]{:S(2)}) copy-start(f32[4,128,1024]{2,1,0:T(8,128)S(1)} %get-tuple-element.5) | copy-start | bytes 6291460
  81.9 31.4 %all-to-all-start.2 = ((bf16[16,32,1024]{2,1,0:T(8,128)(2,1)}), bf16[16,32,1024]{2,1,0:T(8,128)(2,1)S(1)}, u32[]{:S(2)}, u32[]{:S(2)}) async-start(bf16[16,32,1024]{2,1,0:T(8,128)(2,1)} %slice.16), calls=%async_computation.2 | async-start | bytes 2097152 | tf_op jit(solution)/shard_map/all_to_all | solution.py:107
  115.0 5.0 %copy-start.11 = (f32[1024]{0:T(1024)S(1)}, f32[1024]{0:T(1024)}, u32[]{:S(2)}) copy-start(f32[1024]{0:T(1024)} %param.9) | copy-start | bytes 12292
  120.0 3.7 %copy-start.7 = (bf16[512,1024]{1,0:T(8,128)(2,1)S(1)}, bf16[512,1024]{1,0:T(8,128)(2,1)}, u32[]{:S(2)}) copy-start(bf16[512,1024]{1,0:T(8,128)(2,1)} %param.7) | copy-start | bytes 3145732
  125.0 1.9 copy-start.1
  128.1 6.6 %collective-permute-start = (bf16[8,64,1024]{2,1,0:T(8,128)(2,1)}, bf16[8,64,1024]{2,1,0:T(8,128)(2,1)}, u32[]{:S(2)}, u32[]{:S(2)}) collective-permute-start(bf16[8,64,1024]{2,1,0:T(8,128)(2,1)} %fusion.6), channel_id=1, source_target_pairs={{0,1},{1,0},{2,3},{3,2},{4,5},{5,4},{6,7},{7,6},{8,9},{9,8},{10,11... | collective-permute-start | bytes 3145736 | tf_op jit(solution)/shard_map/ppermute | solution.py:47
  137.5 1.3 copy-start.3
  139.7 11.4 %collective-permute-start.1 = (bf16[4,64,1024]{2,1,0:T(8,128)(2,1)}, bf16[4,64,1024]{2,1,0:T(8,128)(2,1)}, u32[]{:S(2)}, u32[]{:S(2)}) collective-permute-start(bf16[4,64,1024]{2,1,0:T(8,128)(2,1)} %fusion.8), channel_id=1, source_target_pairs={{0,2},{1,15},{2,0},{3,5},{4,6},{5,3},{6,4},{7,9},{8,10},{9,7},{10,... | collective-permute-start | bytes 1572872 | tf_op jit(solution)/shard_map/ppermute | solution.py:53
  152.6 1.0 copy-start.5
  154.3 13.8 %collective-permute-start.2 = (bf16[2,64,1024]{2,1,0:T(8,128)(2,1)}, bf16[2,64,1024]{2,1,0:T(8,128)(2,1)S(1)}, u32[]{:S(2)}, u32[]{:S(2)}) collective-permute-start(bf16[2,64,1024]{2,1,0:T(8,128)(2,1)} %fusion.9), channel_id=1, source_target_pairs={{0,4},{1,13},{2,6},{3,7},{4,0},{5,9},{6,2},{7,3},{8,12},{9,5},{10,... | collective-permute-start | bytes 786440 | tf_op jit(solution)/shard_map/ppermute | solution.py:53
  169.2 0.8 copy-start.6
  170.0 10.8 %collective-permute-start.3 = (bf16[1,64,1024]{2,1,0:T(8,128)(2,1)S(1)}, bf16[1,64,1024]{2,1,0:T(8,128)(2,1)S(1)}, u32[]{:S(2)}, u32[]{:S(2)}) collective-permute-start(bf16[1,64,1024]{2,1,0:T(8,128)(2,1)S(1)} %dynamic-slice_convert_fusion.2), channel_id=1, source_target_pairs={{0,8},{1,9},{2,10},{3,11},{4,12},{5,13},{6,14},{7,15},{8,0},{9,1},... | collective-permute-start | bytes 393224 | tf_op jit(solution)/shard_map/ppermute | solution.py:53
  181.7 9.4 %collective-permute-start.4 = (f32[64,1024]{1,0:T(8,128)S(1)}, f32[64,1024]{1,0:T(8,128)S(1)}, u32[]{:S(2)}, u32[]{:S(2)}) collective-permute-start(f32[64,1024]{1,0:T(8,128)S(1)} %add_bitcast_fusion), channel_id=1, source_target_pairs={{0,16},{16,0},{32,48},{48,32},{64,80},{80,64},{96,112},{112,96},{1... | collective-permute-start | bytes 786440 | tf_op jit(solution)/shard_map/ppermute | solution.py:57
  191.1 10.0 %collective-permute-start.5 = (f32[64,1024]{1,0:T(8,128)S(1)}, f32[64,1024]{1,0:T(8,128)S(1)}, u32[]{:S(2)}, u32[]{:S(2)}) collective-permute-start(f32[64,1024]{1,0:T(8,128)S(1)} %add.160), channel_id=1, source_target_pairs={{0,32},{16,48},{32,0},{48,16},{64,96},{80,112},{96,64},{112,80},{1... | collective-permute-start | bytes 786440 | tf_op jit(solution)/shard_map/ppermute | solution.py:57
  201.2 9.1 %collective-permute-start.6 = (f32[64,1024]{1,0:T(8,128)S(1)}, f32[64,1024]{1,0:T(8,128)S(1)}, u32[]{:S(2)}, u32[]{:S(2)}) collective-permute-start(f32[64,1024]{1,0:T(8,128)S(1)} %add.161), channel_id=1, source_target_pairs={{0,64},{16,80},{32,96},{48,112},{64,0},{80,16},{96,32},{112,48},{1... | collective-permute-start | bytes 786440 | tf_op jit(solution)/shard_map/ppermute | solution.py:57
  210.3 13.6 %collective-permute-start.7 = (f32[64,1024]{1,0:T(8,128)S(1)}, f32[64,1024]{1,0:T(8,128)S(1)}, u32[]{:S(2)}, u32[]{:S(2)}) collective-permute-start(f32[64,1024]{1,0:T(8,128)S(1)} %add.162), channel_id=1, source_target_pairs={{0,128},{16,144},{32,160},{48,176},{64,192},{80,208},{96,224},{112... | collective-permute-start | bytes 786440 | tf_op jit(solution)/shard_map/ppermute | solution.py:57
  224.0 18.8 %collective-permute-start.8 = (f32[64,1024]{1,0:T(8,128)S(1)}, f32[64,1024]{1,0:T(8,128)S(1)}, u32[]{:S(2)}, u32[]{:S(2)}) collective-permute-start(f32[64,1024]{1,0:T(8,128)S(1)} %add.163), channel_id=1, source_target_pairs={{0,256},{16,272},{32,288},{48,304},{64,320},{80,336},{96,352},{112... | collective-permute-start | bytes 786440 | tf_op jit(solution)/shard_map/ppermute | solution.py:57

commit v4 on v3

--- a/solution.py
+++ b/solution.py
@@ -6,6 +6,7 @@
 from jax.sharding import PartitionSpec as P
 
 TILE = 32
+GROUP_MINOR = 4
 
 
 def adjacency_of(slot_rows, weights, cand_width):
@@ -25,6 +26,27 @@
         chip, core = divmod(m, 2)
         label = ((chip - core) % chips) ^ (1 << bit)
         pairs.append((m, 2 * ((label + core) % chips) + core))
+    return pairs
+
+
+def group_pairs(groups, members, bit):
+    minor = GROUP_MINOR if groups % GROUP_MINOR == 0 else 1
+    major = groups // minor
+
+    def label(g, core):
+        y, x = divmod(g, minor)
+        return ((y - core) % major) * minor + (x - core) % minor
+
+    def unlabel(l, core):
+        y, x = divmod(l, minor)
+        return ((y + core) % major) * minor + (x + core) % minor
+
+    pairs = []
+    for g in range(groups):
+        for m in range(members):
+            core = m % 2
+            partner = unlabel(label(g, core) ^ (1 << bit), core)
+            pairs.append((g * members + m, partner * members + m))
     return pairs
 
 
@@ -54,7 +76,7 @@
         acc = keep + sent.astype(jnp.float32)
     acc = acc.reshape(rows // members, cols)
     for k in range(groups.bit_length() - 1):
-        acc = acc + lax.ppermute(acc, "group", xor_pairs(groups, k))
+        acc = acc + lax.ppermute(acc, ("group", "member"), group_pairs(groups, members, k))
     return acc
 
 
@@ -82,31 +104,58 @@
     )[:, 0]
     served = jnp.clip(asked_for, 0, tiles_dev - 1)
     remote = lax.all_to_all(own_tiles[served], "member", split_axis=0, concat_axis=0, tiled=True)
-    tile_pool = jnp.concatenate([remote, own_tiles], axis=0)
-    pool_index = jnp.where(foreign, holder, members + local_index).reshape(-1)
-    candidates = tile_pool[pool_index].reshape(blocks, cand_width, hidden_width)
+    pool_index = jnp.where(foreign, holder, members + local_index)
+    pool_rows = (members + tiles_dev) * TILE
+    slot_pool_row = (pool_index[:, :, None] * TILE + jnp.arange(TILE, dtype=jnp.int32)).reshape(
+        blocks, cand_width
+    )
+    place = (
+        slot_pool_row[:, :, None] == lax.broadcasted_iota(jnp.int32, (1, 1, pool_rows), 2)
+    ).astype(jnp.bfloat16)
     slot_rows = nbr_slot.reshape(blocks, block_rows, -1)
     weights = nbr_weight.reshape(blocks, block_rows, -1)
     adjacency = adjacency_of(slot_rows, weights, cand_width)
+    pool_adjacency = jnp.einsum(
+        "brc,bcp->brp", adjacency, place, preferred_element_type=jnp.float32
+    ).astype(jnp.bfloat16)
+    remote_rows = members * TILE
+    pool_adjacency = pool_adjacency.reshape(rows_dev, pool_rows)
     weight_total = jnp.sum(weights, axis=2).astype(jnp.float32)[..., None]
-    gathered = jnp.einsum("brc,bch->brh", adjacency, candidates, preferred_element_type=jnp.float32)
-    combined = gathered / weight_total + message.reshape(blocks, block_rows, hidden_width).astype(
-        jnp.float32
+    gathered = jnp.dot(
+        pool_adjacency[:, remote_rows:], message, preferred_element_type=jnp.float32
+    ) + jnp.dot(
+        pool_adjacency[:, :remote_rows],
+        remote.reshape(remote_rows, hidden_width),
+        preferred_element_type=jnp.float32,
     )
+    combined = gathered.reshape(blocks, block_rows, hidden_width) / weight_total + message.reshape(
+        blocks, block_rows, hidden_width
+    ).astype(jnp.float32)
     inv_rms = lax.rsqrt(jnp.mean(combined * combined, axis=2, keepdims=True) + 1e-06)
     normed = combined * inv_rms
     embedding = normed.astype(jnp.bfloat16).reshape(rows_dev, hidden_width)
     incoming = cotangent.reshape(blocks, block_rows, hidden_width).astype(jnp.float32)
     mixed_grad = inv_rms * (incoming - normed * jnp.mean(incoming * normed, axis=2, keepdims=True))
-    agg_grad = (mixed_grad / weight_total).astype(jnp.bfloat16)
-    cand_grad = jnp.einsum("brc,brh->bch", adjacency, agg_grad, preferred_element_type=jnp.float32)
-    cand_grad = cand_grad.reshape(blocks * tiles_per, TILE, hidden_width)
-    pool_size = members + tiles_dev
-    pool_grad = jax.ops.segment_sum(cand_grad, pool_index, num_segments=pool_size)
-    returned = pool_grad[:members].astype(jnp.bfloat16)
+    agg_grad = (mixed_grad / weight_total).astype(jnp.bfloat16).reshape(rows_dev, hidden_width)
+    by_rows = (((0,), (0,)), ((), ()))
+    remote_grad = lax.dot_general(
+        pool_adjacency[:, :remote_rows], agg_grad, by_rows, preferred_element_type=jnp.float32
+    )
+    returned = remote_grad.astype(jnp.bfloat16).reshape(members, TILE, hidden_width)
     came_back = lax.all_to_all(returned, "member", split_axis=0, concat_axis=0, tiled=True)
-    back_rows = jnp.where((asked_for >= 0)[:, None, None], came_back.astype(jnp.float32), 0.0)
-    tile_grad = pool_grad[members:].at[served].add(back_rows)
+    own_grad = lax.dot_general(
+        pool_adjacency[:, remote_rows:], agg_grad, by_rows, preferred_element_type=jnp.float32
+    )
+    back_to = (
+        (served[:, None] == lax.broadcasted_iota(jnp.int32, (1, tiles_dev), 1))
+        & (asked_for >= 0)[:, None]
+    ).astype(jnp.bfloat16)
+    tile_grad = own_grad.reshape(tiles_dev, TILE * hidden_width) + lax.dot_general(
+        back_to,
+        came_back.reshape(members, TILE * hidden_width),
+        by_rows,
+        preferred_element_type=jnp.float32,
+    )
     message_grad = mixed_grad.reshape(rows_dev, hidden_width) + tile_grad.reshape(
         rows_dev, hidden_width
     )

time: 246 us -> 222 us (0.902)
  the two profiles are of different devices: /device:TPU:6 before, /device:TPU:92 now
where the time goes in v4:
time: 222 us; the launch traced here: 221 us
  waiting for transfers between devices  107 us (48%)
  starting transfers between devices  55.3 us (25%)
  matrix products  21 us (9%)
  other arithmetic  19.3 us (9%)
  local copies, waits for them, and re-layouts  18 us (8%)
    ppermute x5, waiting for transfers between devices, reduce_rows(): lax.ppermute(acc, ('group', 'member'), group_pairs(groups, members, k))  44.1 us
    ppermute x3, waiting for transfers between devices, reduce_rows(): lax.ppermute(send.astype(jnp.bfloat16), 'member', shifted_pairs(members, k))  25.4 us
    all_to_all x1, waiting for transfers between devices, on_device(): lax.all_to_all(returned, 'member', split_axis=0, concat_axis=0, tiled=True)  18.1 us
    ppermute x5, starting transfers between devices, reduce_rows(): lax.ppermute(acc, ('group', 'member'), group_pairs(groups, members, k))  16.1 us
    ppermute x3, starting transfers between devices, reduce_rows(): lax.ppermute(send.astype(jnp.bfloat16), 'member', shifted_pairs(members, k))  14.4 us
    all_to_all x1, waiting for transfers between devices, on_device(): lax.all_to_all(own_tiles[served], 'member', split_axis=0, concat_axis=0,...  14.4 us
    all_to_all x1, starting transfers between devices, on_device(): lax.all_to_all(wanted.reshape(members, 1), 'member', split_axis=0, concat...  9.98 us
    unnamed x35, local copies, waits for them, and re-layouts  7.96 us
  transfers between devices with their start and end apart: 12, of which 12 were waited for; matrix products, arithmetic and copies ran while one was open for 10% of the time, Pallas kernels for 0%

profile of v4, /device:TPU:92, one launch (start us, length us, event | category | flops | bytes accessed | tf_op | source)
XLA Modules:
  0.0 221.1 jit_solution(17141709601125853494)
XLA Ops:
  0.6 0.8 broadcast_compare_fusion
  3.0 10.0 %all-to-all-start = ((s32[16,1,1]{2,1,0:T(1,128)}), s32[16,1,1]{2,1,0:T(1,128)S(1)}, u32[]{:S(2)}, u32[]{:S(2)}) async-start(s32[16,1,1]{2,1,0:T(1,128)} %copy.27), calls=%async_computation | async-start | bytes 16384 | tf_op jit(solution)/shard_map/all_to_all | solution.py:102
  13.0 3.8 %maximum_convert_fusion = (bf16[512,1024]{1,0:T(8,128)(2,1)S(1)}, f32[512,1024]{1,0:T(8,128)}) fusion(f32[1024]{0:T(1024)} %param.9, bf16[512,1024]{1,0:T(8,128)(2,1)} %param.7, bf16[1024,1024]{1,0:T(8,128)(2,1)S(1)} %copy-done), kind=kOutput, calls=%fused_computation.19 | convolution fusion | flops 1075314688 | bytes 6295552 | tf_op jit(solution)/shard_map/dot_general | solution.py:93
  16.8 2.3 %all-to-all-done = s32[16,1,1]{2,1,0:T(1,128)S(1)} async-done(((s32[16,1,1]{2,1,0:T(1,128)}), s32[16,1,1]{2,1,0:T(1,128)S(1)}, u32[]{:S(2)}, u32[]{:S(2)}) %all-to-all-start) | async-done | bytes 96 | tf_op jit(solution)/shard_map/all_to_all | solution.py:102
  19.5 1.6 gather_fusion
  21.1 5.6 %all-to-all-start.1 = ((bf16[16,32,1024]{2,1,0:T(8,128)(2,1)}), bf16[16,32,1024]{2,1,0:T(8,128)(2,1)}, u32[]{:S(2)}, u32[]{:S(2)}) async-start(bf16[16,32,1024]{2,1,0:T(8,128)(2,1)} %gather_fusion), calls=%async_computation.1 | async-start | bytes 2097152 | tf_op jit(solution)/shard_map/all_to_all | solution.py:106
  27.1 0.8 copy.29
  27.9 5.1 %select_reduce_fusion = s32[4,128,256]{2,1,0:T(8,128)S(1)} fusion(s32[4,128,16]{2,1,0:T(8,128)S(1)} %bitcast.60, s32[4,128,16]{2,1,0:T(8,128)} %bitcast.61), kind=kLoop, calls=%fused_computation.2 | loop fusion | flops 6160384 | bytes 589824 | tf_op jit(solution)/shard_map/reduce_sum | solution.py:15
  33.0 1.0 fusion.5
  34.0 1.0 copy-done.11
  35.0 2.1 fusion.12
  37.0 14.4 %all-to-all-done.1 = bf16[16,32,1024]{2,1,0:T(8,128)(2,1)} async-done(((bf16[16,32,1024]{2,1,0:T(8,128)(2,1)}), bf16[16,32,1024]{2,1,0:T(8,128)(2,1)}, u32[]{:S(2)}, u32[]{:S(2)}) %all-to-all-start.1) | async-done | bytes 1048608 | tf_op jit(solution)/shard_map/all_to_all | solution.py:106
  51.4 3.4 %multiply_reduce_fusion = (f32[512]{0:T(512)S(1)}, f32[512,1024]{1,0:T(8,128)S(1)}) fusion(bf16[512,1024]{1,0:T(8,128)(2,1)} %copy-done.9, f32[512]{0:T(512)S(1)} %convert_element_type.87, f32[512,1024]{1,0:T(8,128)} %fusion.12, bf16[512,1024]{1,0:T(8,128)(2,1)} %bitcast.6, bf16[512,1024]{1,0:T(8,128)(2,1)} %bitcast.56), kind=kOutput, calls=%fused_computation.17 | convolution fusion | flops 540016128 | bytes 6819840 | tf_op jit(solution)/shard_map/dot_general | solution.py:126
  56.8 1.7 convolution_convert_fusion.1
  58.5 6.8 %all-to-all-start.2 = ((bf16[16,32,1024]{2,1,0:T(8,128)(2,1)}), bf16[16,32,1024]{2,1,0:T(8,128)(2,1)}, u32[]{:S(2)}, u32[]{:S(2)}) async-start(bf16[16,32,1024]{2,1,0:T(8,128)(2,1)} %bitcast.59), calls=%async_computation.2 | async-start | bytes 2097152 | tf_op jit(solution)/shard_map/all_to_all | solution.py:145
  65.7 3.5 %fusion.10 = f32[512,1024]{1,0:T(8,128)} fusion(bf16[512,1024]{1,0:T(8,128)(2,1)} %copy-done.8, bf16[512,1024]{1,0:T(8,128)(2,1)} %bitcast.57), kind=kOutput, calls=%fused_computation.33 | convolution fusion | flops 536870912 | bytes 3670016 | tf_op jit(solution)/shard_map/dot_general | solution.py:146
  69.2 2.8 %reshape.166 = f32[16,32768]{1,0:T(8,128)} reshape(f32[512,1024]{1,0:T(8,128)} %fusion.10) | data formatting | bytes 4194304 | tf_op jit(solution)/shard_map/reshape | solution.py:153
  72.0 18.1 %all-to-all-done.2 = bf16[16,32,1024]{2,1,0:T(8,128)(2,1)} async-done(((bf16[16,32,1024]{2,1,0:T(8,128)(2,1)}), bf16[16,32,1024]{2,1,0:T(8,128)(2,1)}, u32[]{:S(2)}, u32[]{:S(2)}) %all-to-all-start.2) | async-done | bytes 1048608 | tf_op jit(solution)/shard_map/all_to_all | solution.py:145
  90.0 2.0 copy.32
  92.0 1.9 convolution_add_fusion
  93.9 2.8 %reshape.169 = f32[512,1024]{1,0:T(8,128)} reshape(f32[16,32768]{1,0:T(8,128)} %convolution_add_fusion) | data formatting | bytes 4194304 | tf_op jit(solution)/shard_map/reshape | solution.py:159
  96.7 4.6 %select_convert_fusion = (bf16[512,1024]{1,0:T(8,128)(2,1)S(1)}, bf16[512,1024]{1,0:T(8,128)(2,1)}) fusion(f32[512,1024]{1,0:T(8,128)} %reshape.169, f32[512,1024]{1,0:T(8,128)} %get-tuple-element.10, f32[512,1024]{1,0:T(8,128)} %copy-done.1, bf16[512,1024]{1,0:T(8,128)(2,1)S(1)} %copy-done.3, f32[512]{0:T(512)S(1)} %broadcast_multiply_fusion, ...), kind=kLoop, calls=%fused_computation.15 | loop fusion | flops 5767168 | bytes 9445376 | tf_op jit(solution)/shard_map/convert_element_type | solution.py:162
  101.4 1.3 fusion.23
  102.7 2.0 copy-done.2
  104.9 2.5 %collective-permute-start = (bf16[8,64,1024]{2,1,0:T(8,128)(2,1)S(1)}, bf16[8,64,1024]{2,1,0:T(8,128)(2,1)}, u32[]{:S(2)}, u32[]{:S(2)}) collective-permute-start(bf16[8,64,1024]{2,1,0:T(8,128)(2,1)S(1)} %fusion.6), channel_id=1, source_target_pairs={{0,1},{1,0},{2,3},{3,2},{4,5},{5,4},{6,7},{7,6},{8,9},{9,8},{10,11... | collective-permute-start | bytes 3145736 | tf_op jit(solution)/shard_map/ppermute | solution.py:69
  107.4 2.2 collective-permute-done
  109.6 2.2 %bitcast_add_fusion = f32[8,64,1024]{2,1,0:T(8,128)S(1)} fusion(bf16[8,64,1024]{2,1,0:T(8,128)(2,1)} %collective-permute-done, f32[8,2,64,1024]{3,2,1,0:T(8,128)} %bitcast.48, s32[]{:T(128)S(6)} %select_n.90), kind=kLoop, calls=%fused_computation.14 | loop fusion | flops 1048576 | bytes 5242884 | tf_op jit(solution)/shard_map/add | solution.py:70
  112.3 1.3 copy-done.5
  113.7 5.3 %collective-permute-start.1 = (bf16[4,64,1024]{2,1,0:T(8,128)(2,1)S(1)}, bf16[4,64,1024]{2,1,0:T(8,128)(2,1)}, u32[]{:S(2)}, u32[]{:S(2)}) collective-permute-start(bf16[4,64,1024]{2,1,0:T(8,128)(2,1)S(1)} %fusion.7), channel_id=1, source_target_pairs={{0,2},{1,15},{2,0},{3,5},{4,6},{5,3},{6,4},{7,9},{8,10},{9,7},{10,... | collective-permute-start | bytes 1572872 | tf_op jit(solution)/shard_map/ppermute | solution.py:75
  119.1 7.2 %collective-permute-done.1 = bf16[4,64,1024]{2,1,0:T(8,128)(2,1)} collective-permute-done((bf16[4,64,1024]{2,1,0:T(8,128)(2,1)S(1)}, bf16[4,64,1024]{2,1,0:T(8,128)(2,1)}, u32[]{:S(2)}, u32[]{:S(2)}) %collective-permute-start.1) | collective-permute-done | bytes 524320 | tf_op jit(solution)/shard_map/ppermute | solution.py:75
  126.3 1.5 bitcast_add_fusion.1
  128.6 4.4 %collective-permute-start.2 = (bf16[2,64,1024]{2,1,0:T(8,128)(2,1)}, bf16[2,64,1024]{2,1,0:T(8,128)(2,1)S(1)}, u32[]{:S(2)}, u32[]{:S(2)}) collective-permute-start(bf16[2,64,1024]{2,1,0:T(8,128)(2,1)} %fusion.14), channel_id=1, source_target_pairs={{0,4},{1,13},{2,6},{3,7},{4,0},{5,9},{6,2},{7,3},{8,12},{9,5},{10,... | collective-permute-start | bytes 786440 | tf_op jit(solution)/shard_map/ppermute | solution.py:75
  133.0 9.8 %collective-permute-done.2 = bf16[2,64,1024]{2,1,0:T(8,128)(2,1)S(1)} collective-permute-done((bf16[2,64,1024]{2,1,0:T(8,128)(2,1)}, bf16[2,64,1024]{2,1,0:T(8,128)(2,1)S(1)}, u32[]{:S(2)}, u32[]{:S(2)}) %collective-permute-start.2) | collective-permute-done | bytes 262176 | tf_op jit(solution)/shard_map/ppermute | solution.py:75
  142.9 0.8 copy-done.10
  143.7 4.7 %collective-permute-start.3 = (bf16[1,64,1024]{2,1,0:T(8,128)(2,1)S(1)}, bf16[1,64,1024]{2,1,0:T(8,128)(2,1)S(1)}, u32[]{:S(2)}, u32[]{:S(2)}) collective-permute-start(bf16[1,64,1024]{2,1,0:T(8,128)(2,1)S(1)} %dynamic-slice_convert_fusion.2), channel_id=1, source_target_pairs={{0,8},{1,9},{2,10},{3,11},{4,12},{5,13},{6,14},{7,15},{8,0},{9,1},... | collective-permute-start | bytes 393224 | tf_op jit(solution)/shard_map/ppermute | solution.py:75
  148.3 8.4 %collective-permute-done.3 = bf16[1,64,1024]{2,1,0:T(8,128)(2,1)S(1)} collective-permute-done((bf16[1,64,1024]{2,1,0:T(8,128)(2,1)S(1)}, bf16[1,64,1024]{2,1,0:T(8,128)(2,1)S(1)}, u32[]{:S(2)}, u32[]{:S(2)}) %collective-permute-start.3) | collective-permute-done | bytes 131104 | tf_op jit(solution)/shard_map/ppermute | solution.py:75
  156.8 1.0 add_bitcast_fusion
  157.8 3.1 %collective-permute-start.4 = (f32[64,1024]{1,0:T(8,128)S(1)}, f32[64,1024]{1,0:T(8,128)S(1)}, u32[]{:S(2)}, u32[]{:S(2)}) collective-permute-start(f32[64,1024]{1,0:T(8,128)S(1)} %add_bitcast_fusion), channel_id=1, source_target_pairs={{0,16},{1,49},{2,18},{3,51},{4,20},{5,53},{6,22},{7,55},{8,24},{9,... | collective-permute-start | bytes 786440 | tf_op jit(solution)/shard_map/ppermute | solution.py:79
  160.9 5.2 %collective-permute-done.4 = f32[64,1024]{1,0:T(8,128)S(1)} collective-permute-done((f32[64,1024]{1,0:T(8,128)S(1)}, f32[64,1024]{1,0:T(8,128)S(1)}, u32[]{:S(2)}, u32[]{:S(2)}) %collective-permute-start.4) | collective-permute-done | bytes 262176 | tf_op jit(solution)/shard_map/ppermute | solution.py:79
  166.1 2.4 %collective-permute-start.5 = (f32[64,1024]{1,0:T(8,128)S(1)}, f32[64,1024]{1,0:T(8,128)S(1)}, u32[]{:S(2)}, u32[]{:S(2)}) collective-permute-start(f32[64,1024]{1,0:T(8,128)S(1)} %add.182), channel_id=1, source_target_pairs={{0,32},{1,33},{2,34},{3,35},{4,36},{5,37},{6,38},{7,39},{8,40},{9,... | collective-permute-start | bytes 786440 | tf_op jit(solution)/shard_map/ppermute | solution.py:79
  168.5 7.4 %collective-permute-done.5 = f32[64,1024]{1,0:T(8,128)S(1)} collective-permute-done((f32[64,1024]{1,0:T(8,128)S(1)}, f32[64,1024]{1,0:T(8,128)S(1)}, u32[]{:S(2)}, u32[]{:S(2)}) %collective-permute-start.5) | collective-permute-done | bytes 262176 | tf_op jit(solution)/shard_map/ppermute | solution.py:79
  175.9 2.4 %collective-permute-start.6 = (f32[64,1024]{1,0:T(8,128)S(1)}, f32[64,1024]{1,0:T(8,128)S(1)}, u32[]{:S(2)}, u32[]{:S(2)}) collective-permute-start(f32[64,1024]{1,0:T(8,128)S(1)} %add.183), channel_id=1, source_target_pairs={{0,64},{1,449},{2,66},{3,451},{4,68},{5,453},{6,70},{7,455},{8,72}... | collective-permute-start | bytes 786440 | tf_op jit(solution)/shard_map/ppermute | solution.py:79
  178.2 9.5 %collective-permute-done.6 = f32[64,1024]{1,0:T(8,128)S(1)} collective-permute-done((f32[64,1024]{1,0:T(8,128)S(1)}, f32[64,1024]{1,0:T(8,128)S(1)}, u32[]{:S(2)}, u32[]{:S(2)}) %collective-permute-start.6) | collective-permute-done | bytes 262176 | tf_op jit(solution)/shard_map/ppermute | solution.py:79
  187.8 1.9 collective-permute-start.7
  189.7 15.7 %collective-permute-done.7 = f32[64,1024]{1,0:T(8,128)S(1)} collective-permute-done((f32[64,1024]{1,0:T(8,128)S(1)}, f32[64,1024]{1,0:T(8,128)S(1)}, u32[]{:S(2)}, u32[]{:S(2)}) %collective-permute-start.7) | collective-permute-done | bytes 262176 | tf_op jit(solution)/shard_map/ppermute | solution.py:79
  205.4 6.3 %collective-permute-start.8 = (f32[64,1024]{1,0:T(8,128)S(1)}, f32[64,1024]{1,0:T(8,128)S(1)}, u32[]{:S(2)}, u32[]{:S(2)}) collective-permute-start(f32[64,1024]{1,0:T(8,128)S(1)} %add.185), channel_id=1, source_target_pairs={{0,256},{1,257},{2,258},{3,259},{4,260},{5,261},{6,262},{7,263},{8... | collective-permute-start | bytes 786440 | tf_op jit(solution)/shard_map/ppermute | solution.py:79
  211.7 2.3 %convolution_convert_fusion = bf16[512,1024]{1,0:T(8,128)(2,1)} fusion(bf16[512,1024]{1,0:T(8,128)(2,1)S(1)} %copy-done.7, bf16[1024,1024]{1,0:T(8,128)(2,1)S(1)} %copy-done), kind=kOutput, calls=%fused_computation.23 | convolution fusion | flops 1074266112 | bytes 4194304 | tf_op jit(solution)/shard_map/dot_general | solution.py:163
  214.0 6.4 %collective-permute-done.8 = f32[64,1024]{1,0:T(8,128)S(1)} collective-permute-done((f32[64,1024]{1,0:T(8,128)S(1)}, f32[64,1024]{1,0:T(8,128)S(1)}, u32[]{:S(2)}, u32[]{:S(2)}) %collective-permute-start.8) | collective-permute-done | bytes 262176 | tf_op jit(solution)/shard_map/ppermute | solution.py:79
  (60 shorter events, 7.0 us)
Async XLA Ops:
  0.6 12.3 %copy-start = (bf16[1024,1024]{1,0:T(8,128)(2,1)S(1)}, bf16[1024,1024]{1,0:T(8,128)(2,1)}, u32[]{:S(2)}) copy-start(bf16[1024,1024]{1,0:T(8,128)(2,1)} %param.8) | copy-start | bytes 6291460
  3.0 16.1 %all-to-all-start = ((s32[16,1,1]{2,1,0:T(1,128)}), s32[16,1,1]{2,1,0:T(1,128)S(1)}, u32[]{:S(2)}, u32[]{:S(2)}) async-start(s32[16,1,1]{2,1,0:T(1,128)} %copy.27), calls=%async_computation | async-start | bytes 16384 | tf_op jit(solution)/shard_map/all_to_all | solution.py:102
  16.8 17.2 %copy-start.9 = (bf16[512,1024]{1,0:T(8,128)(2,1)}, bf16[512,1024]{1,0:T(8,128)(2,1)S(1)}, u32[]{:S(2)}) copy-start(bf16[512,1024]{1,0:T(8,128)(2,1)S(1)} %get-tuple-element.9) | copy-start | bytes 3145732
  19.5 7.2 %copy-start.14 = (s32[512,16]{0,1:T(8,128)S(1)}, s32[512,16]{0,1:T(8,128)}, u32[]{:S(2)}) copy-start(s32[512,16]{0,1:T(8,128)} %param.12) | copy-start | bytes 98308
  19.5 7.6 %copy-start.15 = (s32[512,16]{0,1:T(8,128)S(1)}, s32[512,16]{0,1:T(8,128)}, u32[]{:S(2)}) copy-start(s32[512,16]{0,1:T(8,128)} %param.11) | copy-start | bytes 98308
  21.1 30.3 %all-to-all-start.1 = ((bf16[16,32,1024]{2,1,0:T(8,128)(2,1)}), bf16[16,32,1024]{2,1,0:T(8,128)(2,1)}, u32[]{:S(2)}, u32[]{:S(2)}) async-start(bf16[16,32,1024]{2,1,0:T(8,128)(2,1)} %gather_fusion), calls=%async_computation.1 | async-start | bytes 2097152 | tf_op jit(solution)/shard_map/all_to_all | solution.py:106
  34.0 1.0 copy-start.11
  51.4 3.4 %copy-start.3 = (bf16[512,1024]{1,0:T(8,128)(2,1)S(1)}, bf16[512,1024]{1,0:T(8,128)(2,1)}, u32[]{:S(2)}) copy-start(bf16[512,1024]{1,0:T(8,128)(2,1)} %param.13) | copy-start | bytes 3145732
  54.8 1.3 copy-start.1
  55.3 1.5 copy-start.12
  56.8 1.7 copy-start.8
  58.5 31.6 %all-to-all-start.2 = ((bf16[16,32,1024]{2,1,0:T(8,128)(2,1)}), bf16[16,32,1024]{2,1,0:T(8,128)(2,1)}, u32[]{:S(2)}, u32[]{:S(2)}) async-start(bf16[16,32,1024]{2,1,0:T(8,128)(2,1)} %bitcast.59), calls=%async_computation.2 | async-start | bytes 2097152 | tf_op jit(solution)/shard_map/all_to_all | solution.py:145
  90.0 2.0 copy-start.4
  93.9 2.8 %copy-start.16 = (f32[1024]{0:T(1024)S(1)}, f32[1024]{0:T(1024)}, u32[]{:S(2)}) copy-start(f32[1024]{0:T(1024)} %param.9) | copy-start | bytes 12292
  96.7 4.7 %copy-start.13 = (bf16[512,1024]{1,0:T(8,128)(2,1)S(1)}, bf16[512,1024]{1,0:T(8,128)(2,1)}, u32[]{:S(2)}) copy-start(bf16[512,1024]{1,0:T(8,128)(2,1)} %param.7) | copy-start | bytes 3145732
  101.4 1.4 copy-start.6
  102.7 2.0 copy-start.2
  104.9 4.7 %collective-permute-start = (bf16[8,64,1024]{2,1,0:T(8,128)(2,1)S(1)}, bf16[8,64,1024]{2,1,0:T(8,128)(2,1)}, u32[]{:S(2)}, u32[]{:S(2)}) collective-permute-start(bf16[8,64,1024]{2,1,0:T(8,128)(2,1)S(1)} %fusion.6), channel_id=1, source_target_pairs={{0,1},{1,0},{2,3},{3,2},{4,5},{5,4},{6,7},{7,6},{8,9},{9,8},{10,11... | collective-permute-start | bytes 3145736 | tf_op jit(solution)/shard_map/ppermute | solution.py:69
  112.3 1.3 copy-start.5
  113.7 12.6 %collective-permute-start.1 = (bf16[4,64,1024]{2,1,0:T(8,128)(2,1)S(1)}, bf16[4,64,1024]{2,1,0:T(8,128)(2,1)}, u32[]{:S(2)}, u32[]{:S(2)}) collective-permute-start(bf16[4,64,1024]{2,1,0:T(8,128)(2,1)S(1)} %fusion.7), channel_id=1, source_target_pairs={{0,2},{1,15},{2,0},{3,5},{4,6},{5,3},{6,4},{7,9},{8,10},{9,7},{10,... | collective-permute-start | bytes 1572872 | tf_op jit(solution)/shard_map/ppermute | solution.py:75
  128.6 14.2 %collective-permute-start.2 = (bf16[2,64,1024]{2,1,0:T(8,128)(2,1)}, bf16[2,64,1024]{2,1,0:T(8,128)(2,1)S(1)}, u32[]{:S(2)}, u32[]{:S(2)}) collective-permute-start(bf16[2,64,1024]{2,1,0:T(8,128)(2,1)} %fusion.14), channel_id=1, source_target_pairs={{0,4},{1,13},{2,6},{3,7},{4,0},{5,9},{6,2},{7,3},{8,12},{9,5},{10,... | collective-permute-start | bytes 786440 | tf_op jit(solution)/shard_map/ppermute | solution.py:75
  142.9 0.8 copy-start.10
  143.7 68.1 %copy-start.7 = (bf16[512,1024]{1,0:T(8,128)(2,1)S(1)}, bf16[512,1024]{1,0:T(8,128)(2,1)}, u32[]{:S(2)}) copy-start(bf16[512,1024]{1,0:T(8,128)(2,1)} %copy-done.6) | copy-start | bytes 3145732
  143.7 13.1 %collective-permute-start.3 = (bf16[1,64,1024]{2,1,0:T(8,128)(2,1)S(1)}, bf16[1,64,1024]{2,1,0:T(8,128)(2,1)S(1)}, u32[]{:S(2)}, u32[]{:S(2)}) collective-permute-start(bf16[1,64,1024]{2,1,0:T(8,128)(2,1)S(1)} %dynamic-slice_convert_fusion.2), channel_id=1, source_target_pairs={{0,8},{1,9},{2,10},{3,11},{4,12},{5,13},{6,14},{7,15},{8,0},{9,1},... | collective-permute-start | bytes 393224 | tf_op jit(solution)/shard_map/ppermute | solution.py:75
  157.8 8.3 %collective-permute-start.4 = (f32[64,1024]{1,0:T(8,128)S(1)}, f32[64,1024]{1,0:T(8,128)S(1)}, u32[]{:S(2)}, u32[]{:S(2)}) collective-permute-start(f32[64,1024]{1,0:T(8,128)S(1)} %add_bitcast_fusion), channel_id=1, source_target_pairs={{0,16},{1,49},{2,18},{3,51},{4,20},{5,53},{6,22},{7,55},{8,24},{9,... | collective-permute-start | bytes 786440 | tf_op jit(solution)/shard_map/ppermute | solution.py:79
  166.1 9.8 %collective-permute-start.5 = (f32[64,1024]{1,0:T(8,128)S(1)}, f32[64,1024]{1,0:T(8,128)S(1)}, u32[]{:S(2)}, u32[]{:S(2)}) collective-permute-start(f32[64,1024]{1,0:T(8,128)S(1)} %add.182), channel_id=1, source_target_pairs={{0,32},{1,33},{2,34},{3,35},{4,36},{5,37},{6,38},{7,39},{8,40},{9,... | collective-permute-start | bytes 786440 | tf_op jit(solution)/shard_map/ppermute | solution.py:79
  175.9 11.9 %collective-permute-start.6 = (f32[64,1024]{1,0:T(8,128)S(1)}, f32[64,1024]{1,0:T(8,128)S(1)}, u32[]{:S(2)}, u32[]{:S(2)}) collective-permute-start(f32[64,1024]{1,0:T(8,128)S(1)} %add.183), channel_id=1, source_target_pairs={{0,64},{1,449},{2,66},{3,451},{4,68},{5,453},{6,70},{7,455},{8,72}... | collective-permute-start | bytes 786440 | tf_op jit(solution)/shard_map/ppermute | solution.py:79
  187.8 17.6 %collective-permute-start.7 = (f32[64,1024]{1,0:T(8,128)S(1)}, f32[64,1024]{1,0:T(8,128)S(1)}, u32[]{:S(2)}, u32[]{:S(2)}) collective-permute-start(f32[64,1024]{1,0:T(8,128)S(1)} %add.184), channel_id=1, source_target_pairs={{0,128},{1,385},{2,130},{3,387},{4,132},{5,389},{6,134},{7,391},{8... | collective-permute-start | bytes 786440 | tf_op jit(solution)/shard_map/ppermute | solution.py:79
  205.4 15.0 %collective-permute-start.8 = (f32[64,1024]{1,0:T(8,128)S(1)}, f32[64,1024]{1,0:T(8,128)S(1)}, u32[]{:S(2)}, u32[]{:S(2)}) collective-permute-start(f32[64,1024]{1,0:T(8,128)S(1)} %add.185), channel_id=1, source_target_pairs={{0,256},{1,257},{2,258},{3,259},{4,260},{5,261},{6,262},{7,263},{8... | collective-permute-start | bytes 786440 | tf_op jit(solution)/shard_map/ppermute | solution.py:79

commit v5 on v4

--- a/solution.py
+++ b/solution.py
@@ -6,7 +6,6 @@
 from jax.sharding import PartitionSpec as P
 
 TILE = 32
-GROUP_MINOR = 4
 
 
 def adjacency_of(slot_rows, weights, cand_width):
@@ -26,27 +25,6 @@
         chip, core = divmod(m, 2)
         label = ((chip - core) % chips) ^ (1 << bit)
         pairs.append((m, 2 * ((label + core) % chips) + core))
-    return pairs
-
-
-def group_pairs(groups, members, bit):
-    minor = GROUP_MINOR if groups % GROUP_MINOR == 0 else 1
-    major = groups // minor
-
-    def label(g, core):
-        y, x = divmod(g, minor)
-        return ((y - core) % major) * minor + (x - core) % minor
-
-    def unlabel(l, core):
-        y, x = divmod(l, minor)
-        return ((y + core) % major) * minor + (x + core) % minor
-
-    pairs = []
-    for g in range(groups):
-        for m in range(members):
-            core = m % 2
-            partner = unlabel(label(g, core) ^ (1 << bit), core)
-            pairs.append((g * members + m, partner * members + m))
     return pairs
 
 
@@ -74,10 +52,12 @@
         keep, send = halve(acc, (label >> k) & 1)
         sent = lax.ppermute(send.astype(jnp.bfloat16), "member", shifted_pairs(members, k))
         acc = keep + sent.astype(jnp.float32)
-    acc = acc.reshape(rows // members, cols)
-    for k in range(groups.bit_length() - 1):
-        acc = acc + lax.ppermute(acc, ("group", "member"), group_pairs(groups, members, k))
-    return acc
+    slices = acc.reshape(groups, -1)
+    mine = jnp.sum(lax.all_to_all(slices, "group", split_axis=0, concat_axis=0, tiled=True), axis=0)
+    every = lax.all_to_all(
+        jnp.broadcast_to(mine, slices.shape), "group", split_axis=0, concat_axis=0, tiled=True
+    )
+    return every.reshape(rows // members, cols)
 
 
 def on_device(feats, transform, bias, tile_list, nbr_slot, nbr_weight, cotangent):

time: 222 us -> 201 us (0.905)
  the two profiles are of different devices: /device:TPU:92 before, /device:TPU:6 now
where the time goes in v5:
time: 201 us; the launch traced here: 198 us
  waiting for transfers between devices  78.9 us (39%)
  starting transfers between devices  35.5 us (18%)
  local copies, waits for them, and re-layouts  21.5 us (11%)
  matrix products  20.9 us (10%)
  other arithmetic  20.2 us (10%)
  blocking collectives  20.1 us (10%)
    ppermute x3, waiting for transfers between devices, reduce_rows(): lax.ppermute(send.astype(jnp.bfloat16), 'member', shifted_pairs(members, k))  29.3 us
    all_to_all x1, blocking collectives, reduce_rows(): lax.all_to_all(slices, 'group', split_axis=0, concat_axis=0, tiled=True)  20.1 us
    all_to_all x1, waiting for transfers between devices, on_device(): lax.all_to_all(returned, 'member', split_axis=0, concat_axis=0, tiled=True)  19.9 us
    all_to_all x1, waiting for transfers between devices, on_device(): lax.all_to_all(own_tiles[served], 'member', split_axis=0, concat_axis=0,...  16.2 us
    all_to_all x1, starting transfers between devices, on_device(): lax.all_to_all(wanted.reshape(members, 1), 'member', split_axis=0, concat...  10.4 us
    unnamed x37, local copies, waits for them, and re-layouts  8.91 us
    all_to_all x1, waiting for transfers between devices, reduce_rows(): lax.all_to_all(jnp.broadcast_to(mine, slices.shape), 'group', split_axis=...  7.65 us
    ppermute x3, starting transfers between devices, reduce_rows(): lax.ppermute(send.astype(jnp.bfloat16), 'member', shifted_pairs(members, k))  6.26 us
  transfers between devices with their start and end apart: 8, of which 8 were waited for; matrix products, arithmetic and copies ran while one was open for 11% of the time, Pallas kernels for 0%

profile of v5, /device:TPU:6, one launch (start us, length us, event | category | flops | bytes accessed | tf_op | source)
XLA Modules:
  0.0 198.2 jit_solution(9547069968417476772)
XLA Ops:
  0.6 0.8 broadcast_compare_fusion
  3.0 10.4 %all-to-all-start = ((s32[16,1,1]{2,1,0:T(1,128)}), s32[16,1,1]{2,1,0:T(1,128)S(1)}, u32[]{:S(2)}, u32[]{:S(2)}) async-start(s32[16,1,1]{2,1,0:T(1,128)} %copy.26), calls=%async_computation | async-start | bytes 16384 | tf_op jit(solution)/shard_map/all_to_all | solution.py:82
  13.4 3.8 %maximum_convert_fusion = (bf16[512,1024]{1,0:T(8,128)(2,1)S(1)}, f32[512,1024]{1,0:T(8,128)}) fusion(f32[1024]{0:T(1024)} %param.9, bf16[512,1024]{1,0:T(8,128)(2,1)} %param.7, bf16[1024,1024]{1,0:T(8,128)(2,1)S(1)} %copy-done), kind=kOutput, calls=%fused_computation.19 | convolution fusion | flops 1075314688 | bytes 6295552 | tf_op jit(solution)/shard_map/dot_general | solution.py:73
  17.2 3.7 %all-to-all-done = s32[16,1,1]{2,1,0:T(1,128)S(1)} async-done(((s32[16,1,1]{2,1,0:T(1,128)}), s32[16,1,1]{2,1,0:T(1,128)S(1)}, u32[]{:S(2)}, u32[]{:S(2)}) %all-to-all-start) | async-done | bytes 96 | tf_op jit(solution)/shard_map/all_to_all | solution.py:82
  21.3 1.6 gather_fusion
  22.9 4.3 %all-to-all-start.1 = ((bf16[16,32,1024]{2,1,0:T(8,128)(2,1)}), bf16[16,32,1024]{2,1,0:T(8,128)(2,1)}, u32[]{:S(2)}, u32[]{:S(2)}) async-start(bf16[16,32,1024]{2,1,0:T(8,128)(2,1)} %gather_fusion), calls=%async_computation.1 | async-start | bytes 2097152 | tf_op jit(solution)/shard_map/all_to_all | solution.py:86
  27.7 0.8 copy.29
  28.5 5.1 %select_reduce_fusion = s32[4,128,256]{2,1,0:T(8,128)S(1)} fusion(s32[4,128,16]{2,1,0:T(8,128)S(1)} %bitcast.58, s32[4,128,16]{2,1,0:T(8,128)} %bitcast.59), kind=kLoop, calls=%fused_computation.2 | loop fusion | flops 6160384 | bytes 589824 | tf_op jit(solution)/shard_map/reduce_sum | solution.py:14
  33.6 1.0 fusion.5
  34.6 1.0 copy-done.12
  35.6 2.0 %fusion.12 = f32[512,1024]{1,0:T(8,128)} fusion(bf16[512,1024]{1,0:T(8,128)(2,1)S(1)} %get-tuple-element.9, bf16[512,1024]{1,0:T(8,128)(2,1)S(1)} %bitcast.53), kind=kOutput, calls=%fused_computation.35 | convolution fusion | flops 536870912 | bytes 3670016 | tf_op jit(solution)/shard_map/dot_general | solution.py:104
  37.6 16.2 %all-to-all-done.1 = bf16[16,32,1024]{2,1,0:T(8,128)(2,1)} async-done(((bf16[16,32,1024]{2,1,0:T(8,128)(2,1)}), bf16[16,32,1024]{2,1,0:T(8,128)(2,1)}, u32[]{:S(2)}, u32[]{:S(2)}) %all-to-all-start.1) | async-done | bytes 1048608 | tf_op jit(solution)/shard_map/all_to_all | solution.py:86
  53.8 3.4 %multiply_reduce_fusion = (f32[512]{0:T(512)S(1)}, f32[512,1024]{1,0:T(8,128)S(1)}) fusion(bf16[512,1024]{1,0:T(8,128)(2,1)} %copy-done.9, f32[512]{0:T(512)S(1)} %convert_element_type.87, f32[512,1024]{1,0:T(8,128)} %fusion.12, bf16[512,1024]{1,0:T(8,128)(2,1)} %bitcast.6, bf16[512,1024]{1,0:T(8,128)(2,1)} %bitcast.54), kind=kOutput, calls=%fused_computation.17 | convolution fusion | flops 540016128 | bytes 6819840 | tf_op jit(solution)/shard_map/dot_general | solution.py:106
  59.2 1.7 convolution_convert_fusion.1
  60.9 4.9 %all-to-all-start.2 = ((bf16[16,32,1024]{2,1,0:T(8,128)(2,1)}), bf16[16,32,1024]{2,1,0:T(8,128)(2,1)}, u32[]{:S(2)}, u32[]{:S(2)}) async-start(bf16[16,32,1024]{2,1,0:T(8,128)(2,1)} %bitcast.57), calls=%async_computation.2 | async-start | bytes 2097152 | tf_op jit(solution)/shard_map/all_to_all | solution.py:125
  66.2 3.5 %fusion.10 = f32[512,1024]{1,0:T(8,128)} fusion(bf16[512,1024]{1,0:T(8,128)(2,1)} %copy-done.8, bf16[512,1024]{1,0:T(8,128)(2,1)} %bitcast.55), kind=kOutput, calls=%fused_computation.33 | convolution fusion | flops 536870912 | bytes 3670016 | tf_op jit(solution)/shard_map/dot_general | solution.py:126
  69.7 2.8 %reshape.175 = f32[16,32768]{1,0:T(8,128)} reshape(f32[512,1024]{1,0:T(8,128)} %fusion.10) | data formatting | bytes 4194304 | tf_op jit(solution)/shard_map/reshape | solution.py:133
  72.4 19.9 %all-to-all-done.2 = bf16[16,32,1024]{2,1,0:T(8,128)(2,1)} async-done(((bf16[16,32,1024]{2,1,0:T(8,128)(2,1)}), bf16[16,32,1024]{2,1,0:T(8,128)(2,1)}, u32[]{:S(2)}, u32[]{:S(2)}) %all-to-all-start.2) | async-done | bytes 1048608 | tf_op jit(solution)/shard_map/all_to_all | solution.py:125
  92.3 2.0 copy.32
  94.3 1.9 convolution_add_fusion
  96.2 2.8 %reshape.178 = f32[512,1024]{1,0:T(8,128)} reshape(f32[16,32768]{1,0:T(8,128)} %convolution_add_fusion) | data formatting | bytes 4194304 | tf_op jit(solution)/shard_map/reshape | solution.py:139
  99.0 4.6 %select_convert_fusion = (bf16[512,1024]{1,0:T(8,128)(2,1)S(1)}, bf16[512,1024]{1,0:T(8,128)(2,1)}) fusion(f32[512,1024]{1,0:T(8,128)} %reshape.178, f32[512,1024]{1,0:T(8,128)} %get-tuple-element.10, f32[512,1024]{1,0:T(8,128)} %copy-done.1, bf16[512,1024]{1,0:T(8,128)(2,1)S(1)} %copy-done.3, f32[512]{0:T(512)S(1)} %broadcast_multiply_fusion, ...), kind=kLoop, calls=%fused_computation.15 | loop fusion | flops 5767168 | bytes 9445376 | tf_op jit(solution)/shard_map/convert_element_type | solution.py:142
  103.6 1.3 fusion.23
  105.0 1.9 copy-done.2
  107.1 4.0 %collective-permute-start = (bf16[8,64,1024]{2,1,0:T(8,128)(2,1)S(1)}, bf16[8,64,1024]{2,1,0:T(8,128)(2,1)}, u32[]{:S(2)}, u32[]{:S(2)}) collective-permute-start(bf16[8,64,1024]{2,1,0:T(8,128)(2,1)S(1)} %fusion.6), channel_id=1, source_target_pairs={{0,1},{1,0},{2,3},{3,2},{4,5},{5,4},{6,7},{7,6},{8,9},{9,8},{10,11... | collective-permute-start | bytes 3145736 | tf_op jit(solution)/shard_map/ppermute | solution.py:47
  111.1 2.2 %collective-permute-done = bf16[8,64,1024]{2,1,0:T(8,128)(2,1)} collective-permute-done((bf16[8,64,1024]{2,1,0:T(8,128)(2,1)S(1)}, bf16[8,64,1024]{2,1,0:T(8,128)(2,1)}, u32[]{:S(2)}, u32[]{:S(2)}) %collective-permute-start) | collective-permute-done | bytes 1048608 | tf_op jit(solution)/shard_map/ppermute | solution.py:47
  113.3 2.2 %bitcast_add_fusion = f32[8,64,1024]{2,1,0:T(8,128)S(1)} fusion(bf16[8,64,1024]{2,1,0:T(8,128)(2,1)} %collective-permute-done, f32[8,2,64,1024]{3,2,1,0:T(8,128)} %bitcast.46, s32[]{:T(128)S(6)} %select_n.90), kind=kLoop, calls=%fused_computation.14 | loop fusion | flops 1048576 | bytes 5242884 | tf_op jit(solution)/shard_map/add | solution.py:48
  116.0 1.3 copy-done.5
  117.4 1.9 collective-permute-start.1
  119.4 9.1 %collective-permute-done.1 = bf16[4,64,1024]{2,1,0:T(8,128)(2,1)S(1)} collective-permute-done((bf16[4,64,1024]{2,1,0:T(8,128)(2,1)S(1)}, bf16[4,64,1024]{2,1,0:T(8,128)(2,1)S(1)}, u32[]{:S(2)}, u32[]{:S(2)}) %collective-permute-start.1) | collective-permute-done | bytes 524320 | tf_op jit(solution)/shard_map/ppermute | solution.py:53
  128.5 1.4 bitcast_add_fusion.1
  129.9 1.0 copy-done.10
  130.8 0.7 fusion.14
  131.6 2.4 %collective-permute-start.2 = (bf16[2,64,1024]{2,1,0:T(8,128)(2,1)}, bf16[2,64,1024]{2,1,0:T(8,128)(2,1)S(1)}, u32[]{:S(2)}, u32[]{:S(2)}) collective-permute-start(bf16[2,64,1024]{2,1,0:T(8,128)(2,1)} %fusion.14), channel_id=1, source_target_pairs={{0,4},{1,13},{2,6},{3,7},{4,0},{5,9},{6,2},{7,3},{8,12},{9,5},{10,... | collective-permute-start | bytes 786440 | tf_op jit(solution)/shard_map/ppermute | solution.py:53
  134.0 11.3 %collective-permute-done.2 = bf16[2,64,1024]{2,1,0:T(8,128)(2,1)S(1)} collective-permute-done((bf16[2,64,1024]{2,1,0:T(8,128)(2,1)}, bf16[2,64,1024]{2,1,0:T(8,128)(2,1)S(1)}, u32[]{:S(2)}, u32[]{:S(2)}) %collective-permute-start.2) | collective-permute-done | bytes 262176 | tf_op jit(solution)/shard_map/ppermute | solution.py:53
  145.4 1.1 bitcast_add_fusion.2
  146.5 0.8 copy-done.11
  147.3 1.9 collective-permute-start.3
  149.2 8.8 %collective-permute-done.3 = bf16[1,64,1024]{2,1,0:T(8,128)(2,1)S(1)} collective-permute-done((bf16[1,64,1024]{2,1,0:T(8,128)(2,1)S(1)}, bf16[1,64,1024]{2,1,0:T(8,128)(2,1)S(1)}, u32[]{:S(2)}, u32[]{:S(2)}) %collective-permute-start.3) | collective-permute-done | bytes 131104 | tf_op jit(solution)/shard_map/ppermute | solution.py:53
  158.1 1.0 convert_add_fusion.1
  159.0 1.0 all_to_all.29
  160.0 20.1 %all_to_all.35 = f32[32,1,2048]{2,1,0:T(1,128)S(1)} all-to-all(f32[32,1,2048]{2,1,0:T(1,128)} %all_to_all.29), channel_id=1, replica_groups=mesh['group'=32,'member'=16] {'group'}, dimensions={0} | all-to-all | bytes 524288 | tf_op jit(solution)/shard_map/all_to_all | solution.py:56
  180.3 0.8 broadcast_in_dim.48
  181.2 5.7 %all-to-all-start.4 = ((f32[32,1,2048]{2,1,0:T(1,128)}), f32[32,1,2048]{2,1,0:T(1,128)S(1)}, u32[]{:S(2)}, u32[]{:S(2)}) async-start(f32[32,1,2048]{2,1,0:T(1,128)} %broadcast_in_dim.48), calls=%async_computation.4 | async-start | bytes 524288 | tf_op jit(solution)/shard_map/all_to_all | solution.py:57
  186.8 2.3 %convolution_convert_fusion = bf16[512,1024]{1,0:T(8,128)(2,1)} fusion(bf16[512,1024]{1,0:T(8,128)(2,1)S(1)} %copy-done.7, bf16[1024,1024]{1,0:T(8,128)(2,1)S(1)} %copy-done), kind=kOutput, calls=%fused_computation.23 | convolution fusion | flops 1074266112 | bytes 4194304 | tf_op jit(solution)/shard_map/dot_general | solution.py:143
  189.1 7.6 %all-to-all-done.4 = f32[32,1,2048]{2,1,0:T(1,128)S(1)} async-done(((f32[32,1,2048]{2,1,0:T(1,128)}), f32[32,1,2048]{2,1,0:T(1,128)S(1)}, u32[]{:S(2)}, u32[]{:S(2)}) %all-to-all-start.4) | async-done | bytes 262176 | tf_op jit(solution)/shard_map/all_to_all | solution.py:57
  196.7 0.7 multiply_reduce_fusion.1
  197.5 0.7 mul.65
  (55 shorter events, 5.5 us)
Async XLA Ops:
  0.6 12.8 %copy-start = (bf16[1024,1024]{1,0:T(8,128)(2,1)S(1)}, bf16[1024,1024]{1,0:T(8,128)(2,1)}, u32[]{:S(2)}) copy-start(bf16[1024,1024]{1,0:T(8,128)(2,1)} %param.8) | copy-start | bytes 6291460
  3.0 18.0 %all-to-all-start = ((s32[16,1,1]{2,1,0:T(1,128)}), s32[16,1,1]{2,1,0:T(1,128)S(1)}, u32[]{:S(2)}, u32[]{:S(2)}) async-start(s32[16,1,1]{2,1,0:T(1,128)} %copy.26), calls=%async_computation | async-start | bytes 16384 | tf_op jit(solution)/shard_map/all_to_all | solution.py:82
  17.2 17.4 %copy-start.9 = (bf16[512,1024]{1,0:T(8,128)(2,1)}, bf16[512,1024]{1,0:T(8,128)(2,1)S(1)}, u32[]{:S(2)}) copy-start(bf16[512,1024]{1,0:T(8,128)(2,1)S(1)} %get-tuple-element.9) | copy-start | bytes 3145732
  21.3 6.0 %copy-start.15 = (s32[512,16]{0,1:T(8,128)S(1)}, s32[512,16]{0,1:T(8,128)}, u32[]{:S(2)}) copy-start(s32[512,16]{0,1:T(8,128)} %param.12) | copy-start | bytes 98308
  21.3 6.4 %copy-start.16 = (s32[512,16]{0,1:T(8,128)S(1)}, s32[512,16]{0,1:T(8,128)}, u32[]{:S(2)}) copy-start(s32[512,16]{0,1:T(8,128)} %param.11) | copy-start | bytes 98308
  22.9 30.9 %all-to-all-start.1 = ((bf16[16,32,1024]{2,1,0:T(8,128)(2,1)}), bf16[16,32,1024]{2,1,0:T(8,128)(2,1)}, u32[]{:S(2)}, u32[]{:S(2)}) async-start(bf16[16,32,1024]{2,1,0:T(8,128)(2,1)} %gather_fusion), calls=%async_computation.1 | async-start | bytes 2097152 | tf_op jit(solution)/shard_map/all_to_all | solution.py:86
  34.6 1.0 copy-start.12
  53.8 3.4 %copy-start.3 = (bf16[512,1024]{1,0:T(8,128)(2,1)S(1)}, bf16[512,1024]{1,0:T(8,128)(2,1)}, u32[]{:S(2)}) copy-start(bf16[512,1024]{1,0:T(8,128)(2,1)} %param.13) | copy-start | bytes 3145732
  57.2 1.3 copy-start.1
  57.7 1.5 copy-start.13
  59.2 1.7 copy-start.8
  60.9 31.4 %all-to-all-start.2 = ((bf16[16,32,1024]{2,1,0:T(8,128)(2,1)}), bf16[16,32,1024]{2,1,0:T(8,128)(2,1)}, u32[]{:S(2)}, u32[]{:S(2)}) async-start(bf16[16,32,1024]{2,1,0:T(8,128)(2,1)} %bitcast.57), calls=%async_computation.2 | async-start | bytes 2097152 | tf_op jit(solution)/shard_map/all_to_all | solution.py:125
  92.3 2.0 copy-start.4
  96.2 2.8 %copy-start.17 = (f32[1024]{0:T(1024)S(1)}, f32[1024]{0:T(1024)}, u32[]{:S(2)}) copy-start(f32[1024]{0:T(1024)} %param.9) | copy-start | bytes 12292
  99.0 4.7 %copy-start.14 = (bf16[512,1024]{1,0:T(8,128)(2,1)S(1)}, bf16[512,1024]{1,0:T(8,128)(2,1)}, u32[]{:S(2)}) copy-start(bf16[512,1024]{1,0:T(8,128)(2,1)} %param.7) | copy-start | bytes 3145732
  103.6 1.4 copy-start.6
  105.0 1.9 copy-start.2
  107.1 6.2 %collective-permute-start = (bf16[8,64,1024]{2,1,0:T(8,128)(2,1)S(1)}, bf16[8,64,1024]{2,1,0:T(8,128)(2,1)}, u32[]{:S(2)}, u32[]{:S(2)}) collective-permute-start(bf16[8,64,1024]{2,1,0:T(8,128)(2,1)S(1)} %fusion.6), channel_id=1, source_target_pairs={{0,1},{1,0},{2,3},{3,2},{4,5},{5,4},{6,7},{7,6},{8,9},{9,8},{10,11... | collective-permute-start | bytes 3145736 | tf_op jit(solution)/shard_map/ppermute | solution.py:47
  116.0 1.3 copy-start.5
  117.4 11.1 %collective-permute-start.1 = (bf16[4,64,1024]{2,1,0:T(8,128)(2,1)S(1)}, bf16[4,64,1024]{2,1,0:T(8,128)(2,1)S(1)}, u32[]{:S(2)}, u32[]{:S(2)}) collective-permute-start(bf16[4,64,1024]{2,1,0:T(8,128)(2,1)S(1)} %fusion.7), channel_id=1, source_target_pairs={{0,2},{1,15},{2,0},{3,5},{4,6},{5,3},{6,4},{7,9},{8,10},{9,7},{10,... | collective-permute-start | bytes 1572872 | tf_op jit(solution)/shard_map/ppermute | solution.py:53
  129.9 1.0 copy-start.10
  131.6 13.8 %collective-permute-start.2 = (bf16[2,64,1024]{2,1,0:T(8,128)(2,1)}, bf16[2,64,1024]{2,1,0:T(8,128)(2,1)S(1)}, u32[]{:S(2)}, u32[]{:S(2)}) collective-permute-start(bf16[2,64,1024]{2,1,0:T(8,128)(2,1)} %fusion.14), channel_id=1, source_target_pairs={{0,4},{1,13},{2,6},{3,7},{4,0},{5,9},{6,2},{7,3},{8,12},{9,5},{10,... | collective-permute-start | bytes 786440 | tf_op jit(solution)/shard_map/ppermute | solution.py:53
  134.0 52.8 %copy-start.7 = (bf16[512,1024]{1,0:T(8,128)(2,1)S(1)}, bf16[512,1024]{1,0:T(8,128)(2,1)}, u32[]{:S(2)}) copy-start(bf16[512,1024]{1,0:T(8,128)(2,1)} %copy-done.6) | copy-start | bytes 3145732
  146.5 0.8 copy-start.11
  147.3 10.8 %collective-permute-start.3 = (bf16[1,64,1024]{2,1,0:T(8,128)(2,1)S(1)}, bf16[1,64,1024]{2,1,0:T(8,128)(2,1)S(1)}, u32[]{:S(2)}, u32[]{:S(2)}) collective-permute-start(bf16[1,64,1024]{2,1,0:T(8,128)(2,1)S(1)} %dynamic-slice_convert_fusion.2), channel_id=1, source_target_pairs={{0,8},{1,9},{2,10},{3,11},{4,12},{5,13},{6,14},{7,15},{8,0},{9,1},... | collective-permute-start | bytes 393224 | tf_op jit(solution)/shard_map/ppermute | solution.py:53
  181.2 15.6 %all-to-all-start.4 = ((f32[32,1,2048]{2,1,0:T(1,128)}), f32[32,1,2048]{2,1,0:T(1,128)S(1)}, u32[]{:S(2)}, u32[]{:S(2)}) async-start(f32[32,1,2048]{2,1,0:T(1,128)} %broadcast_in_dim.48), calls=%async_computation.4 | async-start | bytes 524288 | tf_op jit(solution)/shard_map/all_to_all | solution.py:57

commit v6 on v5

--- a/solution.py
+++ b/solution.py
@@ -18,40 +18,23 @@
     return [(i, i ^ (1 << bit)) for i in range(n)]
 
 
-def shifted_pairs(members, bit):
-    chips = members // 2
-    pairs = []
-    for m in range(members):
-        chip, core = divmod(m, 2)
-        label = ((chip - core) % chips) ^ (1 << bit)
-        pairs.append((m, 2 * ((label + core) % chips) + core))
-    return pairs
-
-
-def halve(acc, bit):
-    pairs = acc.reshape(acc.shape[0] // 2, 2, *acc.shape[1:])
-    keep = lax.dynamic_index_in_dim(pairs, bit, 1, keepdims=False)
-    send = lax.dynamic_index_in_dim(pairs, 1 - bit, 1, keepdims=False)
-    return keep, send
-
-
 def reduce_rows(part):
     members = lax.axis_size("member")
     groups = lax.axis_size("group")
-    member_here = lax.axis_index("member")
-    chips = members // 2
-    chip, core = member_here // 2, member_here % 2
+    core = lax.axis_index("member") % 2
     rows, cols = part.shape
-    acc = part.reshape(members, rows // members, cols)
-    keep, send = halve(acc, core)
-    sent = lax.ppermute(send.astype(jnp.bfloat16), "member", xor_pairs(members, 0))
-    acc = keep + sent.astype(jnp.float32)
-    acc = lax.dynamic_slice_in_dim(jnp.concatenate([acc, acc], axis=0), core, chips, 0)
-    label = (chip - core) % chips
-    for k in range(chips.bit_length() - 1):
-        keep, send = halve(acc, (label >> k) & 1)
-        sent = lax.ppermute(send.astype(jnp.bfloat16), "member", shifted_pairs(members, k))
-        acc = keep + sent.astype(jnp.float32)
+    halves = part.reshape(rows, 2, cols // 2)
+    keep = lax.dynamic_index_in_dim(halves, core, 1, keepdims=False)
+    send = lax.dynamic_index_in_dim(halves, 1 - core, 1, keepdims=False)
+    pair_sum = keep + lax.ppermute(send.astype(jnp.bfloat16), "member", xor_pairs(members, 0)).astype(
+        jnp.float32
+    )
+    to_members = pair_sum.astype(jnp.bfloat16).reshape(members, rows // members, cols // 2)
+    from_members = lax.all_to_all(to_members, "member", split_axis=0, concat_axis=0, tiled=True)
+    by_half = jnp.sum(
+        from_members.astype(jnp.float32).reshape(members // 2, 2, rows // members, cols // 2), axis=0
+    )
+    acc = jnp.transpose(by_half, (1, 0, 2)).reshape(rows // members, cols)
     slices = acc.reshape(groups, -1)
     mine = jnp.sum(lax.all_to_all(slices, "group", split_axis=0, concat_axis=0, tiled=True), axis=0)
     every = lax.all_to_all(

time: 201 us -> 197 us (0.980)
  blocking collectives: 20.1 us -> 52.5 us
  waiting for transfers between devices: 78.9 us -> 49.4 us
  starting transfers between devices: 35.5 us -> 29.2 us
  other arithmetic: 20.2 us -> 16.1 us
  local copies, waits for them, and re-layouts: 21.5 us -> 25.3 us
    all_to_all x0 -> x1, blocking collectives: none -> 30.2 us  [reduce_rows(): lax.all_to_all(to_members, 'member', split_axis=0, concat_axis=0, tiled=T...]
    ppermute x3 -> x0, waiting for transfers between devices: 29.3 us -> none  [reduce_rows(): lax.ppermute(send.astype(jnp.bfloat16), 'member', shifted_pairs(members, k))]
    dynamic_slice x0 -> x3, local copies, waits for them, and re-layouts: none -> 6.27 us  [the longest x2 6.12 us: reduce_rows(): keep = lax.dynamic_index_in_dim(halves, core, 1, keepdims=False)]
    ppermute x3 -> x0, starting transfers between devices: 6.26 us -> none  [reduce_rows(): lax.ppermute(send.astype(jnp.bfloat16), 'member', shifted_pairs(members, k))]
    add x4 -> x0, other arithmetic: 5.64 us -> none  [reduce_rows(): acc = keep + sent.astype(jnp.float32)]
    all_to_all x1, blocking collectives: 20.1 us -> 22.4 us  [reduce_rows(): lax.all_to_all(slices, 'group', split_axis=0, concat_axis=0, tiled=True)]
    ppermute x1, waiting for transfers between devices: 2.17 us -> 0.01 us  [reduce_rows(): lax.ppermute(send.astype(jnp.bfloat16), 'member', xor_pairs(members, 0))]
    unnamed x37 -> x32, local copies, waits for them, and re-layouts: 8.91 us -> 7.17 us
  transfers between devices with their start and end apart: 8 -> 5, of which waited for: 8 -> 4; matrix products, arithmetic and copies ran while one was open for 11% -> 14% of each run, Pallas kernels for 0% -> 0%
where the time goes in v6:
time: 197 us; the launch traced here: 194 us
  blocking collectives  52.5 us (27%)
  waiting for transfers between devices  49.4 us (25%)
  starting transfers between devices  29.2 us (15%)
  local copies, waits for them, and re-layouts  25.3 us (13%)
  matrix products  20.9 us (11%)
  other arithmetic  16.1 us (8%)
    all_to_all x1, blocking collectives, reduce_rows(): lax.all_to_all(to_members, 'member', split_axis=0, concat_axis=0, tiled=T...  30.2 us
    all_to_all x1, blocking collectives, reduce_rows(): lax.all_to_all(slices, 'group', split_axis=0, concat_axis=0, tiled=True)  22.4 us
    all_to_all x1, waiting for transfers between devices, on_device(): lax.all_to_all(returned, 'member', split_axis=0, concat_axis=0, tiled=True)  19.9 us
    all_to_all x1, waiting for transfers between devices, on_device(): lax.all_to_all(own_tiles[served], 'member', split_axis=0, concat_axis=0,...  16.2 us
    all_to_all x1, starting transfers between devices, on_device(): lax.all_to_all(wanted.reshape(members, 1), 'member', split_axis=0, concat...  10.4 us
    all_to_all x1, waiting for transfers between devices, reduce_rows(): lax.all_to_all(jnp.broadcast_to(mine, slices.shape), 'group', split_axis=...  9.61 us
    unnamed x32, local copies, waits for them, and re-layouts  7.17 us
    dynamic_slice x2, local copies, waits for them, and re-layouts, reduce_rows(): keep = lax.dynamic_index_in_dim(halves, core, 1, keepdims=False)  6.12 us
  transfers between devices with their start and end apart: 5, of which 4 were waited for; matrix products, arithmetic and copies ran while one was open for 14% of the time, Pallas kernels for 0%

profile of v6, /device:TPU:6, one launch (start us, length us, event | category | flops | bytes accessed | tf_op | source)
XLA Modules:
  0.0 194.4 jit_solution(10532418287168690459)
XLA Ops:
  0.6 0.8 broadcast_compare_fusion
  1.5 0.7 add_select_fusion
  2.3 0.7 copy.32
  3.0 10.4 %all-to-all-start = ((s32[16,1,1]{2,1,0:T(1,128)}), s32[16,1,1]{2,1,0:T(1,128)S(1)}, u32[]{:S(2)}, u32[]{:S(2)}) async-start(s32[16,1,1]{2,1,0:T(1,128)} %copy.32), calls=%async_computation | async-start | bytes 16384 | tf_op jit(solution)/shard_map/all_to_all | solution.py:65
  13.4 3.8 %maximum_convert_fusion = (bf16[512,1024]{1,0:T(8,128)(2,1)S(1)}, f32[512,1024]{1,0:T(8,128)}) fusion(f32[1024]{0:T(1024)} %param.9, bf16[512,1024]{1,0:T(8,128)(2,1)} %param.7, bf16[1024,1024]{1,0:T(8,128)(2,1)S(1)} %copy-done), kind=kOutput, calls=%fused_computation.17 | convolution fusion | flops 1075314688 | bytes 6295552 | tf_op jit(solution)/shard_map/dot_general | solution.py:56
  17.2 3.7 %all-to-all-done = s32[16,1,1]{2,1,0:T(1,128)S(1)} async-done(((s32[16,1,1]{2,1,0:T(1,128)}), s32[16,1,1]{2,1,0:T(1,128)S(1)}, u32[]{:S(2)}, u32[]{:S(2)}) %all-to-all-start) | async-done | bytes 96 | tf_op jit(solution)/shard_map/all_to_all | solution.py:65
  20.9 0.4 clamp_reduce_fusion
  21.3 1.6 gather_fusion
  22.9 4.4 %all-to-all-start.1 = ((bf16[16,32,1024]{2,1,0:T(8,128)(2,1)}), bf16[16,32,1024]{2,1,0:T(8,128)(2,1)}, u32[]{:S(2)}, u32[]{:S(2)}) async-start(bf16[16,32,1024]{2,1,0:T(8,128)(2,1)} %gather_fusion), calls=%async_computation.1 | async-start | bytes 2097152 | tf_op jit(solution)/shard_map/all_to_all | solution.py:69
  27.7 0.8 copy.37
  28.5 5.1 %select_reduce_fusion = s32[4,128,256]{2,1,0:T(8,128)S(1)} fusion(s32[4,128,16]{2,1,0:T(8,128)S(1)} %bitcast.51, s32[4,128,16]{2,1,0:T(8,128)} %bitcast.52), kind=kLoop, calls=%fused_computation.2 | loop fusion | flops 6160384 | bytes 589824 | tf_op jit(solution)/shard_map/reduce_sum | solution.py:14
  33.6 1.0 fusion.5
  34.6 1.0 copy-done.9
  35.6 2.0 %fusion.10 = f32[512,1024]{1,0:T(8,128)} fusion(bf16[512,1024]{1,0:T(8,128)(2,1)S(1)} %get-tuple-element.9, bf16[512,1024]{1,0:T(8,128)(2,1)S(1)} %bitcast.44), kind=kOutput, calls=%fused_computation.28 | convolution fusion | flops 536870912 | bytes 3670016 | tf_op jit(solution)/shard_map/dot_general | solution.py:87
  37.7 16.2 %all-to-all-done.1 = bf16[16,32,1024]{2,1,0:T(8,128)(2,1)} async-done(((bf16[16,32,1024]{2,1,0:T(8,128)(2,1)}), bf16[16,32,1024]{2,1,0:T(8,128)(2,1)}, u32[]{:S(2)}, u32[]{:S(2)}) %all-to-all-start.1) | async-done | bytes 1048608 | tf_op jit(solution)/shard_map/all_to_all | solution.py:69
  53.8 3.4 %multiply_reduce_fusion = (f32[512]{0:T(512)S(1)}, f32[512,1024]{1,0:T(8,128)S(1)}) fusion(bf16[512,1024]{1,0:T(8,128)(2,1)} %copy-done.8, f32[512]{0:T(512)S(1)} %convert_element_type.65, f32[512,1024]{1,0:T(8,128)} %fusion.10, bf16[512,1024]{1,0:T(8,128)(2,1)} %bitcast.6, bf16[512,1024]{1,0:T(8,128)(2,1)} %bitcast.45), kind=kOutput, calls=%fused_computation.15 | convolution fusion | flops 540016128 | bytes 6819840 | tf_op jit(solution)/shard_map/dot_general | solution.py:89
  57.3 0.5 fusion.1
  57.8 0.5 divide_convert_fusion
  58.3 0.2 copy-done.1
  58.5 0.7 copy-done.10
  59.2 1.7 convolution_convert_fusion.1
  60.9 4.9 %all-to-all-start.2 = ((bf16[16,32,1024]{2,1,0:T(8,128)(2,1)}), bf16[16,32,1024]{2,1,0:T(8,128)(2,1)}, u32[]{:S(2)}, u32[]{:S(2)}) async-start(bf16[16,32,1024]{2,1,0:T(8,128)(2,1)} %bitcast.49), calls=%async_computation.2 | async-start | bytes 2097152 | tf_op jit(solution)/shard_map/all_to_all | solution.py:108
  65.8 0.4 compare_reduce_fusion
  66.2 3.5 %fusion.8 = f32[512,1024]{1,0:T(8,128)} fusion(bf16[512,1024]{1,0:T(8,128)(2,1)} %copy-done.7, bf16[512,1024]{1,0:T(8,128)(2,1)} %bitcast.46), kind=kOutput, calls=%fused_computation.26 | convolution fusion | flops 536870912 | bytes 3670016 | tf_op jit(solution)/shard_map/dot_general | solution.py:109
  69.7 2.8 %reshape.171 = f32[16,32768]{1,0:T(8,128)} reshape(f32[512,1024]{1,0:T(8,128)} %fusion.8) | data formatting | bytes 4194304 | tf_op jit(solution)/shard_map/reshape | solution.py:116
  72.4 19.9 %all-to-all-done.2 = bf16[16,32,1024]{2,1,0:T(8,128)(2,1)} async-done(((bf16[16,32,1024]{2,1,0:T(8,128)(2,1)}), bf16[16,32,1024]{2,1,0:T(8,128)(2,1)}, u32[]{:S(2)}, u32[]{:S(2)}) %all-to-all-start.2) | async-done | bytes 1048608 | tf_op jit(solution)/shard_map/all_to_all | solution.py:108
  92.4 2.0 %copy.40 = bf16[2,8,32,1024]{3,1,2,0:T(8,128)(2,1)S(1)} copy(bf16[2,8,32,1024]{3,2,1,0:T(8,128)(2,1)} %bitcast.18) | data formatting | bytes 2097152
  94.3 1.9 convolution_add_fusion
  96.2 2.8 %reshape.174 = f32[512,1024]{1,0:T(8,128)} reshape(f32[16,32768]{1,0:T(8,128)} %convolution_add_fusion) | data formatting | bytes 4194304 | tf_op jit(solution)/shard_map/reshape | solution.py:122
  99.0 4.6 %select_convert_fusion = (bf16[512,1024]{1,0:T(8,128)(2,1)S(1)}, bf16[512,1024]{1,0:T(8,128)(2,1)}) fusion(f32[512,1024]{1,0:T(8,128)} %reshape.174, f32[512,1024]{1,0:T(8,128)} %get-tuple-element.10, f32[512,1024]{1,0:T(8,128)} %copy-done.1, bf16[512,1024]{1,0:T(8,128)(2,1)S(1)} %copy-done.3, f32[512]{0:T(512)S(1)} %broadcast_multiply_fusion, ...), kind=kLoop, calls=%fused_computation.13 | loop fusion | flops 5767168 | bytes 9445376 | tf_op jit(solution)/shard_map/convert_element_type | solution.py:125
  103.6 1.3 fusion.20
  105.0 1.9 copy-done.2
  107.0 1.4 copy.39
  108.4 3.9 %collective-permute-start = (bf16[1024,512]{1,0:T(8,128)(2,1)}, bf16[1024,512]{1,0:T(8,128)(2,1)S(1)}, u32[]{:S(2)}, u32[]{:S(2)}) collective-permute-start(bf16[1024,512]{1,0:T(8,128)(2,1)} %bitcast.50), channel_id=1, source_target_pairs={{0,1},{1,0},{2,3},{3,2},{4,5},{5,4},{6,7},{7,6},{8,9},{9,8},{10,11... | collective-permute-start | bytes 3145736 | tf_op jit(solution)/shard_map/ppermute | solution.py:29
  112.3 3.2 %constant_dynamic-slice_fusion.1 = f32[1024,1,512]{0,2,1:T(8,128)} fusion(f32[1024,2,512]{0,2,1:T(8,128)} %bitcast.39, s32[]{:T(128)S(6)} %select_n.58), kind=kLoop, calls=%fused_computation.58 | loop fusion | bytes 4194308 | tf_op jit(solution)/shard_map/jit(dynamic_index_in_dim)/dynamic_slice | solution.py:27
  115.5 2.9 %copy.33 = f32[1024,1,512]{2,0,1:T(8,128)} copy(f32[1024,1,512]{0,2,1:T(8,128)} %constant_dynamic-slice_fusion.1) | data formatting | bytes 4194304 | tf_op jit(solution)/shard_map/jit(dynamic_index_in_dim)/dynamic_slice | solution.py:27
  118.5 1.9 fusion.3
  120.4 30.2 %all_to_all.40 = bf16[16,64,512]{2,1,0:T(8,128)(2,1)S(1)} all-to-all(bf16[16,64,512]{2,1,0:T(8,128)(2,1)S(1)} %bitcast.43), channel_id=1, replica_groups=mesh['group'=32,'member'=16] {'member'}, dimensions={0} | all-to-all | bytes 2097152 | tf_op jit(solution)/shard_map/all_to_all | solution.py:33
  150.7 0.2 copy.35
  150.9 1.1 all_to_all.33
  152.0 22.4 %all_to_all.41 = f32[32,1,2048]{2,1,0:T(1,128)S(1)} all-to-all(f32[32,1,2048]{2,1,0:T(1,128)} %all_to_all.33), channel_id=1, replica_groups=mesh['group'=32,'member'=16] {'group'}, dimensions={0} | all-to-all | bytes 524288 | tf_op jit(solution)/shard_map/all_to_all | solution.py:39
  174.4 0.2 reduce_sum.59
  174.6 0.8 broadcast_in_dim.48
  175.4 5.6 %all-to-all-start.5 = ((f32[32,1,2048]{2,1,0:T(1,128)}), f32[32,1,2048]{2,1,0:T(1,128)S(1)}, u32[]{:S(2)}, u32[]{:S(2)}) async-start(f32[32,1,2048]{2,1,0:T(1,128)} %broadcast_in_dim.48), calls=%async_computation.5 | async-start | bytes 524288 | tf_op jit(solution)/shard_map/all_to_all | solution.py:40
  181.0 2.3 %convolution_convert_fusion = bf16[512,1024]{1,0:T(8,128)(2,1)} fusion(bf16[512,1024]{1,0:T(8,128)(2,1)S(1)} %copy-done.6, bf16[1024,1024]{1,0:T(8,128)(2,1)S(1)} %copy-done), kind=kOutput, calls=%fused_computation.21 | convolution fusion | flops 1074266112 | bytes 4194304 | tf_op jit(solution)/shard_map/dot_general | solution.py:126
  183.3 9.6 %all-to-all-done.5 = f32[32,1,2048]{2,1,0:T(1,128)S(1)} async-done(((f32[32,1,2048]{2,1,0:T(1,128)}), f32[32,1,2048]{2,1,0:T(1,128)S(1)}, u32[]{:S(2)}, u32[]{:S(2)}) %all-to-all-start.5) | async-done | bytes 262176 | tf_op jit(solution)/shard_map/all_to_all | solution.py:40
  192.9 0.7 multiply_reduce_fusion.1
  193.6 0.7 mul.65
  (42 shorter events, 0.9 us)
Async XLA Ops:
  0.6 12.8 %copy-start = (bf16[1024,1024]{1,0:T(8,128)(2,1)S(1)}, bf16[1024,1024]{1,0:T(8,128)(2,1)}, u32[]{:S(2)}) copy-start(bf16[1024,1024]{1,0:T(8,128)(2,1)} %param.8) | copy-start | bytes 6291460
  3.0 18.0 %all-to-all-start = ((s32[16,1,1]{2,1,0:T(1,128)}), s32[16,1,1]{2,1,0:T(1,128)S(1)}, u32[]{:S(2)}, u32[]{:S(2)}) async-start(s32[16,1,1]{2,1,0:T(1,128)} %copy.32), calls=%async_computation | async-start | bytes 16384 | tf_op jit(solution)/shard_map/all_to_all | solution.py:65
  17.2 17.4 %copy-start.8 = (bf16[512,1024]{1,0:T(8,128)(2,1)}, bf16[512,1024]{1,0:T(8,128)(2,1)S(1)}, u32[]{:S(2)}) copy-start(bf16[512,1024]{1,0:T(8,128)(2,1)S(1)} %get-tuple-element.9) | copy-start | bytes 3145732
  21.3 6.0 %copy-start.12 = (s32[512,16]{0,1:T(8,128)S(1)}, s32[512,16]{0,1:T(8,128)}, u32[]{:S(2)}) copy-start(s32[512,16]{0,1:T(8,128)} %param.12) | copy-start | bytes 98308
  21.3 6.4 %copy-start.13 = (s32[512,16]{0,1:T(8,128)S(1)}, s32[512,16]{0,1:T(8,128)}, u32[]{:S(2)}) copy-start(s32[512,16]{0,1:T(8,128)} %param.11) | copy-start | bytes 98308
  22.9 30.9 %all-to-all-start.1 = ((bf16[16,32,1024]{2,1,0:T(8,128)(2,1)}), bf16[16,32,1024]{2,1,0:T(8,128)(2,1)}, u32[]{:S(2)}, u32[]{:S(2)}) async-start(bf16[16,32,1024]{2,1,0:T(8,128)(2,1)} %gather_fusion), calls=%async_computation.1 | async-start | bytes 2097152 | tf_op jit(solution)/shard_map/all_to_all | solution.py:69
  34.6 1.0 copy-start.9
  53.8 3.4 %copy-start.3 = (bf16[512,1024]{1,0:T(8,128)(2,1)S(1)}, bf16[512,1024]{1,0:T(8,128)(2,1)}, u32[]{:S(2)}) copy-start(bf16[512,1024]{1,0:T(8,128)(2,1)} %param.13) | copy-start | bytes 3145732
  57.2 1.3 copy-start.1
  57.7 1.5 copy-start.10
  59.2 1.7 copy-start.7
  60.9 31.4 %all-to-all-start.2 = ((bf16[16,32,1024]{2,1,0:T(8,128)(2,1)}), bf16[16,32,1024]{2,1,0:T(8,128)(2,1)}, u32[]{:S(2)}, u32[]{:S(2)}) async-start(bf16[16,32,1024]{2,1,0:T(8,128)(2,1)} %bitcast.49), calls=%async_computation.2 | async-start | bytes 2097152 | tf_op jit(solution)/shard_map/all_to_all | solution.py:108
  92.4 2.0 %copy-start.4 = (f32[16,32768]{1,0:T(8,128)S(1)}, f32[16,32768]{1,0:T(8,128)}, u32[]{:S(2)}) copy-start(f32[16,32768]{1,0:T(8,128)} %reshape.171) | copy-start | bytes 6291460
  96.2 2.8 %copy-start.14 = (f32[1024]{0:T(1024)S(1)}, f32[1024]{0:T(1024)}, u32[]{:S(2)}) copy-start(f32[1024]{0:T(1024)} %param.9) | copy-start | bytes 12292
  99.0 4.7 %copy-start.11 = (bf16[512,1024]{1,0:T(8,128)(2,1)S(1)}, bf16[512,1024]{1,0:T(8,128)(2,1)}, u32[]{:S(2)}) copy-start(bf16[512,1024]{1,0:T(8,128)(2,1)} %param.7) | copy-start | bytes 3145732
  103.6 1.3 copy-start.5
  104.9 1.9 copy-start.2
  108.4 10.1 %collective-permute-start = (bf16[1024,512]{1,0:T(8,128)(2,1)}, bf16[1024,512]{1,0:T(8,128)(2,1)S(1)}, u32[]{:S(2)}, u32[]{:S(2)}) collective-permute-start(bf16[1024,512]{1,0:T(8,128)(2,1)} %bitcast.50), channel_id=1, source_target_pairs={{0,1},{1,0},{2,3},{3,2},{4,5},{5,4},{6,7},{7,6},{8,9},{9,8},{10,11... | collective-permute-start | bytes 3145736 | tf_op jit(solution)/shard_map/ppermute | solution.py:29
  150.6 30.5 %copy-start.6 = (bf16[512,1024]{1,0:T(8,128)(2,1)S(1)}, bf16[512,1024]{1,0:T(8,128)(2,1)}, u32[]{:S(2)}) copy-start(bf16[512,1024]{1,0:T(8,128)(2,1)} %copy-done.5) | copy-start | bytes 3145732
  175.4 17.5 %all-to-all-start.5 = ((f32[32,1,2048]{2,1,0:T(1,128)}), f32[32,1,2048]{2,1,0:T(1,128)S(1)}, u32[]{:S(2)}, u32[]{:S(2)}) async-start(f32[32,1,2048]{2,1,0:T(1,128)} %broadcast_in_dim.48), calls=%async_computation.5 | async-start | bytes 524288 | tf_op jit(solution)/shard_map/all_to_all | solution.py:40

commit v7 on v6

--- a/solution.py
+++ b/solution.py
@@ -29,16 +29,17 @@
     pair_sum = keep + lax.ppermute(send.astype(jnp.bfloat16), "member", xor_pairs(members, 0)).astype(
         jnp.float32
     )
-    to_members = pair_sum.astype(jnp.bfloat16).reshape(members, rows // members, cols // 2)
-    from_members = lax.all_to_all(to_members, "member", split_axis=0, concat_axis=0, tiled=True)
+    block = rows // members
+    share = block // groups
+    chunks = pair_sum.astype(jnp.bfloat16).reshape(members, groups, share, cols // 2)
+    chunks = jnp.transpose(chunks, (1, 0, 2, 3)).reshape(groups * members, share, cols // 2)
+    got = lax.all_to_all(chunks, ("group", "member"), split_axis=0, concat_axis=0, tiled=True)
     by_half = jnp.sum(
-        from_members.astype(jnp.float32).reshape(members // 2, 2, rows // members, cols // 2), axis=0
+        got.astype(jnp.float32).reshape(groups * members // 2, 2, share, cols // 2), axis=0
     )
-    acc = jnp.transpose(by_half, (1, 0, 2)).reshape(rows // members, cols)
-    slices = acc.reshape(groups, -1)
-    mine = jnp.sum(lax.all_to_all(slices, "group", split_axis=0, concat_axis=0, tiled=True), axis=0)
+    mine = jnp.transpose(by_half, (1, 0, 2)).reshape(share * cols)
     every = lax.all_to_all(
-        jnp.broadcast_to(mine, slices.shape), "group", split_axis=0, concat_axis=0, tiled=True
+        jnp.broadcast_to(mine, (groups, share * cols)), "group", split_axis=0, concat_axis=0, tiled=True
     )
     return every.reshape(rows // members, cols)
 

time: 197 us -> 193 us (0.980)
  blocking collectives: 52.5 us -> 45.5 us
    all_to_all x2 -> x1, blocking collectives: 52.5 us -> 45.5 us  [reduce_rows(): lax.all_to_all(chunks, ('group', 'member'), split_axis=0, concat_axis=0,...]
    reshape x0 -> x2, local copies, waits for them, and re-layouts: none -> 2.55 us  [the longest x1 1.47 us: reduce_rows(): pair_sum.astype(jnp.bfloat16).reshape(members, groups, share, cols // 2)]
    unnamed x32 -> x33, local copies, waits for them, and re-layouts: 7.17 us -> 7.17 us
  transfers between devices with their start and end apart: 5 -> 5, of which waited for: 4 -> 4; matrix products, arithmetic and copies ran while one was open for 14% -> 15% of each run, Pallas kernels for 0% -> 0%
where the time goes in v7:
time: 193 us; the launch traced here: 191 us
  waiting for transfers between devices  49.4 us (26%)
  blocking collectives  45.5 us (24%)
  starting transfers between devices  29.3 us (15%)
  local copies, waits for them, and re-layouts  27.1 us (14%)
  matrix products  20.9 us (11%)
  other arithmetic  17.7 us (9%)
    all_to_all x1, blocking collectives, reduce_rows(): lax.all_to_all(chunks, ('group', 'member'), split_axis=0, concat_axis=0,...  45.5 us
    all_to_all x1, waiting for transfers between devices, on_device(): lax.all_to_all(returned, 'member', split_axis=0, concat_axis=0, tiled=True)  19.9 us
    all_to_all x1, waiting for transfers between devices, on_device(): lax.all_to_all(own_tiles[served], 'member', split_axis=0, concat_axis=0,...  16.2 us
    all_to_all x1, starting transfers between devices, on_device(): lax.all_to_all(wanted.reshape(members, 1), 'member', split_axis=0, concat...  10.4 us
    all_to_all x1, waiting for transfers between devices, reduce_rows(): lax.all_to_all(jnp.broadcast_to(mine, (groups, share * cols)), 'group', s...  9.63 us
    unnamed x33, local copies, waits for them, and re-layouts  7.17 us
    dynamic_slice x2, local copies, waits for them, and re-layouts, reduce_rows(): keep = lax.dynamic_index_in_dim(halves, core, 1, keepdims=False)  6.09 us
    all_to_all x1, starting transfers between devices, reduce_rows(): lax.all_to_all(jnp.broadcast_to(mine, (groups, share * cols)), 'group', s...  5.74 us
  transfers between devices with their start and end apart: 5, of which 4 were waited for; matrix products, arithmetic and copies ran while one was open for 15% of the time, Pallas kernels for 0%

profile of v7, /device:TPU:6, one launch (start us, length us, event | category | flops | bytes accessed | tf_op | source)
XLA Modules:
  0.0 190.9 jit_solution(7701213344558482724)
XLA Ops:
  0.6 0.8 broadcast_compare_fusion
  1.5 0.7 add_select_fusion
  2.3 0.7 copy.41
  3.0 10.4 %all-to-all-start = ((s32[16,1,1]{2,1,0:T(1,128)}), s32[16,1,1]{2,1,0:T(1,128)S(1)}, u32[]{:S(2)}, u32[]{:S(2)}) async-start(s32[16,1,1]{2,1,0:T(1,128)} %copy.41), calls=%async_computation | async-start | bytes 16384 | tf_op jit(solution)/shard_map/all_to_all | solution.py:66
  13.4 3.8 %maximum_convert_fusion = (bf16[512,1024]{1,0:T(8,128)(2,1)S(1)}, f32[512,1024]{1,0:T(8,128)}) fusion(f32[1024]{0:T(1024)} %param.9, bf16[512,1024]{1,0:T(8,128)(2,1)} %param.7, bf16[1024,1024]{1,0:T(8,128)(2,1)S(1)} %copy-done), kind=kOutput, calls=%fused_computation.17 | convolution fusion | flops 1075314688 | bytes 6295552 | tf_op jit(solution)/shard_map/dot_general | solution.py:57
  17.2 3.7 %all-to-all-done = s32[16,1,1]{2,1,0:T(1,128)S(1)} async-done(((s32[16,1,1]{2,1,0:T(1,128)}), s32[16,1,1]{2,1,0:T(1,128)S(1)}, u32[]{:S(2)}, u32[]{:S(2)}) %all-to-all-start) | async-done | bytes 96 | tf_op jit(solution)/shard_map/all_to_all | solution.py:66
  20.9 0.4 clamp_reduce_fusion
  21.3 1.6 gather_fusion
  22.9 4.3 %all-to-all-start.1 = ((bf16[16,32,1024]{2,1,0:T(8,128)(2,1)}), bf16[16,32,1024]{2,1,0:T(8,128)(2,1)}, u32[]{:S(2)}, u32[]{:S(2)}) async-start(bf16[16,32,1024]{2,1,0:T(8,128)(2,1)} %gather_fusion), calls=%async_computation.1 | async-start | bytes 2097152 | tf_op jit(solution)/shard_map/all_to_all | solution.py:70
  27.7 0.8 copy.47
  28.5 5.1 %select_reduce_fusion = s32[4,128,256]{2,1,0:T(8,128)S(1)} fusion(s32[4,128,16]{2,1,0:T(8,128)S(1)} %bitcast.56, s32[4,128,16]{2,1,0:T(8,128)} %bitcast.57), kind=kLoop, calls=%fused_computation.2 | loop fusion | flops 6160384 | bytes 589824 | tf_op jit(solution)/shard_map/reduce_sum | solution.py:14
  33.6 1.0 fusion.5
  34.6 1.0 copy-done.9
  35.6 2.0 %fusion.10 = f32[512,1024]{1,0:T(8,128)} fusion(bf16[512,1024]{1,0:T(8,128)(2,1)S(1)} %get-tuple-element.9, bf16[512,1024]{1,0:T(8,128)(2,1)S(1)} %bitcast.50), kind=kOutput, calls=%fused_computation.28 | convolution fusion | flops 536870912 | bytes 3670016 | tf_op jit(solution)/shard_map/dot_general | solution.py:88
  37.7 16.2 %all-to-all-done.1 = bf16[16,32,1024]{2,1,0:T(8,128)(2,1)} async-done(((bf16[16,32,1024]{2,1,0:T(8,128)(2,1)}), bf16[16,32,1024]{2,1,0:T(8,128)(2,1)}, u32[]{:S(2)}, u32[]{:S(2)}) %all-to-all-start.1) | async-done | bytes 1048608 | tf_op jit(solution)/shard_map/all_to_all | solution.py:70
  53.8 3.4 %multiply_reduce_fusion = (f32[512]{0:T(512)S(1)}, f32[512,1024]{1,0:T(8,128)S(1)}) fusion(bf16[512,1024]{1,0:T(8,128)(2,1)} %copy-done.8, f32[512]{0:T(512)S(1)} %convert_element_type.65, f32[512,1024]{1,0:T(8,128)} %fusion.10, bf16[512,1024]{1,0:T(8,128)(2,1)} %bitcast.6, bf16[512,1024]{1,0:T(8,128)(2,1)} %bitcast.51), kind=kOutput, calls=%fused_computation.15 | convolution fusion | flops 540016128 | bytes 6819840 | tf_op jit(solution)/shard_map/dot_general | solution.py:90
  57.2 0.5 fusion.1
  57.7 0.5 divide_convert_fusion
  58.3 0.2 copy-done.1
  58.5 0.6 copy-done.10
  59.2 1.7 convolution_convert_fusion.1
  60.9 4.9 %all-to-all-start.2 = ((bf16[16,32,1024]{2,1,0:T(8,128)(2,1)}), bf16[16,32,1024]{2,1,0:T(8,128)(2,1)}, u32[]{:S(2)}, u32[]{:S(2)}) async-start(bf16[16,32,1024]{2,1,0:T(8,128)(2,1)} %bitcast.54), calls=%async_computation.2 | async-start | bytes 2097152 | tf_op jit(solution)/shard_map/all_to_all | solution.py:109
  65.8 0.4 compare_reduce_fusion
  66.2 3.4 %fusion.8 = f32[512,1024]{1,0:T(8,128)} fusion(bf16[512,1024]{1,0:T(8,128)(2,1)} %copy-done.7, bf16[512,1024]{1,0:T(8,128)(2,1)} %bitcast.52), kind=kOutput, calls=%fused_computation.26 | convolution fusion | flops 536870912 | bytes 3670016 | tf_op jit(solution)/shard_map/dot_general | solution.py:110
  69.7 2.8 %reshape.175 = f32[16,32768]{1,0:T(8,128)} reshape(f32[512,1024]{1,0:T(8,128)} %fusion.8) | data formatting | bytes 4194304 | tf_op jit(solution)/shard_map/reshape | solution.py:117
  72.4 19.9 %all-to-all-done.2 = bf16[16,32,1024]{2,1,0:T(8,128)(2,1)} async-done(((bf16[16,32,1024]{2,1,0:T(8,128)(2,1)}), bf16[16,32,1024]{2,1,0:T(8,128)(2,1)}, u32[]{:S(2)}, u32[]{:S(2)}) %all-to-all-start.2) | async-done | bytes 1048608 | tf_op jit(solution)/shard_map/all_to_all | solution.py:109
  92.3 2.0 %copy.50 = bf16[2,8,32,1024]{3,1,2,0:T(8,128)(2,1)S(1)} copy(bf16[2,8,32,1024]{3,2,1,0:T(8,128)(2,1)} %bitcast.19) | data formatting | bytes 2097152
  94.3 1.9 convolution_add_fusion
  96.2 2.7 %reshape.178 = f32[512,1024]{1,0:T(8,128)} reshape(f32[16,32768]{1,0:T(8,128)} %convolution_add_fusion) | data formatting | bytes 4194304 | tf_op jit(solution)/shard_map/reshape | solution.py:123
  99.0 4.6 %select_convert_fusion = (bf16[512,1024]{1,0:T(8,128)(2,1)S(1)}, bf16[512,1024]{1,0:T(8,128)(2,1)}) fusion(f32[512,1024]{1,0:T(8,128)} %reshape.178, f32[512,1024]{1,0:T(8,128)} %get-tuple-element.10, f32[512,1024]{1,0:T(8,128)} %copy-done.1, bf16[512,1024]{1,0:T(8,128)(2,1)S(1)} %copy-done.3, f32[512]{0:T(512)S(1)} %broadcast_multiply_fusion, ...), kind=kLoop, calls=%fused_computation.13 | loop fusion | flops 5767168 | bytes 9445376 | tf_op jit(solution)/shard_map/convert_element_type | solution.py:126
  103.6 1.3 fusion.20
  104.9 1.9 %copy-done.2 = f32[1024,1024]{1,0:T(8,128)} copy-done((f32[1024,1024]{1,0:T(8,128)}, f32[1024,1024]{1,0:T(8,128)S(1)}, u32[]{:S(2)}) %copy-start.2) | copy-done | bytes 4194328
  107.0 1.3 copy.49
  108.4 3.9 %collective-permute-start = (bf16[1024,512]{1,0:T(8,128)(2,1)}, bf16[1024,512]{1,0:T(8,128)(2,1)S(1)}, u32[]{:S(2)}, u32[]{:S(2)}) collective-permute-start(bf16[1024,512]{1,0:T(8,128)(2,1)} %bitcast.55), channel_id=1, source_target_pairs={{0,1},{1,0},{2,3},{3,2},{4,5},{5,4},{6,7},{7,6},{8,9},{9,8},{10,11... | collective-permute-start | bytes 3145736 | tf_op jit(solution)/shard_map/ppermute | solution.py:29
  112.3 3.2 %constant_dynamic-slice_fusion.1 = f32[1024,1,512]{0,2,1:T(8,128)} fusion(f32[1024,2,512]{0,2,1:T(8,128)} %bitcast.44, s32[]{:T(128)S(6)} %select_n.58), kind=kLoop, calls=%fused_computation.59 | loop fusion | bytes 4194308 | tf_op jit(solution)/shard_map/jit(dynamic_index_in_dim)/dynamic_slice | solution.py:27
  115.5 2.9 %copy.42 = f32[1024,1,512]{2,0,1:T(8,128)} copy(f32[1024,1,512]{0,2,1:T(8,128)} %constant_dynamic-slice_fusion.1) | data formatting | bytes 4194304 | tf_op jit(solution)/shard_map/jit(dynamic_index_in_dim)/dynamic_slice | solution.py:27
  118.4 2.9 %fusion.3 = bf16[1024,512]{1,0:T(8,128)(2,1)} fusion(f32[1024,1,512]{2,0,1:T(8,128)} %copy.42, bf16[1024,512]{1,0:T(8,128)(2,1)S(1)} %collective-permute-done), kind=kLoop, calls=%fused_computation.12 | loop fusion | flops 1572864 | bytes 4194304 | tf_op jit(solution)/shard_map/convert_element_type | solution.py:34
  121.3 1.5 reshape.180
  122.8 0.6 copy.44
  123.4 1.1 copy.45
  124.5 45.5 %all_to_all.30 = bf16[512,2,512]{2,1,0:T(2,128)(2,1)S(1)} all-to-all(bf16[512,2,512]{2,1,0:T(2,128)(2,1)S(1)} %copy.45), channel_id=1, replica_groups=mesh['group'=32,'member'=16] {'group','member'}, dimensions={0} | all-to-all | bytes 2097152 | tf_op jit(solution)/shard_map/all_to_all | solution.py:36
  170.0 0.9 convert_reduce_fusion
  170.9 0.8 broadcast_in_dim.51
  171.8 5.7 %all-to-all-start.4 = ((f32[32,1,2048]{2,1,0:T(1,128)}), f32[32,1,2048]{2,1,0:T(1,128)S(1)}, u32[]{:S(2)}, u32[]{:S(2)}) async-start(f32[32,1,2048]{2,1,0:T(1,128)} %broadcast_in_dim.51), calls=%async_computation.4 | async-start | bytes 524288 | tf_op jit(solution)/shard_map/all_to_all | solution.py:41
  177.5 2.3 %convolution_convert_fusion = bf16[512,1024]{1,0:T(8,128)(2,1)} fusion(bf16[512,1024]{1,0:T(8,128)(2,1)S(1)} %copy-done.6, bf16[1024,1024]{1,0:T(8,128)(2,1)S(1)} %copy-done), kind=kOutput, calls=%fused_computation.21 | convolution fusion | flops 1074266112 | bytes 4194304 | tf_op jit(solution)/shard_map/dot_general | solution.py:127
  179.8 9.6 %all-to-all-done.4 = f32[32,1,2048]{2,1,0:T(1,128)S(1)} async-done(((f32[32,1,2048]{2,1,0:T(1,128)}), f32[32,1,2048]{2,1,0:T(1,128)S(1)}, u32[]{:S(2)}, u32[]{:S(2)}) %all-to-all-start.4) | async-done | bytes 262176 | tf_op jit(solution)/shard_map/all_to_all | solution.py:41
  189.4 0.7 multiply_reduce_fusion.1
  190.1 0.7 mul.65
  (43 shorter events, 0.7 us)
Async XLA Ops:
  0.6 12.8 %copy-start = (bf16[1024,1024]{1,0:T(8,128)(2,1)S(1)}, bf16[1024,1024]{1,0:T(8,128)(2,1)}, u32[]{:S(2)}) copy-start(bf16[1024,1024]{1,0:T(8,128)(2,1)} %param.8) | copy-start | bytes 6291460
  3.0 18.0 %all-to-all-start = ((s32[16,1,1]{2,1,0:T(1,128)}), s32[16,1,1]{2,1,0:T(1,128)S(1)}, u32[]{:S(2)}, u32[]{:S(2)}) async-start(s32[16,1,1]{2,1,0:T(1,128)} %copy.41), calls=%async_computation | async-start | bytes 16384 | tf_op jit(solution)/shard_map/all_to_all | solution.py:66
  17.2 17.4 %copy-start.8 = (bf16[512,1024]{1,0:T(8,128)(2,1)}, bf16[512,1024]{1,0:T(8,128)(2,1)S(1)}, u32[]{:S(2)}) copy-start(bf16[512,1024]{1,0:T(8,128)(2,1)S(1)} %get-tuple-element.9) | copy-start | bytes 3145732
  21.3 6.0 %copy-start.12 = (s32[512,16]{0,1:T(8,128)S(1)}, s32[512,16]{0,1:T(8,128)}, u32[]{:S(2)}) copy-start(s32[512,16]{0,1:T(8,128)} %param.12) | copy-start | bytes 98308
  21.3 6.4 %copy-start.13 = (s32[512,16]{0,1:T(8,128)S(1)}, s32[512,16]{0,1:T(8,128)}, u32[]{:S(2)}) copy-start(s32[512,16]{0,1:T(8,128)} %param.11) | copy-start | bytes 98308
  22.9 30.9 %all-to-all-start.1 = ((bf16[16,32,1024]{2,1,0:T(8,128)(2,1)}), bf16[16,32,1024]{2,1,0:T(8,128)(2,1)}, u32[]{:S(2)}, u32[]{:S(2)}) async-start(bf16[16,32,1024]{2,1,0:T(8,128)(2,1)} %gather_fusion), calls=%async_computation.1 | async-start | bytes 2097152 | tf_op jit(solution)/shard_map/all_to_all | solution.py:70
  34.6 1.0 copy-start.9
  53.8 3.4 %copy-start.3 = (bf16[512,1024]{1,0:T(8,128)(2,1)S(1)}, bf16[512,1024]{1,0:T(8,128)(2,1)}, u32[]{:S(2)}) copy-start(bf16[512,1024]{1,0:T(8,128)(2,1)} %param.13) | copy-start | bytes 3145732
  57.2 1.3 copy-start.1
  57.7 1.5 copy-start.10
  59.2 1.7 copy-start.7
  60.9 31.4 %all-to-all-start.2 = ((bf16[16,32,1024]{2,1,0:T(8,128)(2,1)}), bf16[16,32,1024]{2,1,0:T(8,128)(2,1)}, u32[]{:S(2)}, u32[]{:S(2)}) async-start(bf16[16,32,1024]{2,1,0:T(8,128)(2,1)} %bitcast.54), calls=%async_computation.2 | async-start | bytes 2097152 | tf_op jit(solution)/shard_map/all_to_all | solution.py:109
  92.3 2.0 %copy-start.4 = (f32[16,32768]{1,0:T(8,128)S(1)}, f32[16,32768]{1,0:T(8,128)}, u32[]{:S(2)}) copy-start(f32[16,32768]{1,0:T(8,128)} %reshape.175) | copy-start | bytes 6291460
  96.2 2.8 %copy-start.14 = (f32[1024]{0:T(1024)S(1)}, f32[1024]{0:T(1024)}, u32[]{:S(2)}) copy-start(f32[1024]{0:T(1024)} %param.9) | copy-start | bytes 12292
  99.0 4.7 %copy-start.11 = (bf16[512,1024]{1,0:T(8,128)(2,1)S(1)}, bf16[512,1024]{1,0:T(8,128)(2,1)}, u32[]{:S(2)}) copy-start(bf16[512,1024]{1,0:T(8,128)(2,1)} %param.7) | copy-start | bytes 3145732
  103.6 1.3 copy-start.5
  104.9 1.9 %copy-start.2 = (f32[1024,1024]{1,0:T(8,128)}, f32[1024,1024]{1,0:T(8,128)S(1)}, u32[]{:S(2)}) copy-start(f32[1024,1024]{1,0:T(8,128)S(1)} %fusion.20) | copy-start | bytes 12582916
  108.4 10.0 %collective-permute-start = (bf16[1024,512]{1,0:T(8,128)(2,1)}, bf16[1024,512]{1,0:T(8,128)(2,1)S(1)}, u32[]{:S(2)}, u32[]{:S(2)}) collective-permute-start(bf16[1024,512]{1,0:T(8,128)(2,1)} %bitcast.55), channel_id=1, source_target_pairs={{0,1},{1,0},{2,3},{3,2},{4,5},{5,4},{6,7},{7,6},{8,9},{9,8},{10,11... | collective-permute-start | bytes 3145736 | tf_op jit(solution)/shard_map/ppermute | solution.py:29
  124.5 53.0 %copy-start.6 = (bf16[512,1024]{1,0:T(8,128)(2,1)S(1)}, bf16[512,1024]{1,0:T(8,128)(2,1)}, u32[]{:S(2)}) copy-start(bf16[512,1024]{1,0:T(8,128)(2,1)} %copy-done.5) | copy-start | bytes 3145732
  171.8 17.6 %all-to-all-start.4 = ((f32[32,1,2048]{2,1,0:T(1,128)}), f32[32,1,2048]{2,1,0:T(1,128)S(1)}, u32[]{:S(2)}, u32[]{:S(2)}) async-start(f32[32,1,2048]{2,1,0:T(1,128)} %broadcast_in_dim.51), calls=%async_computation.4 | async-start | bytes 524288 | tf_op jit(solution)/shard_map/all_to_all | solution.py:41

commit v8 on v7

--- a/solution.py
+++ b/solution.py
@@ -23,9 +23,9 @@
     groups = lax.axis_size("group")
     core = lax.axis_index("member") % 2
     rows, cols = part.shape
-    halves = part.reshape(rows, 2, cols // 2)
-    keep = lax.dynamic_index_in_dim(halves, core, 1, keepdims=False)
-    send = lax.dynamic_index_in_dim(halves, 1 - core, 1, keepdims=False)
+    left, right = part[:, : cols // 2], part[:, cols // 2 :]
+    keep = jnp.where(core == 0, left, right)
+    send = jnp.where(core == 0, right, left)
     pair_sum = keep + lax.ppermute(send.astype(jnp.bfloat16), "member", xor_pairs(members, 0)).astype(
         jnp.float32
     )

time: 193 us -> 185 us (0.959)
  local copies, waits for them, and re-layouts: 27.1 us -> 18.5 us
  waiting for transfers between devices: 49.4 us -> 51.5 us
  other arithmetic: 17.7 us -> 15.6 us
    dynamic_slice x3 -> x0, local copies, waits for them, and re-layouts: 6.24 us -> none  [the longest x2 6.09 us: reduce_rows(): keep = lax.dynamic_index_in_dim(halves, core, 1, keepdims=False)]
    unnamed x33 -> x30, local copies, waits for them, and re-layouts: 7.17 us -> 3.89 us
    convert_element_type x1, other arithmetic: 2.94 us -> 0.63 us  [reduce_rows(): pair_sum.astype(jnp.bfloat16).reshape(members, groups, share, cols // 2)]
    ppermute x1, waiting for transfers between devices: 0.01 us -> 2.08 us  [reduce_rows(): lax.ppermute(send.astype(jnp.bfloat16), 'member', xor_pairs(members, 0))]
  transfers between devices with their start and end apart: 5 -> 5, of which waited for: 4 -> 5; matrix products, arithmetic and copies ran while one was open for 15% -> 12% of each run, Pallas kernels for 0% -> 0%
where the time goes in v8:
time: 185 us; the launch traced here: 183 us
  waiting for transfers between devices  51.5 us (28%)
  blocking collectives  45.8 us (25%)
  starting transfers between devices  29.4 us (16%)
  matrix products  20.9 us (11%)
  local copies, waits for them, and re-layouts  18.5 us (10%)
  other arithmetic  15.6 us (8%)
    all_to_all x1, blocking collectives, reduce_rows(): lax.all_to_all(chunks, ('group', 'member'), split_axis=0, concat_axis=0,...  45.8 us
    all_to_all x1, waiting for transfers between devices, on_device(): lax.all_to_all(returned, 'member', split_axis=0, concat_axis=0, tiled=True)  19.9 us
    all_to_all x1, waiting for transfers between devices, on_device(): lax.all_to_all(own_tiles[served], 'member', split_axis=0, concat_axis=0,...  16.2 us
    all_to_all x1, starting transfers between devices, on_device(): lax.all_to_all(wanted.reshape(members, 1), 'member', split_axis=0, concat...  10.4 us
    all_to_all x1, waiting for transfers between devices, reduce_rows(): lax.all_to_all(jnp.broadcast_to(mine, (groups, share * cols)), 'group', s...  9.63 us
    all_to_all x1, starting transfers between devices, reduce_rows(): lax.all_to_all(jnp.broadcast_to(mine, (groups, share * cols)), 'group', s...  5.74 us
    reduce_sum x1, other arithmetic, adjacency_of(): return jnp.sum(matched_weights, axis=-2).astype(jnp.bfloat16)  5.07 us
    all_to_all x1, starting transfers between devices, on_device(): lax.all_to_all(returned, 'member', split_axis=0, concat_axis=0, tiled=True)  4.91 us
  transfers between devices with their start and end apart: 5, of which 5 were waited for; matrix products, arithmetic and copies ran while one was open for 12% of the time, Pallas kernels for 0%

profile of v8, /device:TPU:6, one launch (start us, length us, event | category | flops | bytes accessed | tf_op | source)
XLA Modules:
  0.0 182.6 jit_solution(4230265918773044874)
XLA Ops:
  0.6 0.8 broadcast_compare_fusion
  1.5 0.7 add_select_fusion
  2.2 0.1 select_reduce_fusion.1
  2.3 0.7 copy.33
  3.0 10.4 %all-to-all-start = ((s32[16,1,1]{2,1,0:T(1,128)}), s32[16,1,1]{2,1,0:T(1,128)S(1)}, u32[]{:S(2)}, u32[]{:S(2)}) async-start(s32[16,1,1]{2,1,0:T(1,128)} %copy.33), calls=%async_computation | async-start | bytes 16384 | tf_op jit(solution)/shard_map/all_to_all | solution.py:66
  13.4 3.8 %maximum_convert_fusion = (bf16[512,1024]{1,0:T(8,128)(2,1)S(1)}, f32[512,1024]{1,0:T(8,128)}) fusion(f32[1024]{0:T(1024)} %param.9, bf16[512,1024]{1,0:T(8,128)(2,1)} %param.7, bf16[1024,1024]{1,0:T(8,128)(2,1)S(1)} %copy-done), kind=kOutput, calls=%fused_computation.18 | convolution fusion | flops 1075314688 | bytes 6295552 | tf_op jit(solution)/shard_map/dot_general | solution.py:57
  17.2 3.7 %all-to-all-done = s32[16,1,1]{2,1,0:T(1,128)S(1)} async-done(((s32[16,1,1]{2,1,0:T(1,128)}), s32[16,1,1]{2,1,0:T(1,128)S(1)}, u32[]{:S(2)}, u32[]{:S(2)}) %all-to-all-start) | async-done | bytes 96 | tf_op jit(solution)/shard_map/all_to_all | solution.py:66
  20.9 0.4 clamp_reduce_fusion
  21.3 1.6 gather_fusion
  22.9 4.4 %all-to-all-start.1 = ((bf16[16,32,1024]{2,1,0:T(8,128)(2,1)}), bf16[16,32,1024]{2,1,0:T(8,128)(2,1)}, u32[]{:S(2)}, u32[]{:S(2)}) async-start(bf16[16,32,1024]{2,1,0:T(8,128)(2,1)} %gather_fusion), calls=%async_computation.1 | async-start | bytes 2097152 | tf_op jit(solution)/shard_map/all_to_all | solution.py:70
  27.3 0.1 copy.38
  27.7 0.8 copy.37
  28.5 5.1 %select_reduce_fusion = s32[4,128,256]{2,1,0:T(8,128)S(1)} fusion(s32[4,128,16]{2,1,0:T(8,128)S(1)} %bitcast.45, s32[4,128,16]{2,1,0:T(8,128)} %bitcast.46), kind=kLoop, calls=%fused_computation.2 | loop fusion | flops 6160384 | bytes 589824 | tf_op jit(solution)/shard_map/reduce_sum | solution.py:14
  33.6 1.0 fusion.4
  34.6 1.0 copy-done.8
  35.6 2.0 %fusion.9 = f32[512,1024]{1,0:T(8,128)} fusion(bf16[512,1024]{1,0:T(8,128)(2,1)S(1)} %get-tuple-element.9, bf16[512,1024]{1,0:T(8,128)(2,1)S(1)} %bitcast.40), kind=kOutput, calls=%fused_computation.28 | convolution fusion | flops 536870912 | bytes 3670016 | tf_op jit(solution)/shard_map/dot_general | solution.py:88
  37.6 16.2 %all-to-all-done.1 = bf16[16,32,1024]{2,1,0:T(8,128)(2,1)} async-done(((bf16[16,32,1024]{2,1,0:T(8,128)(2,1)}), bf16[16,32,1024]{2,1,0:T(8,128)(2,1)}, u32[]{:S(2)}, u32[]{:S(2)}) %all-to-all-start.1) | async-done | bytes 1048608 | tf_op jit(solution)/shard_map/all_to_all | solution.py:70
  53.8 3.4 %multiply_reduce_fusion = (f32[512]{0:T(512)S(1)}, f32[512,1024]{1,0:T(8,128)S(1)}) fusion(bf16[512,1024]{1,0:T(8,128)(2,1)} %copy-done.7, f32[512]{0:T(512)S(1)} %convert_element_type.62, f32[512,1024]{1,0:T(8,128)} %fusion.9, bf16[512,1024]{1,0:T(8,128)(2,1)} %bitcast.6, bf16[512,1024]{1,0:T(8,128)(2,1)} %bitcast.41), kind=kOutput, calls=%fused_computation.16 | convolution fusion | flops 540016128 | bytes 6819840 | tf_op jit(solution)/shard_map/dot_general | solution.py:90
  57.3 0.5 fusion.1
  57.8 0.5 divide_convert_fusion
  58.3 0.2 copy-done.1
  58.5 0.7 copy-done.9
  59.2 1.7 convolution_convert_fusion.1
  60.9 4.9 %all-to-all-start.2 = ((bf16[16,32,1024]{2,1,0:T(8,128)(2,1)}), bf16[16,32,1024]{2,1,0:T(8,128)(2,1)}, u32[]{:S(2)}, u32[]{:S(2)}) async-start(bf16[16,32,1024]{2,1,0:T(8,128)(2,1)} %bitcast.44), calls=%async_computation.2 | async-start | bytes 2097152 | tf_op jit(solution)/shard_map/all_to_all | solution.py:109
  65.8 0.4 compare_reduce_fusion
  66.2 3.4 %fusion.7 = f32[512,1024]{1,0:T(8,128)} fusion(bf16[512,1024]{1,0:T(8,128)(2,1)} %copy-done.6, bf16[512,1024]{1,0:T(8,128)(2,1)} %bitcast.42), kind=kOutput, calls=%fused_computation.26 | convolution fusion | flops 536870912 | bytes 3670016 | tf_op jit(solution)/shard_map/dot_general | solution.py:110
  69.7 2.8 %reshape.171 = f32[16,32768]{1,0:T(8,128)} reshape(f32[512,1024]{1,0:T(8,128)} %fusion.7) | data formatting | bytes 4194304 | tf_op jit(solution)/shard_map/reshape | solution.py:117
  72.4 19.9 %all-to-all-done.2 = bf16[16,32,1024]{2,1,0:T(8,128)(2,1)} async-done(((bf16[16,32,1024]{2,1,0:T(8,128)(2,1)}), bf16[16,32,1024]{2,1,0:T(8,128)(2,1)}, u32[]{:S(2)}, u32[]{:S(2)}) %all-to-all-start.2) | async-done | bytes 1048608 | tf_op jit(solution)/shard_map/all_to_all | solution.py:109
  92.4 2.0 %copy.39 = bf16[2,8,32,1024]{3,1,2,0:T(8,128)(2,1)S(1)} copy(bf16[2,8,32,1024]{3,2,1,0:T(8,128)(2,1)} %bitcast.16) | data formatting | bytes 2097152
  94.3 1.9 %convolution_add_fusion = f32[16,32768]{1,0:T(8,128)} fusion(f32[16,32768]{1,0:T(8,128)S(1)} %copy-done.3, bf16[16,32768]{1,0:T(8,128)(2,1)S(1)} %bitcast.39, s32[16]{0:T(128)S(1)} %clamp_reduce_fusion, pred[16]{0:T(512)(128)(4,1)S(1)} %compare_reduce_fusion), kind=kOutput, calls=%fused_computation.1 | convolution fusion | flops 17302016 | bytes 5242960 | tf_op jit(solution)/shard_map/dot_general | solution.py:117
  96.2 2.8 %reshape.174 = f32[512,1024]{1,0:T(8,128)} reshape(f32[16,32768]{1,0:T(8,128)} %convolution_add_fusion) | data formatting | bytes 4194304 | tf_op jit(solution)/shard_map/reshape | solution.py:123
  99.0 4.6 %select_convert_fusion.1 = (bf16[512,1024]{1,0:T(8,128)(2,1)S(1)}, bf16[512,1024]{1,0:T(8,128)(2,1)}) fusion(f32[512,1024]{1,0:T(8,128)} %reshape.174, f32[512,1024]{1,0:T(8,128)} %get-tuple-element.10, f32[512,1024]{1,0:T(8,128)} %copy-done.1, bf16[512,1024]{1,0:T(8,128)(2,1)S(1)} %copy-done.2, f32[512]{0:T(512)S(1)} %broadcast_multiply_fusion, ...), kind=kLoop, calls=%fused_computation.14 | loop fusion | flops 5767168 | bytes 9445376 | tf_op jit(solution)/shard_map/convert_element_type | solution.py:126
  103.6 1.3 convolution_bitcast_fusion
  105.0 0.2 select_convert_fusion
  105.2 3.9 %collective-permute-start = (bf16[1024,512]{1,0:T(8,128)(2,1)S(1)}, bf16[1024,512]{1,0:T(8,128)(2,1)S(1)}, u32[]{:S(2)}, u32[]{:S(2)}) collective-permute-start(bf16[1024,512]{1,0:T(8,128)(2,1)S(1)} %select_convert_fusion), channel_id=1, source_target_pairs={{0,1},{1,0},{2,3},{3,2},{4,5},{5,4},{6,7},{7,6},{8,9},{9,8},{10,11... | collective-permute-start | bytes 3145736 | tf_op jit(solution)/shard_map/ppermute | solution.py:29
  109.1 2.1 %collective-permute-done = bf16[1024,512]{1,0:T(8,128)(2,1)S(1)} collective-permute-done((bf16[1024,512]{1,0:T(8,128)(2,1)S(1)}, bf16[1024,512]{1,0:T(8,128)(2,1)S(1)}, u32[]{:S(2)}, u32[]{:S(2)}) %collective-permute-start) | collective-permute-done | bytes 1048608 | tf_op jit(solution)/shard_map/ppermute | solution.py:29
  111.2 0.6 add_convert_fusion
  111.8 1.2 reshape.175
  113.0 1.8 copy.34
  114.8 1.1 copy.35
  115.9 45.8 %all_to_all.30 = bf16[512,2,512]{2,1,0:T(2,128)(2,1)S(1)} all-to-all(bf16[512,2,512]{2,1,0:T(2,128)(2,1)S(1)} %copy.35), channel_id=1, replica_groups=mesh['group'=32,'member'=16] {'group','member'}, dimensions={0} | all-to-all | bytes 2097152 | tf_op jit(solution)/shard_map/all_to_all | solution.py:36
  161.7 0.9 convert_reduce_fusion
  162.6 0.8 broadcast_in_dim.51
  163.5 5.7 %all-to-all-start.4 = ((f32[32,1,2048]{2,1,0:T(1,128)}), f32[32,1,2048]{2,1,0:T(1,128)S(1)}, u32[]{:S(2)}, u32[]{:S(2)}) async-start(f32[32,1,2048]{2,1,0:T(1,128)} %broadcast_in_dim.51), calls=%async_computation.4 | async-start | bytes 524288 | tf_op jit(solution)/shard_map/all_to_all | solution.py:41
  169.2 2.3 %convolution_convert_fusion = bf16[512,1024]{1,0:T(8,128)(2,1)} fusion(bf16[512,1024]{1,0:T(8,128)(2,1)S(1)} %copy-done.5, bf16[1024,1024]{1,0:T(8,128)(2,1)S(1)} %copy-done), kind=kOutput, calls=%fused_computation.22 | convolution fusion | flops 1074266112 | bytes 4194304 | tf_op jit(solution)/shard_map/dot_general | solution.py:127
  171.5 9.6 %all-to-all-done.4 = f32[32,1,2048]{2,1,0:T(1,128)S(1)} async-done(((f32[32,1,2048]{2,1,0:T(1,128)}), f32[32,1,2048]{2,1,0:T(1,128)S(1)}, u32[]{:S(2)}, u32[]{:S(2)}) %all-to-all-start.4) | async-done | bytes 262176 | tf_op jit(solution)/shard_map/all_to_all | solution.py:41
  181.1 0.7 multiply_reduce_fusion.1
  181.8 0.7 mul.65
  (38 shorter events, 0.4 us)
Async XLA Ops:
  0.6 12.8 %copy-start = (bf16[1024,1024]{1,0:T(8,128)(2,1)S(1)}, bf16[1024,1024]{1,0:T(8,128)(2,1)}, u32[]{:S(2)}) copy-start(bf16[1024,1024]{1,0:T(8,128)(2,1)} %param.8) | copy-start | bytes 6291460
  3.0 18.0 %all-to-all-start = ((s32[16,1,1]{2,1,0:T(1,128)}), s32[16,1,1]{2,1,0:T(1,128)S(1)}, u32[]{:S(2)}, u32[]{:S(2)}) async-start(s32[16,1,1]{2,1,0:T(1,128)} %copy.33), calls=%async_computation | async-start | bytes 16384 | tf_op jit(solution)/shard_map/all_to_all | solution.py:66
  17.2 17.4 %copy-start.7 = (bf16[512,1024]{1,0:T(8,128)(2,1)}, bf16[512,1024]{1,0:T(8,128)(2,1)S(1)}, u32[]{:S(2)}) copy-start(bf16[512,1024]{1,0:T(8,128)(2,1)S(1)} %get-tuple-element.9) | copy-start | bytes 3145732
  21.3 6.0 %copy-start.11 = (s32[512,16]{0,1:T(8,128)S(1)}, s32[512,16]{0,1:T(8,128)}, u32[]{:S(2)}) copy-start(s32[512,16]{0,1:T(8,128)} %param.12) | copy-start | bytes 98308
  21.3 6.4 %copy-start.12 = (s32[512,16]{0,1:T(8,128)S(1)}, s32[512,16]{0,1:T(8,128)}, u32[]{:S(2)}) copy-start(s32[512,16]{0,1:T(8,128)} %param.11) | copy-start | bytes 98308
  22.9 30.9 %all-to-all-start.1 = ((bf16[16,32,1024]{2,1,0:T(8,128)(2,1)}), bf16[16,32,1024]{2,1,0:T(8,128)(2,1)}, u32[]{:S(2)}, u32[]{:S(2)}) async-start(bf16[16,32,1024]{2,1,0:T(8,128)(2,1)} %gather_fusion), calls=%async_computation.1 | async-start | bytes 2097152 | tf_op jit(solution)/shard_map/all_to_all | solution.py:70
  34.6 1.0 copy-start.8
  53.8 3.4 %copy-start.2 = (bf16[512,1024]{1,0:T(8,128)(2,1)S(1)}, bf16[512,1024]{1,0:T(8,128)(2,1)}, u32[]{:S(2)}) copy-start(bf16[512,1024]{1,0:T(8,128)(2,1)} %param.13) | copy-start | bytes 3145732
  57.2 1.3 copy-start.1
  57.7 1.5 copy-start.9
  59.2 1.7 copy-start.6
  60.9 31.4 %all-to-all-start.2 = ((bf16[16,32,1024]{2,1,0:T(8,128)(2,1)}), bf16[16,32,1024]{2,1,0:T(8,128)(2,1)}, u32[]{:S(2)}, u32[]{:S(2)}) async-start(bf16[16,32,1024]{2,1,0:T(8,128)(2,1)} %bitcast.44), calls=%async_computation.2 | async-start | bytes 2097152 | tf_op jit(solution)/shard_map/all_to_all | solution.py:109
  92.4 2.0 %copy-start.3 = (f32[16,32768]{1,0:T(8,128)S(1)}, f32[16,32768]{1,0:T(8,128)}, u32[]{:S(2)}) copy-start(f32[16,32768]{1,0:T(8,128)} %reshape.171) | copy-start | bytes 6291460
  96.2 2.8 %copy-start.13 = (f32[1024]{0:T(1024)S(1)}, f32[1024]{0:T(1024)}, u32[]{:S(2)}) copy-start(f32[1024]{0:T(1024)} %param.9) | copy-start | bytes 12292
  99.0 4.7 %copy-start.10 = (bf16[512,1024]{1,0:T(8,128)(2,1)S(1)}, bf16[512,1024]{1,0:T(8,128)(2,1)}, u32[]{:S(2)}) copy-start(bf16[512,1024]{1,0:T(8,128)(2,1)} %param.7) | copy-start | bytes 3145732
  103.6 1.3 copy-start.4
  105.2 6.0 %collective-permute-start = (bf16[1024,512]{1,0:T(8,128)(2,1)S(1)}, bf16[1024,512]{1,0:T(8,128)(2,1)S(1)}, u32[]{:S(2)}, u32[]{:S(2)}) collective-permute-start(bf16[1024,512]{1,0:T(8,128)(2,1)S(1)} %select_convert_fusion), channel_id=1, source_target_pairs={{0,1},{1,0},{2,3},{3,2},{4,5},{5,4},{6,7},{7,6},{8,9},{9,8},{10,11... | collective-permute-start | bytes 3145736 | tf_op jit(solution)/shard_map/ppermute | solution.py:29
  115.9 53.3 %copy-start.5 = (bf16[512,1024]{1,0:T(8,128)(2,1)S(1)}, bf16[512,1024]{1,0:T(8,128)(2,1)}, u32[]{:S(2)}) copy-start(bf16[512,1024]{1,0:T(8,128)(2,1)} %copy-done.4) | copy-start | bytes 3145732
  163.5 17.6 %all-to-all-start.4 = ((f32[32,1,2048]{2,1,0:T(1,128)}), f32[32,1,2048]{2,1,0:T(1,128)S(1)}, u32[]{:S(2)}, u32[]{:S(2)}) async-start(f32[32,1,2048]{2,1,0:T(1,128)} %broadcast_in_dim.51), calls=%async_computation.4 | async-start | bytes 524288 | tf_op jit(solution)/shard_map/all_to_all | solution.py:41

commit v9 on v8

--- a/solution.py
+++ b/solution.py
@@ -23,17 +23,22 @@
     groups = lax.axis_size("group")
     core = lax.axis_index("member") % 2
     rows, cols = part.shape
+    block = rows // members
+    share = block // groups
+
+    def chunk_order(x):
+        x = x.reshape(members, groups, share, cols // 2)
+        return jnp.transpose(x, (1, 0, 2, 3)).reshape(groups * members, share, cols // 2)
+
     left, right = part[:, : cols // 2], part[:, cols // 2 :]
-    keep = jnp.where(core == 0, left, right)
-    send = jnp.where(core == 0, right, left)
+    keep = chunk_order(jnp.where(core == 0, left, right))
+    send = chunk_order(jnp.where(core == 0, right, left))
     pair_sum = keep + lax.ppermute(send.astype(jnp.bfloat16), "member", xor_pairs(members, 0)).astype(
         jnp.float32
     )
-    block = rows // members
-    share = block // groups
-    chunks = pair_sum.astype(jnp.bfloat16).reshape(members, groups, share, cols // 2)
-    chunks = jnp.transpose(chunks, (1, 0, 2, 3)).reshape(groups * members, share, cols // 2)
-    got = lax.all_to_all(chunks, ("group", "member"), split_axis=0, concat_axis=0, tiled=True)
+    got = lax.all_to_all(
+        pair_sum.astype(jnp.bfloat16), ("group", "member"), split_axis=0, concat_axis=0, tiled=True
+    )
     by_half = jnp.sum(
         got.astype(jnp.float32).reshape(groups * members // 2, 2, share, cols // 2), axis=0
     )

time: 185 us -> 195 us (1.054)
  local copies, waits for them, and re-layouts: 18.5 us -> 26.8 us
  other arithmetic: 15.6 us -> 20.3 us
  waiting for transfers between devices: 51.5 us -> 49.4 us
    convert_element_type x0 -> x3, local copies, waits for them, and re-layouts: none -> 4.13 us  [the longest x2 3.05 us: reduce_rows(): send.astype(jnp.bfloat16)]
    select_n x0 -> x1, other arithmetic: none -> 4.02 us  [reduce_rows(): keep = chunk_order(jnp.where(core == 0, left, right))]
    reshape x3 -> x2, local copies, waits for them, and re-layouts: 4.1 us -> 6.3 us  [chunk_order(): x = x.reshape(members, groups, share, cols // 2)]
    ppermute x1, waiting for transfers between devices: 2.08 us -> 0.01 us  [reduce_rows(): lax.ppermute(send.astype(jnp.bfloat16), 'member', xor_pairs(members, 0))]
    unnamed x30 -> x32, local copies, waits for them, and re-layouts: 3.89 us -> 5.83 us
  transfers between devices with their start and end apart: 5 -> 5, of which waited for: 5 -> 4; matrix products, arithmetic and copies ran while one was open for 12% -> 17% of each run, Pallas kernels for 0% -> 0%
where the time goes in v9:
time: 195 us; the launch traced here: 193 us
  waiting for transfers between devices  49.4 us (25%)
  blocking collectives  45.5 us (23%)
  starting transfers between devices  29.2 us (15%)
  local copies, waits for them, and re-layouts  26.8 us (14%)
  matrix products  20.9 us (11%)
  other arithmetic  20.3 us (10%)
    all_to_all x1, blocking collectives, reduce_rows(): lax.all_to_all(pair_sum.astype(jnp.bfloat16), ('group', 'member'), split_...  45.5 us
    all_to_all x1, waiting for transfers between devices, on_device(): lax.all_to_all(returned, 'member', split_axis=0, concat_axis=0, tiled=True)  19.9 us
    all_to_all x1, waiting for transfers between devices, on_device(): lax.all_to_all(own_tiles[served], 'member', split_axis=0, concat_axis=0,...  16.2 us
    all_to_all x1, starting transfers between devices, on_device(): lax.all_to_all(wanted.reshape(members, 1), 'member', split_axis=0, concat...  10.4 us
    all_to_all x1, waiting for transfers between devices, reduce_rows(): lax.all_to_all(jnp.broadcast_to(mine, (groups, share * cols)), 'group', s...  9.63 us
    reshape x2, local copies, waits for them, and re-layouts, chunk_order(): x = x.reshape(members, groups, share, cols // 2)  6.3 us
    unnamed x32, local copies, waits for them, and re-layouts  5.83 us
    all_to_all x1, starting transfers between devices, reduce_rows(): lax.all_to_all(jnp.broadcast_to(mine, (groups, share * cols)), 'group', s...  5.74 us
  transfers between devices with their start and end apart: 5, of which 4 were waited for; matrix products, arithmetic and copies ran while one was open for 17% of the time, Pallas kernels for 0%

profile of v9, /device:TPU:6, one launch (start us, length us, event | category | flops | bytes accessed | tf_op | source)
XLA Modules:
  0.0 193.0 jit_solution(10944385645293961330)
XLA Ops:
  0.6 0.8 broadcast_compare_fusion
  1.5 0.7 add_select_fusion
  2.3 0.7 copy.37
  3.0 10.4 %all-to-all-start = ((s32[16,1,1]{2,1,0:T(1,128)}), s32[16,1,1]{2,1,0:T(1,128)S(1)}, u32[]{:S(2)}, u32[]{:S(2)}) async-start(s32[16,1,1]{2,1,0:T(1,128)} %copy.37), calls=%async_computation | async-start | bytes 16384 | tf_op jit(solution)/shard_map/all_to_all | solution.py:71
  13.4 3.8 %maximum_convert_fusion = (bf16[512,1024]{1,0:T(8,128)(2,1)S(1)}, f32[512,1024]{1,0:T(8,128)}) fusion(f32[1024]{0:T(1024)} %param.9, bf16[512,1024]{1,0:T(8,128)(2,1)} %param.7, bf16[1024,1024]{1,0:T(8,128)(2,1)S(1)} %copy-done), kind=kOutput, calls=%fused_computation.19 | convolution fusion | flops 1075314688 | bytes 6295552 | tf_op jit(solution)/shard_map/dot_general | solution.py:62
  17.2 3.7 %all-to-all-done = s32[16,1,1]{2,1,0:T(1,128)S(1)} async-done(((s32[16,1,1]{2,1,0:T(1,128)}), s32[16,1,1]{2,1,0:T(1,128)S(1)}, u32[]{:S(2)}, u32[]{:S(2)}) %all-to-all-start) | async-done | bytes 96 | tf_op jit(solution)/shard_map/all_to_all | solution.py:71
  20.9 0.4 clamp_reduce_fusion
  21.3 1.6 gather_fusion
  22.9 4.3 %all-to-all-start.1 = ((bf16[16,32,1024]{2,1,0:T(8,128)(2,1)}), bf16[16,32,1024]{2,1,0:T(8,128)(2,1)}, u32[]{:S(2)}, u32[]{:S(2)}) async-start(bf16[16,32,1024]{2,1,0:T(8,128)(2,1)} %gather_fusion), calls=%async_computation.1 | async-start | bytes 2097152 | tf_op jit(solution)/shard_map/all_to_all | solution.py:75
  27.7 0.8 copy.42
  28.5 5.1 %select_reduce_fusion = s32[4,128,256]{2,1,0:T(8,128)S(1)} fusion(s32[4,128,16]{2,1,0:T(8,128)S(1)} %bitcast.50, s32[4,128,16]{2,1,0:T(8,128)} %bitcast.51), kind=kLoop, calls=%fused_computation.2 | loop fusion | flops 6160384 | bytes 589824 | tf_op jit(solution)/shard_map/reduce_sum | solution.py:14
  33.6 1.0 fusion.5
  34.6 1.0 copy-done.9
  35.6 2.0 %fusion.10 = f32[512,1024]{1,0:T(8,128)} fusion(bf16[512,1024]{1,0:T(8,128)(2,1)S(1)} %get-tuple-element.9, bf16[512,1024]{1,0:T(8,128)(2,1)S(1)} %bitcast.45), kind=kOutput, calls=%fused_computation.30 | convolution fusion | flops 536870912 | bytes 3670016 | tf_op jit(solution)/shard_map/dot_general | solution.py:93
  37.7 16.2 %all-to-all-done.1 = bf16[16,32,1024]{2,1,0:T(8,128)(2,1)} async-done(((bf16[16,32,1024]{2,1,0:T(8,128)(2,1)}), bf16[16,32,1024]{2,1,0:T(8,128)(2,1)}, u32[]{:S(2)}, u32[]{:S(2)}) %all-to-all-start.1) | async-done | bytes 1048608 | tf_op jit(solution)/shard_map/all_to_all | solution.py:75
  53.8 3.4 %multiply_reduce_fusion = (f32[512]{0:T(512)S(1)}, f32[512,1024]{1,0:T(8,128)S(1)}) fusion(bf16[512,1024]{1,0:T(8,128)(2,1)} %copy-done.8, f32[512]{0:T(512)S(1)} %convert_element_type.71, f32[512,1024]{1,0:T(8,128)} %fusion.10, bf16[512,1024]{1,0:T(8,128)(2,1)} %bitcast.6, bf16[512,1024]{1,0:T(8,128)(2,1)} %bitcast.46), kind=kOutput, calls=%fused_computation.17 | convolution fusion | flops 540016128 | bytes 6819840 | tf_op jit(solution)/shard_map/dot_general | solution.py:95
  57.2 0.5 fusion.1
  57.7 0.5 divide_convert_fusion
  58.5 0.6 copy-done.10
  59.2 1.7 convolution_convert_fusion.1
  60.9 4.9 %all-to-all-start.2 = ((bf16[16,32,1024]{2,1,0:T(8,128)(2,1)}), bf16[16,32,1024]{2,1,0:T(8,128)(2,1)}, u32[]{:S(2)}, u32[]{:S(2)}) async-start(bf16[16,32,1024]{2,1,0:T(8,128)(2,1)} %bitcast.49), calls=%async_computation.2 | async-start | bytes 2097152 | tf_op jit(solution)/shard_map/all_to_all | solution.py:114
  65.8 0.4 compare_reduce_fusion
  66.2 3.4 %fusion.8 = f32[512,1024]{1,0:T(8,128)} fusion(bf16[512,1024]{1,0:T(8,128)(2,1)} %copy-done.7, bf16[512,1024]{1,0:T(8,128)(2,1)} %bitcast.47), kind=kOutput, calls=%fused_computation.28 | convolution fusion | flops 536870912 | bytes 3670016 | tf_op jit(solution)/shard_map/dot_general | solution.py:115
  69.7 2.8 %reshape.175 = f32[16,32768]{1,0:T(8,128)} reshape(f32[512,1024]{1,0:T(8,128)} %fusion.8) | data formatting | bytes 4194304 | tf_op jit(solution)/shard_map/reshape | solution.py:122
  72.4 19.9 %all-to-all-done.2 = bf16[16,32,1024]{2,1,0:T(8,128)(2,1)} async-done(((bf16[16,32,1024]{2,1,0:T(8,128)(2,1)}), bf16[16,32,1024]{2,1,0:T(8,128)(2,1)}, u32[]{:S(2)}, u32[]{:S(2)}) %all-to-all-start.2) | async-done | bytes 1048608 | tf_op jit(solution)/shard_map/all_to_all | solution.py:114
  92.3 2.0 %copy.44 = bf16[2,8,32,1024]{3,1,2,0:T(8,128)(2,1)S(1)} copy(bf16[2,8,32,1024]{3,2,1,0:T(8,128)(2,1)} %bitcast.19) | data formatting | bytes 2097152
  94.3 1.9 convolution_add_fusion
  96.2 2.7 %reshape.178 = f32[512,1024]{1,0:T(8,128)} reshape(f32[16,32768]{1,0:T(8,128)} %convolution_add_fusion) | data formatting | bytes 4194304 | tf_op jit(solution)/shard_map/reshape | solution.py:128
  99.0 4.6 %select_convert_fusion.1 = (bf16[512,1024]{1,0:T(8,128)(2,1)S(1)}, bf16[512,1024]{1,0:T(8,128)(2,1)}) fusion(f32[512,1024]{1,0:T(8,128)} %reshape.178, f32[512,1024]{1,0:T(8,128)} %get-tuple-element.10, f32[512,1024]{1,0:T(8,128)} %copy-done.2, bf16[512,1024]{1,0:T(8,128)(2,1)S(1)} %copy-done.3, f32[512]{0:T(512)S(1)} %broadcast_multiply_fusion, ...), kind=kLoop, calls=%fused_computation.15 | loop fusion | flops 5767168 | bytes 9445376 | tf_op jit(solution)/shard_map/convert_element_type | solution.py:131
  103.6 1.3 convolution_bitcast_fusion
  105.0 1.9 copy-done.1
  106.9 1.2 select_convert_fusion
  108.1 1.5 convert_element_type.80
  109.5 1.6 copy.39
  111.1 3.8 %collective-permute-start = (bf16[512,2,512]{2,0,1:T(8,128)(2,1)}, bf16[512,2,512]{2,0,1:T(8,128)(2,1)S(1)}, u32[]{:S(2)}, u32[]{:S(2)}) collective-permute-start(bf16[512,2,512]{2,0,1:T(8,128)(2,1)} %bitcast.12), channel_id=1, source_target_pairs={{0,1},{1,0},{2,3},{3,2},{4,5},{5,4},{6,7},{7,6},{8,9},{9,8},{10,11... | collective-permute-start | bytes 3145736 | tf_op jit(solution)/shard_map/ppermute | solution.py:36
  114.9 4.0 %slice_select_fusion = f32[1024,512]{1,0:T(8,128)} fusion(f32[1024,1024]{1,0:T(8,128)} %copy-done.1, pred[]{:T(512)S(6)} %eq.69), kind=kLoop, calls=%fused_computation.21 | loop fusion | flops 524288 | bytes 6291457 | tf_op jit(solution)/shard_map/jit(_where)/select_n | solution.py:34
  118.9 3.5 %reshape.179 = f32[16,32,2,512]{3,2,1,0:T(2,128)} reshape(f32[1024,512]{1,0:T(8,128)} %slice_select_fusion) | data formatting | bytes 4194304 | tf_op jit(solution)/shard_map/reshape | solution.py:30
  122.4 2.8 %copy.38 = f32[16,32,2,512]{3,0,1,2:T(8,128)S(1)} copy(f32[16,32,2,512]{3,2,1,0:T(2,128)} %reshape.179) | data formatting | bytes 4194304 | tf_op jit(solution)/shard_map/reshape | solution.py:30
  125.2 0.4 fusion.3
  125.6 1.1 copy.40
  126.7 45.5 %all_to_all.30 = bf16[512,2,512]{2,1,0:T(2,128)(2,1)S(1)} all-to-all(bf16[512,2,512]{2,1,0:T(2,128)(2,1)S(1)} %copy.40), channel_id=1, replica_groups=mesh['group'=32,'member'=16] {'group','member'}, dimensions={0} | all-to-all | bytes 2097152 | tf_op jit(solution)/shard_map/all_to_all | solution.py:39
  172.2 0.9 convert_reduce_fusion
  173.1 0.8 broadcast_in_dim.51
  173.9 5.7 %all-to-all-start.4 = ((f32[32,1,2048]{2,1,0:T(1,128)}), f32[32,1,2048]{2,1,0:T(1,128)S(1)}, u32[]{:S(2)}, u32[]{:S(2)}) async-start(f32[32,1,2048]{2,1,0:T(1,128)} %broadcast_in_dim.51), calls=%async_computation.4 | async-start | bytes 524288 | tf_op jit(solution)/shard_map/all_to_all | solution.py:46
  179.7 2.3 %convolution_convert_fusion = bf16[512,1024]{1,0:T(8,128)(2,1)} fusion(bf16[512,1024]{1,0:T(8,128)(2,1)S(1)} %copy-done.6, bf16[1024,1024]{1,0:T(8,128)(2,1)S(1)} %copy-done), kind=kOutput, calls=%fused_computation.24 | convolution fusion | flops 1074266112 | bytes 4194304 | tf_op jit(solution)/shard_map/dot_general | solution.py:132
  182.0 9.6 %all-to-all-done.4 = f32[32,1,2048]{2,1,0:T(1,128)S(1)} async-done(((f32[32,1,2048]{2,1,0:T(1,128)}), f32[32,1,2048]{2,1,0:T(1,128)S(1)}, u32[]{:S(2)}, u32[]{:S(2)}) %all-to-all-start.4) | async-done | bytes 262176 | tf_op jit(solution)/shard_map/all_to_all | solution.py:46
  191.6 0.7 multiply_reduce_fusion.1
  192.3 0.7 mul.65
  (43 shorter events, 0.8 us)
Async XLA Ops:
  0.6 12.8 %copy-start = (bf16[1024,1024]{1,0:T(8,128)(2,1)S(1)}, bf16[1024,1024]{1,0:T(8,128)(2,1)}, u32[]{:S(2)}) copy-start(bf16[1024,1024]{1,0:T(8,128)(2,1)} %param.8) | copy-start | bytes 6291460
  3.0 18.0 %all-to-all-start = ((s32[16,1,1]{2,1,0:T(1,128)}), s32[16,1,1]{2,1,0:T(1,128)S(1)}, u32[]{:S(2)}, u32[]{:S(2)}) async-start(s32[16,1,1]{2,1,0:T(1,128)} %copy.37), calls=%async_computation | async-start | bytes 16384 | tf_op jit(solution)/shard_map/all_to_all | solution.py:71
  17.2 17.4 %copy-start.8 = (bf16[512,1024]{1,0:T(8,128)(2,1)}, bf16[512,1024]{1,0:T(8,128)(2,1)S(1)}, u32[]{:S(2)}) copy-start(bf16[512,1024]{1,0:T(8,128)(2,1)S(1)} %get-tuple-element.9) | copy-start | bytes 3145732
  21.3 6.0 %copy-start.12 = (s32[512,16]{0,1:T(8,128)S(1)}, s32[512,16]{0,1:T(8,128)}, u32[]{:S(2)}) copy-start(s32[512,16]{0,1:T(8,128)} %param.12) | copy-start | bytes 98308
  21.3 6.4 %copy-start.13 = (s32[512,16]{0,1:T(8,128)S(1)}, s32[512,16]{0,1:T(8,128)}, u32[]{:S(2)}) copy-start(s32[512,16]{0,1:T(8,128)} %param.11) | copy-start | bytes 98308
  22.9 30.9 %all-to-all-start.1 = ((bf16[16,32,1024]{2,1,0:T(8,128)(2,1)}), bf16[16,32,1024]{2,1,0:T(8,128)(2,1)}, u32[]{:S(2)}, u32[]{:S(2)}) async-start(bf16[16,32,1024]{2,1,0:T(8,128)(2,1)} %gather_fusion), calls=%async_computation.1 | async-start | bytes 2097152 | tf_op jit(solution)/shard_map/all_to_all | solution.py:75
  34.6 1.0 copy-start.9
  53.8 3.4 %copy-start.3 = (bf16[512,1024]{1,0:T(8,128)(2,1)S(1)}, bf16[512,1024]{1,0:T(8,128)(2,1)}, u32[]{:S(2)}) copy-start(bf16[512,1024]{1,0:T(8,128)(2,1)} %param.13) | copy-start | bytes 3145732
  57.2 1.3 copy-start.2
  57.7 1.5 copy-start.10
  59.2 1.7 copy-start.7
  60.9 31.4 %all-to-all-start.2 = ((bf16[16,32,1024]{2,1,0:T(8,128)(2,1)}), bf16[16,32,1024]{2,1,0:T(8,128)(2,1)}, u32[]{:S(2)}, u32[]{:S(2)}) async-start(bf16[16,32,1024]{2,1,0:T(8,128)(2,1)} %bitcast.49), calls=%async_computation.2 | async-start | bytes 2097152 | tf_op jit(solution)/shard_map/all_to_all | solution.py:114
  92.3 2.0 %copy-start.4 = (f32[16,32768]{1,0:T(8,128)S(1)}, f32[16,32768]{1,0:T(8,128)}, u32[]{:S(2)}) copy-start(f32[16,32768]{1,0:T(8,128)} %reshape.175) | copy-start | bytes 6291460
  96.2 2.8 %copy-start.14 = (f32[1024]{0:T(1024)S(1)}, f32[1024]{0:T(1024)}, u32[]{:S(2)}) copy-start(f32[1024]{0:T(1024)} %param.9) | copy-start | bytes 12292
  99.0 4.7 %copy-start.11 = (bf16[512,1024]{1,0:T(8,128)(2,1)S(1)}, bf16[512,1024]{1,0:T(8,128)(2,1)}, u32[]{:S(2)}) copy-start(bf16[512,1024]{1,0:T(8,128)(2,1)} %param.7) | copy-start | bytes 3145732
  103.6 1.3 copy-start.5
  105.0 1.9 %copy-start.1 = (f32[1024,1024]{1,0:T(8,128)}, f32[1024,1024]{1,0:T(8,128)S(1)}, u32[]{:S(2)}) copy-start(f32[1024,1024]{1,0:T(8,128)S(1)} %convolution_bitcast_fusion) | copy-start | bytes 12582916
  111.1 14.1 %collective-permute-start = (bf16[512,2,512]{2,0,1:T(8,128)(2,1)}, bf16[512,2,512]{2,0,1:T(8,128)(2,1)S(1)}, u32[]{:S(2)}, u32[]{:S(2)}) collective-permute-start(bf16[512,2,512]{2,0,1:T(8,128)(2,1)} %bitcast.12), channel_id=1, source_target_pairs={{0,1},{1,0},{2,3},{3,2},{4,5},{5,4},{6,7},{7,6},{8,9},{9,8},{10,11... | collective-permute-start | bytes 3145736 | tf_op jit(solution)/shard_map/ppermute | solution.py:36
  126.7 53.0 %copy-start.6 = (bf16[512,1024]{1,0:T(8,128)(2,1)S(1)}, bf16[512,1024]{1,0:T(8,128)(2,1)}, u32[]{:S(2)}) copy-start(bf16[512,1024]{1,0:T(8,128)(2,1)} %copy-done.5) | copy-start | bytes 3145732
  173.9 17.6 %all-to-all-start.4 = ((f32[32,1,2048]{2,1,0:T(1,128)}), f32[32,1,2048]{2,1,0:T(1,128)S(1)}, u32[]{:S(2)}, u32[]{:S(2)}) async-start(f32[32,1,2048]{2,1,0:T(1,128)} %broadcast_in_dim.51), calls=%async_computation.4 | async-start | bytes 524288 | tf_op jit(solution)/shard_map/all_to_all | solution.py:46

commit v10 on v8

--- a/solution.py
+++ b/solution.py
@@ -114,11 +114,8 @@
         (served[:, None] == lax.broadcasted_iota(jnp.int32, (1, tiles_dev), 1))
         & (asked_for >= 0)[:, None]
     ).astype(jnp.bfloat16)
-    tile_grad = own_grad.reshape(tiles_dev, TILE * hidden_width) + lax.dot_general(
-        back_to,
-        came_back.reshape(members, TILE * hidden_width),
-        by_rows,
-        preferred_element_type=jnp.float32,
+    tile_grad = own_grad.reshape(tiles_dev, TILE, hidden_width) + jnp.einsum(
+        "jt,jrh->trh", back_to, came_back, preferred_element_type=jnp.float32
     )
     message_grad = mixed_grad.reshape(rows_dev, hidden_width) + tile_grad.reshape(
         rows_dev, hidden_width

time: 185 us -> 180 us (0.973)
  other arithmetic: 15.6 us -> 12.7 us
  local copies, waits for them, and re-layouts: 18.5 us -> 15.6 us
  waiting for transfers between devices: 51.5 us -> 53.8 us
    reshape x2 -> x0, local copies, waits for them, and re-layouts: 5.5 us -> none  [the longest x1 2.75 us: on_device(): own_grad.reshape(tiles_dev, TILE * hidden_width)]
    dot_general x0 -> x2, local copies, waits for them, and re-layouts: none -> 3.96 us  [on_device(): lax.dot_general(pool_adjacency[:, remote_rows:], agg_grad, by_rows, prefe...]
    convert_element_type x1, other arithmetic: 4.65 us -> 1.75 us  [on_device(): pre_grad = jnp.where(preact > 0, message_grad, 0.0).astype(jnp.bfloat16)]
    all_to_all x1, waiting for transfers between devices: 19.9 us -> 22.2 us  [on_device(): lax.all_to_all(returned, 'member', split_axis=0, concat_axis=0, tiled=True)]
    dot_general x1, matrix products: 3.45 us -> 1.59 us  [on_device(): lax.dot_general(pool_adjacency[:, remote_rows:], agg_grad, by_rows, prefe...]
    unnamed x30 -> x35, local copies, waits for them, and re-layouts: 3.89 us -> 2.53 us
  transfers between devices with their start and end apart: 5 -> 5, of which waited for: 5 -> 5; matrix products, arithmetic and copies ran while one was open for 12% -> 11% of each run, Pallas kernels for 0% -> 0%
where the time goes in v10:
time: 180 us; the launch traced here: 177 us
  waiting for transfers between devices  53.8 us (30%)
  blocking collectives  45.8 us (25%)
  starting transfers between devices  29.4 us (16%)
  matrix products  19.3 us (11%)
  local copies, waits for them, and re-layouts  15.6 us (9%)
  other arithmetic  12.7 us (7%)
    all_to_all x1, blocking collectives, reduce_rows(): lax.all_to_all(chunks, ('group', 'member'), split_axis=0, concat_axis=0,...  45.8 us
    all_to_all x1, waiting for transfers between devices, on_device(): lax.all_to_all(returned, 'member', split_axis=0, concat_axis=0, tiled=True)  22.2 us
    all_to_all x1, waiting for transfers between devices, on_device(): lax.all_to_all(own_tiles[served], 'member', split_axis=0, concat_axis=0,...  16.2 us
    all_to_all x1, starting transfers between devices, on_device(): lax.all_to_all(wanted.reshape(members, 1), 'member', split_axis=0, concat...  10.4 us
    all_to_all x1, waiting for transfers between devices, reduce_rows(): lax.all_to_all(jnp.broadcast_to(mine, (groups, share * cols)), 'group', s...  9.63 us
    all_to_all x1, starting transfers between devices, reduce_rows(): lax.all_to_all(jnp.broadcast_to(mine, (groups, share * cols)), 'group', s...  5.74 us
    reduce_sum x1, other arithmetic, adjacency_of(): return jnp.sum(matched_weights, axis=-2).astype(jnp.bfloat16)  5.07 us
    all_to_all x1, starting transfers between devices, on_device(): lax.all_to_all(returned, 'member', split_axis=0, concat_axis=0, tiled=True)  4.91 us
  transfers between devices with their start and end apart: 5, of which 5 were waited for; matrix products, arithmetic and copies ran while one was open for 11% of the time, Pallas kernels for 0%

profile of v10, /device:TPU:6, one launch (start us, length us, event | category | flops | bytes accessed | tf_op | source)
XLA Modules:
  0.0 177.5 jit_solution(3637786319612415024)
XLA Ops:
  0.6 0.8 broadcast_compare_fusion
  1.5 0.7 add_select_fusion
  2.2 0.1 select_reduce_fusion.1
  2.3 0.7 copy.48
  3.0 10.4 %all-to-all-start = ((s32[16,1,1]{2,1,0:T(1,128)}), s32[16,1,1]{2,1,0:T(1,128)S(1)}, u32[]{:S(2)}, u32[]{:S(2)}) async-start(s32[16,1,1]{2,1,0:T(1,128)} %copy.48), calls=%async_computation | async-start | bytes 16384 | tf_op jit(solution)/shard_map/all_to_all | solution.py:66
  13.4 3.8 %maximum_convert_fusion = (bf16[512,1024]{1,0:T(8,128)(2,1)S(1)}, f32[512,1024]{1,0:T(8,128)}) fusion(f32[1024]{0:T(1024)} %param.9, bf16[512,1024]{1,0:T(8,128)(2,1)} %param.7, bf16[1024,1024]{1,0:T(8,128)(2,1)S(1)} %copy-done), kind=kOutput, calls=%fused_computation.20 | convolution fusion | flops 1075314688 | bytes 6295552 | tf_op jit(solution)/shard_map/dot_general | solution.py:57
  17.2 3.7 %all-to-all-done = s32[16,1,1]{2,1,0:T(1,128)S(1)} async-done(((s32[16,1,1]{2,1,0:T(1,128)}), s32[16,1,1]{2,1,0:T(1,128)S(1)}, u32[]{:S(2)}, u32[]{:S(2)}) %all-to-all-start) | async-done | bytes 96 | tf_op jit(solution)/shard_map/all_to_all | solution.py:66
  20.9 0.4 clamp_reduce_fusion
  21.3 1.6 gather_fusion
  22.9 4.4 %all-to-all-start.1 = ((bf16[16,32,1024]{2,1,0:T(8,128)(2,1)}), bf16[16,32,1024]{2,1,0:T(8,128)(2,1)}, u32[]{:S(2)}, u32[]{:S(2)}) async-start(bf16[16,32,1024]{2,1,0:T(8,128)(2,1)} %gather_fusion), calls=%async_computation.1 | async-start | bytes 2097152 | tf_op jit(solution)/shard_map/all_to_all | solution.py:70
  27.3 0.1 copy.56
  27.7 0.8 copy.55
  28.5 5.1 %select_reduce_fusion = s32[4,128,256]{2,1,0:T(8,128)S(1)} fusion(s32[4,128,16]{2,1,0:T(8,128)S(1)} %bitcast.57, s32[4,128,16]{2,1,0:T(8,128)} %bitcast.58), kind=kLoop, calls=%fused_computation.1 | loop fusion | flops 6160384 | bytes 589824 | tf_op jit(solution)/shard_map/reduce_sum | solution.py:14
  33.6 1.0 fusion.6
  34.6 1.0 copy-done.11
  35.6 2.0 %fusion.12 = f32[512,1024]{1,0:T(8,128)} fusion(bf16[512,1024]{1,0:T(8,128)(2,1)S(1)} %get-tuple-element.9, bf16[512,1024]{1,0:T(8,128)(2,1)S(1)} %bitcast.52), kind=kOutput, calls=%fused_computation.32 | convolution fusion | flops 536870912 | bytes 3670016 | tf_op jit(solution)/shard_map/dot_general | solution.py:88
  37.6 16.2 %all-to-all-done.1 = bf16[16,32,1024]{2,1,0:T(8,128)(2,1)} async-done(((bf16[16,32,1024]{2,1,0:T(8,128)(2,1)}), bf16[16,32,1024]{2,1,0:T(8,128)(2,1)}, u32[]{:S(2)}, u32[]{:S(2)}) %all-to-all-start.1) | async-done | bytes 1048608 | tf_op jit(solution)/shard_map/all_to_all | solution.py:70
  53.8 3.4 %multiply_reduce_fusion = (f32[512]{0:T(512)S(1)}, f32[512,1024]{1,0:T(8,128)S(1)}) fusion(bf16[512,1024]{1,0:T(8,128)(2,1)} %copy-done.6, f32[512]{0:T(512)S(1)} %convert_element_type.62, f32[512,1024]{1,0:T(8,128)} %fusion.12, bf16[512,1024]{1,0:T(8,128)(2,1)} %bitcast.6, bf16[512,1024]{1,0:T(8,128)(2,1)} %bitcast.53), kind=kOutput, calls=%fused_computation.18 | convolution fusion | flops 540016128 | bytes 6819840 | tf_op jit(solution)/shard_map/dot_general | solution.py:90
  57.3 0.5 fusion.1
  57.7 0.5 divide_convert_fusion
  58.3 0.2 copy-done.1
  58.5 0.6 copy-done.12
  59.2 1.7 convolution_convert_fusion.1
  60.9 4.9 %all-to-all-start.2 = ((bf16[16,32,1024]{2,1,0:T(8,128)(2,1)}), bf16[16,32,1024]{2,1,0:T(8,128)(2,1)}, u32[]{:S(2)}, u32[]{:S(2)}) async-start(bf16[16,32,1024]{2,1,0:T(8,128)(2,1)} %bitcast.56), calls=%async_computation.2 | async-start | bytes 2097152 | tf_op jit(solution)/shard_map/all_to_all | solution.py:109
  65.8 1.9 %slice_bitcast_fusion = bf16[512,512]{0,1:T(8,128)(2,1)} fusion(bf16[512,1024]{1,0:T(8,128)(2,1)} %bitcast.54), kind=kLoop, calls=%fused_computation.31 | loop fusion | bytes 1048576 | tf_op jit(solution)/shard_map/dot_general | solution.py:110
  67.7 2.1 %copy.49 = bf16[512,512]{1,0:T(8,128)(2,1)} copy(bf16[512,512]{0,1:T(8,128)(2,1)} %slice_bitcast_fusion) | data formatting | bytes 1048576 | tf_op jit(solution)/shard_map/dot_general | solution.py:110
  69.8 0.4 compare_reduce_fusion
  70.2 22.2 %all-to-all-done.2 = bf16[16,32,1024]{2,1,0:T(8,128)(2,1)} async-done(((bf16[16,32,1024]{2,1,0:T(8,128)(2,1)}), bf16[16,32,1024]{2,1,0:T(8,128)(2,1)}, u32[]{:S(2)}, u32[]{:S(2)}) %all-to-all-start.2) | async-done | bytes 1048608 | tf_op jit(solution)/shard_map/all_to_all | solution.py:109
  92.4 2.1 %fusion.8 = f32[16,32,1024]{2,0,1:T(8,128)S(1)} fusion(bf16[16,32,1024]{2,1,0:T(8,128)(2,1)} %all-to-all-done.2, s32[16]{0:T(128)S(1)} %clamp_reduce_fusion, pred[16]{0:T(512)(128)(4,1)S(1)} %compare_reduce_fusion), kind=kOutput, calls=%fused_computation.27 | convolution fusion | flops 16777728 | bytes 3145808 | tf_op jit(solution)/shard_map/jt,jrh->trh/dot_general | solution.py:117
  94.6 1.6 copy_add_fusion
  96.2 0.6 copy-done.9
  96.8 1.7 fusion.4
  98.5 1.3 convolution_bitcast_fusion
  99.9 0.2 select_convert_fusion
  100.0 4.0 %collective-permute-start = (bf16[1024,512]{1,0:T(8,128)(2,1)S(1)}, bf16[1024,512]{1,0:T(8,128)(2,1)S(1)}, u32[]{:S(2)}, u32[]{:S(2)}) collective-permute-start(bf16[1024,512]{1,0:T(8,128)(2,1)S(1)} %select_convert_fusion), channel_id=1, source_target_pairs={{0,1},{1,0},{2,3},{3,2},{4,5},{5,4},{6,7},{7,6},{8,9},{9,8},{10,11... | collective-permute-start | bytes 3145736 | tf_op jit(solution)/shard_map/ppermute | solution.py:29
  104.0 2.1 %collective-permute-done = bf16[1024,512]{1,0:T(8,128)(2,1)S(1)} collective-permute-done((bf16[1024,512]{1,0:T(8,128)(2,1)S(1)}, bf16[1024,512]{1,0:T(8,128)(2,1)S(1)}, u32[]{:S(2)}, u32[]{:S(2)}) %collective-permute-start) | collective-permute-done | bytes 1048608 | tf_op jit(solution)/shard_map/ppermute | solution.py:29
  106.1 0.6 add_convert_fusion
  106.7 1.2 reshape.169
  107.9 1.8 %copy.52 = bf16[16,32,2,512]{3,0,1,2:T(8,128)(2,1)S(1)} copy(bf16[16,32,2,512]{3,2,1,0:T(2,128)(2,1)} %reshape.169) | data formatting | bytes 2097152 | tf_op jit(solution)/shard_map/reshape | solution.py:34
  109.8 1.1 copy.53
  110.9 45.8 %all_to_all.30 = bf16[512,2,512]{2,1,0:T(2,128)(2,1)S(1)} all-to-all(bf16[512,2,512]{2,1,0:T(2,128)(2,1)S(1)} %copy.53), channel_id=1, replica_groups=mesh['group'=32,'member'=16] {'group','member'}, dimensions={0} | all-to-all | bytes 2097152 | tf_op jit(solution)/shard_map/all_to_all | solution.py:36
  156.6 0.9 convert_reduce_fusion
  157.5 0.8 broadcast_in_dim.51
  158.4 5.7 %all-to-all-start.4 = ((f32[32,1,2048]{2,1,0:T(1,128)}), f32[32,1,2048]{2,1,0:T(1,128)S(1)}, u32[]{:S(2)}, u32[]{:S(2)}) async-start(f32[32,1,2048]{2,1,0:T(1,128)} %broadcast_in_dim.51), calls=%async_computation.4 | async-start | bytes 524288 | tf_op jit(solution)/shard_map/all_to_all | solution.py:41
  164.1 2.3 %convolution_convert_fusion = bf16[512,1024]{1,0:T(8,128)(2,1)} fusion(bf16[512,1024]{1,0:T(8,128)(2,1)S(1)} %copy-done.5, bf16[1024,1024]{1,0:T(8,128)(2,1)S(1)} %copy-done), kind=kOutput, calls=%fused_computation.24 | convolution fusion | flops 1074266112 | bytes 4194304 | tf_op jit(solution)/shard_map/dot_general | solution.py:124
  166.4 9.6 %all-to-all-done.4 = f32[32,1,2048]{2,1,0:T(1,128)S(1)} async-done(((f32[32,1,2048]{2,1,0:T(1,128)}), f32[32,1,2048]{2,1,0:T(1,128)S(1)}, u32[]{:S(2)}, u32[]{:S(2)}) %all-to-all-start.4) | async-done | bytes 262176 | tf_op jit(solution)/shard_map/all_to_all | solution.py:41
  176.0 0.7 multiply_reduce_fusion.1
  176.7 0.7 mul.65
  (43 shorter events, 0.4 us)
Async XLA Ops:
  0.6 12.8 %copy-start = (bf16[1024,1024]{1,0:T(8,128)(2,1)S(1)}, bf16[1024,1024]{1,0:T(8,128)(2,1)}, u32[]{:S(2)}) copy-start(bf16[1024,1024]{1,0:T(8,128)(2,1)} %param.8) | copy-start | bytes 6291460
  3.0 18.0 %all-to-all-start = ((s32[16,1,1]{2,1,0:T(1,128)}), s32[16,1,1]{2,1,0:T(1,128)S(1)}, u32[]{:S(2)}, u32[]{:S(2)}) async-start(s32[16,1,1]{2,1,0:T(1,128)} %copy.48), calls=%async_computation | async-start | bytes 16384 | tf_op jit(solution)/shard_map/all_to_all | solution.py:66
  17.2 17.4 %copy-start.6 = (bf16[512,1024]{1,0:T(8,128)(2,1)}, bf16[512,1024]{1,0:T(8,128)(2,1)S(1)}, u32[]{:S(2)}) copy-start(bf16[512,1024]{1,0:T(8,128)(2,1)S(1)} %get-tuple-element.9) | copy-start | bytes 3145732
  21.3 6.0 %copy-start.14 = (s32[512,16]{0,1:T(8,128)S(1)}, s32[512,16]{0,1:T(8,128)}, u32[]{:S(2)}) copy-start(s32[512,16]{0,1:T(8,128)} %param.12) | copy-start | bytes 98308
  21.3 6.4 %copy-start.15 = (s32[512,16]{0,1:T(8,128)S(1)}, s32[512,16]{0,1:T(8,128)}, u32[]{:S(2)}) copy-start(s32[512,16]{0,1:T(8,128)} %param.11) | copy-start | bytes 98308
  22.9 30.9 %all-to-all-start.1 = ((bf16[16,32,1024]{2,1,0:T(8,128)(2,1)}), bf16[16,32,1024]{2,1,0:T(8,128)(2,1)}, u32[]{:S(2)}, u32[]{:S(2)}) async-start(bf16[16,32,1024]{2,1,0:T(8,128)(2,1)} %gather_fusion), calls=%async_computation.1 | async-start | bytes 2097152 | tf_op jit(solution)/shard_map/all_to_all | solution.py:70
  34.6 1.0 copy-start.11
  53.8 3.4 %copy-start.3 = (bf16[512,1024]{1,0:T(8,128)(2,1)S(1)}, bf16[512,1024]{1,0:T(8,128)(2,1)}, u32[]{:S(2)}) copy-start(bf16[512,1024]{1,0:T(8,128)(2,1)} %param.13) | copy-start | bytes 3145732
  57.2 1.3 copy-start.1
  57.7 1.5 copy-start.12
  59.2 1.7 copy-start.7
  60.9 31.4 %all-to-all-start.2 = ((bf16[16,32,1024]{2,1,0:T(8,128)(2,1)}), bf16[16,32,1024]{2,1,0:T(8,128)(2,1)}, u32[]{:S(2)}, u32[]{:S(2)}) async-start(bf16[16,32,1024]{2,1,0:T(8,128)(2,1)} %bitcast.56), calls=%async_computation.2 | async-start | bytes 2097152 | tf_op jit(solution)/shard_map/all_to_all | solution.py:109
  92.4 2.2 %copy-start.8 = (bf16[512,1024]{1,0:T(8,128)(2,1)S(1)}, bf16[512,1024]{1,0:T(8,128)(2,1)}, u32[]{:S(2)}) copy-start(bf16[512,1024]{1,0:T(8,128)(2,1)} %copy-done.7) | copy-start | bytes 3145732
  92.4 2.2 %copy-start.10 = (bf16[512,512]{1,0:T(8,128)(2,1)S(1)}, bf16[512,512]{1,0:T(8,128)(2,1)}, u32[]{:S(2)}) copy-start(bf16[512,512]{1,0:T(8,128)(2,1)} %copy.49) | copy-start | bytes 1572868
  94.5 1.6 copy-start.2
  94.5 2.2 %copy-start.9 = (f32[512,1024]{1,0:T(8,128)S(1)}, f32[512,1024]{1,0:T(8,128)}, u32[]{:S(2)}) copy-start(f32[512,1024]{1,0:T(8,128)} %get-tuple-element.10) | copy-start | bytes 6291460
  94.6 2.2 %copy-start.16 = (f32[1024]{0:T(1024)S(1)}, f32[1024]{0:T(1024)}, u32[]{:S(2)}) copy-start(f32[1024]{0:T(1024)} %param.9) | copy-start | bytes 12292
  96.8 1.8 copy-start.13
  98.5 1.3 copy-start.4
  100.0 6.0 %collective-permute-start = (bf16[1024,512]{1,0:T(8,128)(2,1)S(1)}, bf16[1024,512]{1,0:T(8,128)(2,1)S(1)}, u32[]{:S(2)}, u32[]{:S(2)}) collective-permute-start(bf16[1024,512]{1,0:T(8,128)(2,1)S(1)} %select_convert_fusion), channel_id=1, source_target_pairs={{0,1},{1,0},{2,3},{3,2},{4,5},{5,4},{6,7},{7,6},{8,9},{9,8},{10,11... | collective-permute-start | bytes 3145736 | tf_op jit(solution)/shard_map/ppermute | solution.py:29
  110.8 53.3 %copy-start.5 = (bf16[512,1024]{1,0:T(8,128)(2,1)S(1)}, bf16[512,1024]{1,0:T(8,128)(2,1)}, u32[]{:S(2)}) copy-start(bf16[512,1024]{1,0:T(8,128)(2,1)} %copy-done.4) | copy-start | bytes 3145732
  158.4 17.6 %all-to-all-start.4 = ((f32[32,1,2048]{2,1,0:T(1,128)}), f32[32,1,2048]{2,1,0:T(1,128)S(1)}, u32[]{:S(2)}, u32[]{:S(2)}) async-start(f32[32,1,2048]{2,1,0:T(1,128)} %broadcast_in_dim.51), calls=%async_computation.4 | async-start | bytes 524288 | tf_op jit(solution)/shard_map/all_to_all | solution.py:41

commit v11 on v10

--- a/solution.py
+++ b/solution.py
@@ -39,9 +39,13 @@
     )
     mine = jnp.transpose(by_half, (1, 0, 2)).reshape(share * cols)
     every = lax.all_to_all(
-        jnp.broadcast_to(mine, (groups, share * cols)), "group", split_axis=0, concat_axis=0, tiled=True
+        jnp.broadcast_to(mine.astype(jnp.bfloat16), (groups, share * cols)),
+        "group",
+        split_axis=0,
+        concat_axis=0,
+        tiled=True,
     )
-    return every.reshape(rows // members, cols)
+    return every.astype(jnp.float32).reshape(rows // members, cols)
 
 
 def on_device(feats, transform, bias, tile_list, nbr_slot, nbr_weight, cotangent):

time: 180 us -> 181 us (level)
  other arithmetic: 12.7 us -> 15.3 us
  waiting for transfers between devices: 53.8 us -> 51.4 us
    all_to_all x1, waiting for transfers between devices: 9.63 us -> 7.26 us  [reduce_rows(): lax.all_to_all(jnp.broadcast_to(mine.astype(jnp.bfloat16), (groups, share...]
where the time goes in v11:
time: 181 us; the launch traced here: 178 us
  waiting for transfers between devices  51.4 us (28%)
  blocking collectives  45.9 us (25%)
  starting transfers between devices  29.3 us (16%)
  matrix products  19.3 us (11%)
  local copies, waits for them, and re-layouts  16.2 us (9%)
  other arithmetic  15.3 us (8%)
    all_to_all x1, blocking collectives, reduce_rows(): lax.all_to_all(chunks, ('group', 'member'), split_axis=0, concat_axis=0,...  45.9 us
    all_to_all x1, waiting for transfers between devices, on_device(): lax.all_to_all(returned, 'member', split_axis=0, concat_axis=0, tiled=True)  22.2 us
    all_to_all x1, waiting for transfers between devices, on_device(): lax.all_to_all(own_tiles[served], 'member', split_axis=0, concat_axis=0,...  16.2 us
    all_to_all x1, starting transfers between devices, on_device(): lax.all_to_all(wanted.reshape(members, 1), 'member', split_axis=0, concat...  10.4 us
    all_to_all x1, waiting for transfers between devices, reduce_rows(): lax.all_to_all(jnp.broadcast_to(mine.astype(jnp.bfloat16), (groups, share...  7.26 us
    all_to_all x1, starting transfers between devices, reduce_rows(): lax.all_to_all(jnp.broadcast_to(mine.astype(jnp.bfloat16), (groups, share...  5.72 us
    reduce_sum x1, other arithmetic, adjacency_of(): return jnp.sum(matched_weights, axis=-2).astype(jnp.bfloat16)  5.08 us
    all_to_all x1, starting transfers between devices, on_device(): lax.all_to_all(returned, 'member', split_axis=0, concat_axis=0, tiled=True)  4.91 us
  transfers between devices with their start and end apart: 5, of which 5 were waited for; matrix products, arithmetic and copies ran while one was open for 11% of the time, Pallas kernels for 0%

profile of v11, /device:TPU:6, one launch (start us, length us, event | category | flops | bytes accessed | tf_op | source)
XLA Modules:
  0.0 178.5 jit_solution(16181173063821145707)
XLA Ops:
  0.6 0.8 broadcast_compare_fusion
  1.5 0.7 add_select_fusion
  2.3 0.7 copy.48
  3.0 10.4 %all-to-all-start = ((s32[16,1,1]{2,1,0:T(1,128)}), s32[16,1,1]{2,1,0:T(1,128)S(1)}, u32[]{:S(2)}, u32[]{:S(2)}) async-start(s32[16,1,1]{2,1,0:T(1,128)} %copy.48), calls=%async_computation | async-start | bytes 16384 | tf_op jit(solution)/shard_map/all_to_all | solution.py:70
  13.4 3.8 %maximum_convert_fusion = (bf16[512,1024]{1,0:T(8,128)(2,1)S(1)}, f32[512,1024]{1,0:T(8,128)}) fusion(f32[1024]{0:T(1024)} %param.9, bf16[512,1024]{1,0:T(8,128)(2,1)} %param.7, bf16[1024,1024]{1,0:T(8,128)(2,1)S(1)} %copy-done), kind=kOutput, calls=%fused_computation.19 | convolution fusion | flops 1075314688 | bytes 6295552 | tf_op jit(solution)/shard_map/dot_general | solution.py:61
  17.2 3.7 %all-to-all-done = s32[16,1,1]{2,1,0:T(1,128)S(1)} async-done(((s32[16,1,1]{2,1,0:T(1,128)}), s32[16,1,1]{2,1,0:T(1,128)S(1)}, u32[]{:S(2)}, u32[]{:S(2)}) %all-to-all-start) | async-done | bytes 96 | tf_op jit(solution)/shard_map/all_to_all | solution.py:70
  20.9 0.4 clamp_reduce_fusion
  21.3 1.6 gather_fusion
  22.9 4.3 %all-to-all-start.1 = ((bf16[16,32,1024]{2,1,0:T(8,128)(2,1)}), bf16[16,32,1024]{2,1,0:T(8,128)(2,1)}, u32[]{:S(2)}, u32[]{:S(2)}) async-start(bf16[16,32,1024]{2,1,0:T(8,128)(2,1)} %gather_fusion), calls=%async_computation.1 | async-start | bytes 2097152 | tf_op jit(solution)/shard_map/all_to_all | solution.py:74
  27.7 0.8 copy.56
  28.5 5.1 %select_reduce_fusion = s32[4,128,256]{2,1,0:T(8,128)S(1)} fusion(s32[4,128,16]{2,1,0:T(8,128)} %bitcast.57, s32[4,128,16]{2,1,0:T(8,128)S(1)} %bitcast.56), kind=kLoop, calls=%fused_computation.1 | loop fusion | flops 6160384 | bytes 589824 | tf_op jit(solution)/shard_map/reduce_sum | solution.py:14
  33.6 1.0 fusion.6
  34.6 1.0 copy-done.11
  35.6 2.0 %fusion.12 = f32[512,1024]{1,0:T(8,128)} fusion(bf16[512,1024]{1,0:T(8,128)(2,1)S(1)} %get-tuple-element.9, bf16[512,1024]{1,0:T(8,128)(2,1)S(1)} %bitcast.51), kind=kOutput, calls=%fused_computation.31 | convolution fusion | flops 536870912 | bytes 3670016 | tf_op jit(solution)/shard_map/dot_general | solution.py:92
  37.6 16.2 %all-to-all-done.1 = bf16[16,32,1024]{2,1,0:T(8,128)(2,1)} async-done(((bf16[16,32,1024]{2,1,0:T(8,128)(2,1)}), bf16[16,32,1024]{2,1,0:T(8,128)(2,1)}, u32[]{:S(2)}, u32[]{:S(2)}) %all-to-all-start.1) | async-done | bytes 1048608 | tf_op jit(solution)/shard_map/all_to_all | solution.py:74
  53.8 3.4 %multiply_reduce_fusion = (f32[512]{0:T(512)S(1)}, f32[512,1024]{1,0:T(8,128)S(1)}) fusion(bf16[512,1024]{1,0:T(8,128)(2,1)} %copy-done.6, f32[512]{0:T(512)S(1)} %convert_element_type.76, f32[512,1024]{1,0:T(8,128)} %fusion.12, bf16[512,1024]{1,0:T(8,128)(2,1)} %bitcast.6, bf16[512,1024]{1,0:T(8,128)(2,1)} %bitcast.52), kind=kOutput, calls=%fused_computation.17 | convolution fusion | flops 540016128 | bytes 6819840 | tf_op jit(solution)/shard_map/dot_general | solution.py:94
  57.3 0.5 fusion.1
  57.7 0.5 divide_convert_fusion
  58.3 0.2 copy-done.1
  58.5 0.7 copy-done.12
  59.2 1.7 convolution_convert_fusion.1
  60.9 4.9 %all-to-all-start.2 = ((bf16[16,32,1024]{2,1,0:T(8,128)(2,1)}), bf16[16,32,1024]{2,1,0:T(8,128)(2,1)}, u32[]{:S(2)}, u32[]{:S(2)}) async-start(bf16[16,32,1024]{2,1,0:T(8,128)(2,1)} %bitcast.55), calls=%async_computation.2 | async-start | bytes 2097152 | tf_op jit(solution)/shard_map/all_to_all | solution.py:113
  65.8 1.9 %slice_bitcast_fusion = bf16[512,512]{0,1:T(8,128)(2,1)} fusion(bf16[512,1024]{1,0:T(8,128)(2,1)} %bitcast.53), kind=kLoop, calls=%fused_computation.30 | loop fusion | bytes 1048576 | tf_op jit(solution)/shard_map/dot_general | solution.py:114
  67.7 2.0 %copy.49 = bf16[512,512]{1,0:T(8,128)(2,1)} copy(bf16[512,512]{0,1:T(8,128)(2,1)} %slice_bitcast_fusion) | data formatting | bytes 1048576 | tf_op jit(solution)/shard_map/dot_general | solution.py:114
  69.7 0.4 compare_reduce_fusion
  70.1 22.2 %all-to-all-done.2 = bf16[16,32,1024]{2,1,0:T(8,128)(2,1)} async-done(((bf16[16,32,1024]{2,1,0:T(8,128)(2,1)}), bf16[16,32,1024]{2,1,0:T(8,128)(2,1)}, u32[]{:S(2)}, u32[]{:S(2)}) %all-to-all-start.2) | async-done | bytes 1048608 | tf_op jit(solution)/shard_map/all_to_all | solution.py:113
  92.3 2.1 %fusion.8 = f32[16,32,1024]{2,0,1:T(8,128)S(1)} fusion(bf16[16,32,1024]{2,1,0:T(8,128)(2,1)} %all-to-all-done.2, s32[16]{0:T(128)S(1)} %clamp_reduce_fusion, pred[16]{0:T(512)(128)(4,1)S(1)} %compare_reduce_fusion), kind=kOutput, calls=%fused_computation.26 | convolution fusion | flops 16777728 | bytes 3145808 | tf_op jit(solution)/shard_map/jt,jrh->trh/dot_general | solution.py:121
  94.6 1.6 copy_add_fusion
  96.2 0.6 copy-done.9
  96.8 1.7 fusion.4
  98.5 1.3 convolution_bitcast_fusion
  99.8 0.2 select_convert_fusion
  100.0 3.9 %collective-permute-start = (bf16[1024,512]{1,0:T(8,128)(2,1)S(1)}, bf16[1024,512]{1,0:T(8,128)(2,1)S(1)}, u32[]{:S(2)}, u32[]{:S(2)}) collective-permute-start(bf16[1024,512]{1,0:T(8,128)(2,1)S(1)} %select_convert_fusion), channel_id=1, source_target_pairs={{0,1},{1,0},{2,3},{3,2},{4,5},{5,4},{6,7},{7,6},{8,9},{9,8},{10,11... | collective-permute-start | bytes 3145736 | tf_op jit(solution)/shard_map/ppermute | solution.py:29
  104.0 2.1 %collective-permute-done = bf16[1024,512]{1,0:T(8,128)(2,1)S(1)} collective-permute-done((bf16[1024,512]{1,0:T(8,128)(2,1)S(1)}, bf16[1024,512]{1,0:T(8,128)(2,1)S(1)}, u32[]{:S(2)}, u32[]{:S(2)}) %collective-permute-start) | collective-permute-done | bytes 1048608 | tf_op jit(solution)/shard_map/ppermute | solution.py:29
  106.1 0.6 add_convert_fusion
  106.7 1.2 reshape.168
  107.9 1.8 %copy.52 = bf16[16,32,2,512]{3,0,1,2:T(8,128)(2,1)S(1)} copy(bf16[16,32,2,512]{3,2,1,0:T(2,128)(2,1)} %reshape.168) | data formatting | bytes 2097152 | tf_op jit(solution)/shard_map/reshape | solution.py:34
  109.7 1.1 copy.53
  110.8 45.9 %all_to_all.30 = bf16[512,2,512]{2,1,0:T(2,128)(2,1)} all-to-all(bf16[512,2,512]{2,1,0:T(2,128)(2,1)S(1)} %copy.53), channel_id=1, replica_groups=mesh['group'=32,'member'=16] {'group','member'}, dimensions={0} | all-to-all | bytes 2097152 | tf_op jit(solution)/shard_map/all_to_all | solution.py:36
  156.7 2.1 %reduce.3 = bf16[2,2,512]{2,1,0:T(2,128)(2,1)S(1)} reduce(bf16[256,2,2,512]{3,2,1,0:T(2,128)(2,1)} %bitcast.48, bf16[]{:T(256)} %constant.65), dimensions={0}, to_apply=%region_5.6.clone | reduce | flops 522240 | bytes 1052674 | tf_op jit(solution)/shard_map/reduce_sum | solution.py:37
  159.0 0.5 broadcast.151
  159.5 1.4 reduce.11
  160.9 0.7 reshape.186
  161.6 5.7 %all-to-all-start.4 = ((bf16[32,2,1024]{2,1,0:T(2,128)(2,1)}), bf16[32,2,1024]{2,1,0:T(2,128)(2,1)S(1)}, u32[]{:S(2)}, u32[]{:S(2)}) async-start(bf16[32,2,1024]{2,1,0:T(2,128)(2,1)} %reshape.186), calls=%async_computation.4 | async-start | bytes 262144 | tf_op jit(solution)/shard_map/all_to_all | solution.py:41
  167.4 2.3 %convolution_convert_fusion = bf16[512,1024]{1,0:T(8,128)(2,1)} fusion(bf16[512,1024]{1,0:T(8,128)(2,1)S(1)} %copy-done.5, bf16[1024,1024]{1,0:T(8,128)(2,1)S(1)} %copy-done), kind=kOutput, calls=%fused_computation.23 | convolution fusion | flops 1074266112 | bytes 4194304 | tf_op jit(solution)/shard_map/dot_general | solution.py:128
  169.6 7.3 %all-to-all-done.4 = bf16[32,2,1024]{2,1,0:T(2,128)(2,1)S(1)} async-done(((bf16[32,2,1024]{2,1,0:T(2,128)(2,1)}), bf16[32,2,1024]{2,1,0:T(2,128)(2,1)S(1)}, u32[]{:S(2)}, u32[]{:S(2)}) %all-to-all-start.4) | async-done | bytes 131104 | tf_op jit(solution)/shard_map/all_to_all | solution.py:41
  177.0 0.8 multiply_reduce_fusion.1
  177.7 0.7 mul.65
  (47 shorter events, 0.8 us)
Async XLA Ops:
  0.6 12.8 %copy-start = (bf16[1024,1024]{1,0:T(8,128)(2,1)S(1)}, bf16[1024,1024]{1,0:T(8,128)(2,1)}, u32[]{:S(2)}) copy-start(bf16[1024,1024]{1,0:T(8,128)(2,1)} %param.8) | copy-start | bytes 6291460
  3.0 18.0 %all-to-all-start = ((s32[16,1,1]{2,1,0:T(1,128)}), s32[16,1,1]{2,1,0:T(1,128)S(1)}, u32[]{:S(2)}, u32[]{:S(2)}) async-start(s32[16,1,1]{2,1,0:T(1,128)} %copy.48), calls=%async_computation | async-start | bytes 16384 | tf_op jit(solution)/shard_map/all_to_all | solution.py:70
  17.2 17.4 %copy-start.6 = (bf16[512,1024]{1,0:T(8,128)(2,1)}, bf16[512,1024]{1,0:T(8,128)(2,1)S(1)}, u32[]{:S(2)}) copy-start(bf16[512,1024]{1,0:T(8,128)(2,1)S(1)} %get-tuple-element.9) | copy-start | bytes 3145732
  21.3 6.2 %copy-start.15 = (s32[512,16]{0,1:T(8,128)S(1)}, s32[512,16]{0,1:T(8,128)}, u32[]{:S(2)}) copy-start(s32[512,16]{0,1:T(8,128)} %param.11) | copy-start | bytes 98308
  21.3 6.3 %copy-start.14 = (s32[512,16]{0,1:T(8,128)S(1)}, s32[512,16]{0,1:T(8,128)}, u32[]{:S(2)}) copy-start(s32[512,16]{0,1:T(8,128)} %param.12) | copy-start | bytes 98308
  22.9 30.9 %all-to-all-start.1 = ((bf16[16,32,1024]{2,1,0:T(8,128)(2,1)}), bf16[16,32,1024]{2,1,0:T(8,128)(2,1)}, u32[]{:S(2)}, u32[]{:S(2)}) async-start(bf16[16,32,1024]{2,1,0:T(8,128)(2,1)} %gather_fusion), calls=%async_computation.1 | async-start | bytes 2097152 | tf_op jit(solution)/shard_map/all_to_all | solution.py:74
  34.6 1.0 copy-start.11
  53.8 3.4 %copy-start.3 = (bf16[512,1024]{1,0:T(8,128)(2,1)S(1)}, bf16[512,1024]{1,0:T(8,128)(2,1)}, u32[]{:S(2)}) copy-start(bf16[512,1024]{1,0:T(8,128)(2,1)} %param.13) | copy-start | bytes 3145732
  57.2 1.3 copy-start.1
  57.7 1.5 copy-start.12
  59.2 1.7 copy-start.7
  60.9 31.4 %all-to-all-start.2 = ((bf16[16,32,1024]{2,1,0:T(8,128)(2,1)}), bf16[16,32,1024]{2,1,0:T(8,128)(2,1)}, u32[]{:S(2)}, u32[]{:S(2)}) async-start(bf16[16,32,1024]{2,1,0:T(8,128)(2,1)} %bitcast.55), calls=%async_computation.2 | async-start | bytes 2097152 | tf_op jit(solution)/shard_map/all_to_all | solution.py:113
  92.3 2.2 %copy-start.8 = (bf16[512,1024]{1,0:T(8,128)(2,1)S(1)}, bf16[512,1024]{1,0:T(8,128)(2,1)}, u32[]{:S(2)}) copy-start(bf16[512,1024]{1,0:T(8,128)(2,1)} %copy-done.7) | copy-start | bytes 3145732
  92.3 2.2 %copy-start.10 = (bf16[512,512]{1,0:T(8,128)(2,1)S(1)}, bf16[512,512]{1,0:T(8,128)(2,1)}, u32[]{:S(2)}) copy-start(bf16[512,512]{1,0:T(8,128)(2,1)} %copy.49) | copy-start | bytes 1572868
  94.5 1.6 copy-start.2
  94.5 2.2 %copy-start.9 = (f32[512,1024]{1,0:T(8,128)S(1)}, f32[512,1024]{1,0:T(8,128)}, u32[]{:S(2)}) copy-start(f32[512,1024]{1,0:T(8,128)} %get-tuple-element.10) | copy-start | bytes 6291460
  94.5 2.2 %copy-start.16 = (f32[1024]{0:T(1024)S(1)}, f32[1024]{0:T(1024)}, u32[]{:S(2)}) copy-start(f32[1024]{0:T(1024)} %param.9) | copy-start | bytes 12292
  96.8 1.8 copy-start.13
  98.5 1.3 copy-start.4
  100.0 6.0 %collective-permute-start = (bf16[1024,512]{1,0:T(8,128)(2,1)S(1)}, bf16[1024,512]{1,0:T(8,128)(2,1)S(1)}, u32[]{:S(2)}, u32[]{:S(2)}) collective-permute-start(bf16[1024,512]{1,0:T(8,128)(2,1)S(1)} %select_convert_fusion), channel_id=1, source_target_pairs={{0,1},{1,0},{2,3},{3,2},{4,5},{5,4},{6,7},{7,6},{8,9},{9,8},{10,11... | collective-permute-start | bytes 3145736 | tf_op jit(solution)/shard_map/ppermute | solution.py:29
  110.8 56.5 %copy-start.5 = (bf16[512,1024]{1,0:T(8,128)(2,1)S(1)}, bf16[512,1024]{1,0:T(8,128)(2,1)}, u32[]{:S(2)}) copy-start(bf16[512,1024]{1,0:T(8,128)(2,1)} %copy-done.4) | copy-start | bytes 3145732
  161.6 15.3 %all-to-all-start.4 = ((bf16[32,2,1024]{2,1,0:T(2,128)(2,1)}), bf16[32,2,1024]{2,1,0:T(2,128)(2,1)S(1)}, u32[]{:S(2)}, u32[]{:S(2)}) async-start(bf16[32,2,1024]{2,1,0:T(2,128)(2,1)} %reshape.186), calls=%async_computation.4 | async-start | bytes 262144 | tf_op jit(solution)/shard_map/all_to_all | solution.py:41
